TPU v7x, 32 devices: a whole 2x2x4 slice. The times are simulated.
32 devices in a mesh: groups: 2 (over y), rows: 4 (over x, core), rep: 4 (over z).
Axes of the slice: x: 2, y: 2, z: 4, core: 2. Of those that a mesh axis runs over, the one named last changes fastest.
Arguments:
- images: bfloat16 [8, 64, 128, 256], P(('groups', 'rep'), 'rows'), parts along dimension 0, may hold values from -6 to 6
- cotangent: bfloat16 [8, 64, 128, 256], P(('groups', 'rep'), 'rows'), parts along dimension 0, may hold values from -6 to 6
- row_taps: float32 [102, 256], P('groups'), parts along dimension 0, may hold values from -0.875 to 0.875
- col_taps: float32 [102, 256], P('groups'), parts along dimension 0, may hold values from -0.875 to 0.875
- norm_gain: float32 [512], P('groups'), parts along dimension 0, may hold values from 0.25 to 1.75
- norm_shift: float32 [512], P('groups'), parts along dimension 0, may hold values from -3 to 3
- up_weight: bfloat16 [512, 1024], P('groups'), parts along dimension 0, may hold values from -0.375 to 0.375
- up_bias: float32 [2048], P('groups'), parts along dimension 0, may hold values from -3 to 3
- down_weight: bfloat16 [2048, 256], P('groups'), parts along dimension 0, may hold values from -0.1875 to 0.1875
- down_bias: float32 [512], P('groups'), parts along dimension 0, may hold values from -3 to 3
- layer_scale: float32 [512], P('groups'), parts along dimension 0, may hold values from 0.5 to 1.5
Outputs:
- block_out: bfloat16 [8, 64, 128, 256], P(('groups', 'rep'), 'rows'), parts along dimension 0
- image_grad: bfloat16 [8, 64, 128, 256], P(('groups', 'rep'), 'rows'), parts along dimension 0
- row_taps_grad: float32 [102, 256], P('groups'), parts along dimension 0
- col_taps_grad: float32 [102, 256], P('groups'), parts along dimension 0
- scale_grad: float32 [512], P('groups'), parts along dimension 0
- down_bias_grad: float32 [512], P('groups'), parts along dimension 0
- down_grad: float32 [2048, 256], P('groups'), parts along dimension 0
- up_bias_grad: float32 [2048], P('groups'), parts along dimension 0
- up_grad: float32 [512, 1024], P('groups'), parts along dimension 0
- gain_grad: float32 [512], P('groups'), parts along dimension 0
- shift_grad: float32 [512], P('groups'), parts along dimension 0
There are 2 independent parts, one for each index of `groups`. A program takes and returns all parts, laid end to end along the dimension named above; each array names one. Nothing has to cross between parts.
All inputs are finite; a program needn't handle non-finite values.
Results may differ from a plain program's by a relative error of at most 0.0086.
Values may be sent and summed in bfloat16 or wider, within the bound.
No kernel may reach another device: no remote copies, remote signals or barrier semaphores. Data moves between devices by JAX's collectives and lax.ppermute only.
A program may use at most 64 MiB of HBM per device.

v0:
```python
import math

import jax
import jax.numpy as jnp
from jax import lax
from jax.sharding import PartitionSpec as P

EPSILON = 1e-06
CUBIC_TERM = 0.044715
TANH_SCALE = 0.7978845608028654


def activate(pre_act):
    return (
        0.5
        * pre_act
        * (1.0 + jnp.tanh(TANH_SCALE * (pre_act + CUBIC_TERM * pre_act * pre_act * pre_act)))
    )


def activate_slope(pre_act):
    inner = jnp.tanh(TANH_SCALE * (pre_act + CUBIC_TERM * pre_act * pre_act * pre_act))
    return 0.5 * (1.0 + inner) + 0.5 * pre_act * (1.0 - inner * inner) * TANH_SCALE * (
        1.0 + 3.0 * CUBIC_TERM * pre_act * pre_act
    )


def pad_along(source, direction, half_reach):
    widths = [(0, 0)] * source.ndim
    widths[direction] = (half_reach, half_reach)
    return jnp.pad(source, widths)


def slide_padded(padded, taps_table, direction, length):
    shape_out = padded.shape[:direction] + (length,) + padded.shape[direction + 1 :]
    result = jnp.zeros(shape_out, jnp.float32)
    for offset in range(taps_table.shape[0]):
        result = result + taps_table[offset] * lax.slice_in_dim(
            padded, offset, offset + length, axis=direction
        )
    return result


def tap_sums(cot_field, padded, taps_count, direction):
    length = cot_field.shape[direction]
    lead_axes = tuple(range(cot_field.ndim - 1))
    return jnp.stack(
        [
            jnp.sum(
                cot_field * lax.slice_in_dim(padded, offset, offset + length, axis=direction),
                axis=lead_axes,
            )
            for offset in range(taps_count)
        ]
    )


def pointwise(
    mix_rows,
    image_rows,
    cot_rows,
    norm_gain,
    norm_shift,
    up_weight,
    up_bias,
    down_weight,
    down_bias,
    layer_scale,
):
    mix_float = mix_rows.astype(jnp.float32)
    centered = mix_float - jnp.mean(mix_float, axis=-1, keepdims=True)
    inv_dev = lax.rsqrt(jnp.mean(centered * centered, axis=-1, keepdims=True) + EPSILON)
    standardized = centered * inv_dev
    normed = (standardized * norm_gain + norm_shift).astype(jnp.bfloat16)
    pre_act = jnp.dot(normed, up_weight, preferred_element_type=jnp.float32) + up_bias
    activated = activate(pre_act).astype(jnp.bfloat16)
    branch = jnp.dot(activated, down_weight, preferred_element_type=jnp.float32) + down_bias
    cot_float = cot_rows.astype(jnp.float32)
    block_rows = (image_rows.astype(jnp.float32) + layer_scale * branch).astype(jnp.bfloat16)
    branch_cot = cot_float * layer_scale
    branch_grad = branch_cot.astype(jnp.bfloat16)
    act_cot = lax.dot_general(
        branch_grad, down_weight, (((1,), (1,)), ((), ())), preferred_element_type=jnp.float32
    )
    pre_cot = act_cot * activate_slope(pre_act)
    pre_grad = pre_cot.astype(jnp.bfloat16)
    normed_cot = lax.dot_general(
        pre_grad, up_weight, (((1,), (1,)), ((), ())), preferred_element_type=jnp.float32
    )
    scaled_cot = normed_cot * norm_gain
    grad_rows = (
        inv_dev
        * (
            scaled_cot
            - jnp.mean(scaled_cot, axis=-1, keepdims=True)
            - standardized * jnp.mean(scaled_cot * standardized, axis=-1, keepdims=True)
        )
    ).astype(jnp.bfloat16)
    partials = (
        jnp.sum(cot_float * branch, axis=0),
        jnp.sum(branch_cot, axis=0),
        lax.dot_general(
            activated, branch_grad, (((0,), (0,)), ((), ())), preferred_element_type=jnp.float32
        ),
        jnp.sum(pre_cot, axis=0),
        lax.dot_general(
            normed, pre_grad, (((0,), (0,)), ((), ())), preferred_element_type=jnp.float32
        ),
        jnp.sum(normed_cot * standardized, axis=0),
        jnp.sum(normed_cot, axis=0),
    )
    return (block_rows, grad_rows, partials)


def per_device(
    images,
    cotangent,
    row_taps,
    col_taps,
    norm_gain,
    norm_shift,
    up_weight,
    up_bias,
    down_weight,
    down_bias,
    layer_scale,
):
    tiles_here, band_rows, columns, channels = images.shape
    taps_count = row_taps.shape[0]
    half_reach = (taps_count - 1) // 2
    pixel_scale = 1.0 / math.sqrt(
        tiles_here * lax.axis_size("rep") * band_rows * lax.axis_size("rows") * columns
    )
    image_padded = pad_along(images.astype(jnp.float32), 2, half_reach)
    row_mix = slide_padded(image_padded, row_taps, 2, columns).astype(jnp.bfloat16)
    row_mix = lax.optimization_barrier(row_mix)
    mix_columns = lax.all_to_all(row_mix, "rows", split_axis=2, concat_axis=1, tiled=True)
    mix_padded = pad_along(mix_columns.astype(jnp.float32), 1, half_reach)
    col_local = slide_padded(mix_padded, col_taps, 1, mix_columns.shape[1]).astype(jnp.bfloat16)
    col_mix = lax.all_to_all(col_local, "rows", split_axis=1, concat_axis=2, tiled=True)
    col_mix = lax.optimization_barrier(col_mix)
    block_rows, grad_rows, partials = pointwise(
        col_mix.reshape(-1, channels),
        images.reshape(-1, channels),
        cotangent.reshape(-1, channels),
        norm_gain,
        norm_shift,
        up_weight,
        up_bias,
        down_weight,
        down_bias,
        layer_scale,
    )
    scale_part, down_bias_part, down_part, up_bias_part, up_part, gain_part, shift_part = partials
    block_out = block_rows.reshape(images.shape)
    grad_rows = lax.optimization_barrier(grad_rows)
    col_grad = grad_rows.reshape(images.shape)
    grad_columns = lax.all_to_all(col_grad, "rows", split_axis=2, concat_axis=1, tiled=True)
    grad_float = grad_columns.astype(jnp.float32)
    col_part = tap_sums(grad_float, mix_padded, taps_count, 1)
    row_local = slide_padded(
        pad_along(grad_float, 1, half_reach), col_taps[::-1], 1, grad_columns.shape[1]
    ).astype(jnp.bfloat16)
    row_grad = lax.all_to_all(row_local, "rows", split_axis=1, concat_axis=2, tiled=True)
    row_grad = lax.optimization_barrier(row_grad)
    row_float = row_grad.astype(jnp.float32)
    row_part = tap_sums(row_float, image_padded, taps_count, 2)
    image_grad = (
        cotangent.astype(jnp.float32)
        + slide_padded(pad_along(row_float, 2, half_reach), row_taps[::-1], 2, columns)
    ).astype(jnp.bfloat16)
    (
        row_total,
        col_total,
        scale_total,
        down_bias_total,
        down_total,
        up_bias_total,
        up_total,
        gain_total,
        shift_total,
    ) = lax.psum(
        (
            row_part,
            col_part,
            scale_part,
            down_bias_part,
            down_part,
            up_bias_part,
            up_part,
            gain_part,
            shift_part,
        ),
        ("rows", "rep"),
    )
    return (
        block_out,
        image_grad,
        row_total * pixel_scale,
        col_total * pixel_scale,
        scale_total * pixel_scale,
        down_bias_total * pixel_scale,
        down_total * pixel_scale,
        up_bias_total * pixel_scale,
        up_total * pixel_scale,
        gain_total * pixel_scale,
        shift_total * pixel_scale,
    )


def solution(mesh):
    placed = (
        P(("groups", "rep"), "rows", None, None),
        P(("groups", "rep"), "rows", None, None),
        P("groups", None),
        P("groups", None),
        P("groups"),
        P("groups"),
        P("groups", None),
        P("groups"),
        P("groups", None),
        P("groups"),
        P("groups"),
    )
    return jax.shard_map(
        per_device,
        mesh=mesh,
        in_specs=placed,
        out_specs=(
            P(("groups", "rep"), "rows", None, None),
            P(("groups", "rep"), "rows", None, None),
            P("groups", None),
            P("groups", None),
            P("groups"),
            P("groups"),
            P("groups", None),
            P("groups"),
            P("groups", None),
            P("groups"),
            P("groups"),
        ),
        check_vma=False,
    )
```

profile of v0, /device:TPU:0, one launch (start us, length us, event | category | flops | bytes accessed | tf_op | source)
XLA Modules:
  0.0 352.1 jit_solution(6242885263664934508)
XLA Ops:
  11.6 16.8 %add_convert_fusion.2 = bf16[1,16,128,256]{3,2,1,0:T(8,128)(2,1)} fusion(f32[1,16,128,256]{3,2,1,0:T(8,128)S(1)} %convert_element_type.158, f32[256]{0:T(256)S(1)} %bitcast.486, f32[256]{0:T(256)S(1)} %bitcast.488, f32[256]{0:T(256)S(1)} %bitcast.428, f32[256]{0:T(256)S(1)} %bitcast.430, f32[256]{0:T(256)S(1)} %bitcast.432, f32[256]{0:T(256)S(1)} %bitcast.434, ...), kind=kLoop, calls=%fused_computation.587 | loop fusion | flops 53477376 | bytes 3197952 | tf_op jit(solution)/shard_map/convert_element_type | solution.py:135
  28.4 2.8 copy.26
  31.2 4.3 %all-to-all-start = ((bf16[1,16,128,256]{3,1,0,2:T(8,128)(2,1)}), bf16[1,16,128,256]{3,1,0,2:T(8,128)(2,1)}, u32[]{:S(2)}, u32[]{:S(2)}) async-start(bf16[1,16,128,256]{3,1,0,2:T(8,128)(2,1)} %copy.26), calls=%async_computation | async-start | bytes 2097152 | tf_op jit(solution)/shard_map/all_to_all | solution.py:137
  35.6 15.0 %all-to-all-done = bf16[1,16,128,256]{3,1,0,2:T(8,128)(2,1)} async-done(((bf16[1,16,128,256]{3,1,0,2:T(8,128)(2,1)}), bf16[1,16,128,256]{3,1,0,2:T(8,128)(2,1)}, u32[]{:S(2)}, u32[]{:S(2)}) %all-to-all-start) | async-done | bytes 1048608 | tf_op jit(solution)/shard_map/all_to_all | solution.py:137
  53.7 17.2 %fusion.269 = bf16[1,64,32,256]{3,2,0,1:T(8,128)(2,1)} fusion(f32[1,64,32,256]{3,2,1,0:T(8,128)S(1)} %bitcast.265, f32[256]{0:T(256)S(1)} %bitcast.384, f32[256]{0:T(256)S(1)} %bitcast.386, f32[256]{0:T(256)S(1)} %bitcast.288, f32[256]{0:T(256)S(1)} %bitcast.290, f32[256]{0:T(256)S(1)} %bitcast.292, f32[256]{0:T(256)S(1)} %bitcast.294, ...), kind=kLoop, calls=%fused_computation.592 | loop fusion | flops 53477376 | bytes 3197952 | tf_op jit(solution)/shard_map/convert_element_type | solution.py:139
  70.9 4.4 %all-to-all-start.1 = ((bf16[1,64,32,256]{3,2,0,1:T(8,128)(2,1)}), bf16[1,64,32,256]{3,2,0,1:T(8,128)(2,1)}, u32[]{:S(2)}, u32[]{:S(2)}) async-start(bf16[1,64,32,256]{3,2,0,1:T(8,128)(2,1)} %fusion.269), calls=%async_computation.1 | async-start | bytes 2097152 | tf_op jit(solution)/shard_map/all_to_all | solution.py:140
  75.4 2.1 fusion.260
  77.4 12.2 %all-to-all-done.1 = bf16[1,64,32,256]{3,2,0,1:T(8,128)(2,1)} async-done(((bf16[1,64,32,256]{3,2,0,1:T(8,128)(2,1)}), bf16[1,64,32,256]{3,2,0,1:T(8,128)(2,1)}, u32[]{:S(2)}, u32[]{:S(2)}) %all-to-all-start.1) | async-done | bytes 1048608 | tf_op jit(solution)/shard_map/all_to_all | solution.py:140
  92.9 3.7 %multiply_convert_fusion = (bf16[2048,1024]{1,0:T(8,128)(2,1)S(1)}, f32[2048,1024]{1,0:T(8,128)S(1)}) fusion(f32[1024]{0:T(1024)S(1)} %copy-done.15, bf16[2048,256]{1,0:T(8,128)(2,1)S(1)} %add_convert_fusion, bf16[256,1024]{1,0:T(8,128)(2,1)S(1)} %copy-done), kind=kOutput, calls=%fused_computation.260 | convolution fusion | flops 1094713344 | bytes 14159872 | tf_op jit(solution)/shard_map/dot_general | solution.py:75
  96.7 3.1 fusion.262
  99.8 7.0 %fusion.278 = (f32[1024]{0:T(1024)}, bf16[2048,1024]{1,0:T(8,128)(2,1)S(1)}) fusion(f32[2048,1024]{1,0:T(8,128)S(1)} %get-tuple-element.233, f32[1024]{0:T(1024)S(1)} %copy-done.15, bf16[2048,256]{1,0:T(8,128)(2,1)S(1)} %get-tuple-element.127, bf16[1024,256]{1,0:T(8,128)(2,1)S(1)} %copy-done.14), kind=kOutput, calls=%fused_computation.614 | convolution fusion | flops 1117780992 | bytes 14163968 | tf_op jit(solution)/shard_map/dot_general | solution.py:82
  106.8 2.3 multiply_reduce_fusion
  111.9 4.2 %all-to-all-start.2 = ((bf16[1,16,128,256]{3,1,0,2:T(8,128)(2,1)}), bf16[1,16,128,256]{3,1,0,2:T(8,128)(2,1)}, u32[]{:S(2)}, u32[]{:S(2)}) async-start(bf16[1,16,128,256]{3,1,0,2:T(8,128)(2,1)} %copy.31), calls=%async_computation.2 | async-start | bytes 2097152 | tf_op jit(solution)/shard_map/all_to_all | solution.py:158
  116.4 5.0 %fusion.265 = f32[256,1024]{1,0:T(8,128)} fusion(bf16[2048,256]{1,0:T(8,128)(2,1)} %copy-done.8, bf16[2048,1024]{1,0:T(8,128)(2,1)} %copy-done.17), kind=kOutput, calls=%fused_computation.580 | convolution fusion | flops 1073741824 | bytes 6291456 | tf_op jit(solution)/shard_map/dot_general | solution.py:106
  121.4 2.3 fusion.279
  123.7 6.9 %all-to-all-done.2 = bf16[1,16,128,256]{3,1,0,2:T(8,128)(2,1)} async-done(((bf16[1,16,128,256]{3,1,0,2:T(8,128)(2,1)}), bf16[1,16,128,256]{3,1,0,2:T(8,128)(2,1)}, u32[]{:S(2)}, u32[]{:S(2)}) %all-to-all-start.2) | async-done | bytes 1048608 | tf_op jit(solution)/shard_map/all_to_all | solution.py:158
  132.6 2.2 copy-done.2
  134.7 4.1 %multiply_reduce_fusion.1 = (f32[256]{0:T(256)S(1)}, f32[256]{0:T(256)S(1)}, f32[256]{0:T(256)S(1)}, f32[256]{0:T(256)S(1)}, f32[256]{0:T(256)S(1)}, /*index=5*/...) fusion(f32[1,64,32,256]{3,2,1,0:T(8,128)S(1)} %bitcast.269, ...), kind=kLoop, calls=%fused_computation.527 | loop fusion | flops 18869760 | bytes 4212736 | tf_op jit(solution)/shard_map/reduce_sum | solution.py:49
  138.9 4.9 %multiply_reduce_fusion.19 = (f32[256]{0:T(256)S(1)}, f32[256]{0:T(256)S(1)}, f32[256]{0:T(256)S(1)}, f32[256]{0:T(256)S(1)}, f32[256]{0:T(256)S(1)}, /*index=5*...) fusion(f32[1,64,32,256]{3,2,1,0:T(8,128)S(1)} %bitcast.270, ...), kind=kLoop, calls=%fused_computation.545 | loop fusion | flops 18869760 | bytes 4212736 | tf_op jit(solution)/shard_map/reduce_sum | solution.py:49
  143.8 17.4 %fusion.270 = bf16[1,64,32,256]{3,2,0,1:T(8,128)(2,1)} fusion(f32[1,64,32,256]{3,2,1,0:T(8,128)S(1)} %bitcast.271, f32[256]{0:T(256)S(1)} %bitcast.287, f32[256]{0:T(256)S(1)} %bitcast.325, f32[256]{0:T(256)S(1)} %bitcast.363, f32[256]{0:T(256)S(1)} %bitcast.383, f32[256]{0:T(256)S(1)} %bitcast.381, f32[256]{0:T(256)S(1)} %bitcast.379, ...), kind=kLoop, calls=%fused_computation.593 | loop fusion | flops 53477376 | bytes 3197952 | tf_op jit(solution)/shard_map/convert_element_type | solution.py:163
  161.2 4.2 %all-to-all-start.3 = ((bf16[1,64,32,256]{3,2,0,1:T(8,128)(2,1)}), bf16[1,64,32,256]{3,2,0,1:T(8,128)(2,1)}, u32[]{:S(2)}, u32[]{:S(2)}) async-start(bf16[1,64,32,256]{3,2,0,1:T(8,128)(2,1)} %fusion.270), calls=%async_computation.3 | async-start | bytes 2097152 | tf_op jit(solution)/shard_map/all_to_all | solution.py:164
  165.7 12.7 %multiply_reduce_fusion.38 = (f32[256]{0:T(256)S(1)}, f32[256]{0:T(256)S(1)}, f32[256]{0:T(256)S(1)}, f32[256]{0:T(256)S(1)}, f32[256]{0:T(256)S(1)}, /*index=5*...) fusion(f32[1,64,32,256]{3,2,1,0:T(8,128)} %bitcast.272, ...), kind=kLoop, calls=%fused_computation.564 | loop fusion | flops 14676480 | bytes 4208640 | tf_op jit(solution)/shard_map/reduce_sum | solution.py:49
  178.4 2.1 multiply_reduce_fusion.26
  180.5 4.3 %stack.415 = f32[51,256]{1,0:T(8,128)} concatenate(f32[1,256]{1,0:T(1,128)S(1)} %bitcast.503, f32[1,256]{1,0:T(1,128)S(1)} %bitcast.502, f32[1,256]{1,0:T(1,128)S(1)} %bitcast.501, f32[1,256]{1,0:T(1,128)S(1)} %bitcast.500, f32[1,256]{1,0:T(1,128)S(1)} %bitcast.499, f32[1,256]{1,0:T(1,128)S(1)} %bitcast.498, f32[1,256]{1,0:T(1,128)S(1)} %bitcast.497, f32[1,256]{1,0:T(1,128)S(1)} %bitcast.496, ...), dimensions={0} | concatenate | bytes 104448 | tf_op jit(solution)/shard_map/stack | solution.py:47
  184.8 39.6 %all-reduce.11.cloned.1.call-done = (f32[1024,256]{1,0:T(8,128)}, f32[256,1024]{1,0:T(8,128)}) async-done(((f32[1024,256]{1,0:T(8,128)}, f32[256,1024]{1,0:T(8,128)}), (f32[1024,256]{1,0:T(8,128)}, f32[256,1024]{1,0:T(8,128)})) %all-reduce.11.cloned.1.call-update) | async-done | bytes 2097168 | tf_op jit(solution)/shard_map/psum | solution.py:182
  224.5 2.4 broadcast_multiply_fusion
  229.3 4.6 %fusion.158 = (f32[256]{0:T(256)S(1)}, f32[256]{0:T(256)S(1)}, f32[256]{0:T(256)S(1)}, f32[256]{0:T(256)S(1)}, f32[256]{0:T(256)S(1)}, /*index=5*/f32[256]{0:T(2...) fusion(bf16[1,16,128,256]{3,2,1,0:T(8,128)(2,1)S(1)} %bitcast.2, ...), kind=kLoop, calls=%fused_computation.414 | loop fusion | flops 19394048 | bytes 3164160 | tf_op jit(solution)/shard_map/reduce_sum | solution.py:49
  233.9 4.8 %fusion.157 = (f32[256]{0:T(256)S(1)}, f32[256]{0:T(256)S(1)}, f32[256]{0:T(256)S(1)}, f32[256]{0:T(256)S(1)}, f32[256]{0:T(256)S(1)}, /*index=5*/f32[256]{0:T(2...) fusion(bf16[1,16,128,256]{3,2,1,0:T(8,128)(2,1)S(1)} %bitcast.2, ...), kind=kLoop, calls=%fused_computation.413 | loop fusion | flops 19394048 | bytes 3164160 | tf_op jit(solution)/shard_map/reduce_sum | solution.py:49
  238.7 3.9 %fusion.156 = (f32[256]{0:T(256)S(1)}, f32[256]{0:T(256)S(1)}, f32[256]{0:T(256)S(1)}, f32[256]{0:T(256)S(1)}, f32[256]{0:T(256)S(1)}, /*index=5*/f32[256]{0:T(2...) fusion(bf16[1,16,128,256]{3,2,1,0:T(8,128)(2,1)S(1)} %bitcast.2, ...), kind=kLoop, calls=%fused_computation.412 | loop fusion | flops 16773376 | bytes 4209664 | tf_op jit(solution)/shard_map/reduce_sum | solution.py:49
  242.8 4.3 %stack.363 = f32[51,256]{1,0:T(8,128)} concatenate(f32[1,256]{1,0:T(1,128)S(1)} %bitcast.505, f32[1,256]{1,0:T(1,128)S(1)} %bitcast.506, f32[1,256]{1,0:T(1,128)S(1)} %bitcast.507, f32[1,256]{1,0:T(1,128)S(1)} %bitcast.508, f32[1,256]{1,0:T(1,128)S(1)} %bitcast.509, f32[1,256]{1,0:T(1,128)S(1)} %bitcast.510, f32[1,256]{1,0:T(1,128)S(1)} %bitcast.511, f32[1,256]{1,0:T(1,128)S(1)} %bitcast.512, ...), dimensions={0} | concatenate | bytes 104448 | tf_op jit(solution)/shard_map/stack | solution.py:47
  247.2 18.0 %fusion.102 = bf16[1,16,128,256]{3,2,1,0:T(8,128)(2,1)} fusion(f32[1,16,128,256]{3,2,1,0:T(8,128)S(1)} %convert_element_type.154, bf16[1,16,128,256]{3,2,1,0:T(8,128)(2,1)} %param.12, bf16[1,16,128,256]{3,2,1,0:T(8,128)(2,1)} %bitcast.277, f32[256]{0:T(256)S(1)} %bitcast.487, f32[256]{0:T(256)S(1)} %bitcast.489, f32[256]{0:T(256)S(1)} %bitcast.429, ...), kind=kLoop, calls=%fused_computation.358 | loop fusion | flops 55050240 | bytes 5295104 | tf_op jit(solution)/shard_map/convert_element_type | solution.py:171
  265.1 71.1 %all-reduce.9.cloned.1.call-done = (f32[51,256]{1,0:T(8,128)}, f32[51,256]{1,0:T(8,128)}, f32[256]{0:T(256)}, f32[256]{0:T(256)}, f32[1024]{0:T(1024)}, /*index=5*/f32[256]{0:T(256)}, f32[256]{0:T(256)}) async-done(((f32[51,256]{1,0:T(8,128)}, f32[51,256]{1,0:T(8,128)}, f32[256]{0:T(256)}, f32[256]{0:T(256)}, f32[1024]{0:T(1024)}, /*index=5*/f32[256]{0:T(256)}, f32[256]{0:T(256)}), (f32[51,256]{1,0:T(8,128)}, ...) | async-done | bytes 112656 | tf_op jit(solution)/shard_map/psum | solution.py:182
  (78 shorter events, 27.6 us)
Async XLA Ops:
  7.2 85.6 %copy-start = (bf16[256,1024]{1,0:T(8,128)(2,1)S(1)}, bf16[256,1024]{1,0:T(8,128)(2,1)}, u32[]{:S(2)}) copy-start(bf16[256,1024]{1,0:T(8,128)(2,1)} %param.17) | copy-start | bytes 1572868
  28.4 7.1 %copy-start.10 = (f32[51,256]{1,0:T(8,128)S(1)}, f32[51,256]{1,0:T(8,128)}, u32[]{:S(2)}) copy-start(f32[51,256]{1,0:T(8,128)} %param.14) | copy-start | bytes 156676
  31.2 19.4 %all-to-all-start = ((bf16[1,16,128,256]{3,1,0,2:T(8,128)(2,1)}), bf16[1,16,128,256]{3,1,0,2:T(8,128)(2,1)}, u32[]{:S(2)}, u32[]{:S(2)}) async-start(bf16[1,16,128,256]{3,1,0,2:T(8,128)(2,1)} %copy.26), calls=%async_computation | async-start | bytes 2097152 | tf_op jit(solution)/shard_map/all_to_all | solution.py:137
  52.3 1.4 copy-start.1
  53.7 21.6 %copy-start.13 = (f32[256]{0:T(256)S(1)}, f32[256]{0:T(256)}, u32[]{:S(2)}) copy-start(f32[256]{0:T(256)} %param.21) | copy-start | bytes 3076
  70.9 18.7 %all-to-all-start.1 = ((bf16[1,64,32,256]{3,2,0,1:T(8,128)(2,1)}), bf16[1,64,32,256]{3,2,0,1:T(8,128)(2,1)}, u32[]{:S(2)}, u32[]{:S(2)}) async-start(bf16[1,64,32,256]{3,2,0,1:T(8,128)(2,1)} %fusion.269), calls=%async_computation.1 | async-start | bytes 2097152 | tf_op jit(solution)/shard_map/all_to_all | solution.py:140
  89.7 2.4 copy-start.11
  89.7 2.4 copy-start.12
  91.0 1.8 copy-start.15
  92.8 3.8 %copy-start.8 = (bf16[2048,256]{1,0:T(8,128)(2,1)}, bf16[2048,256]{1,0:T(8,128)(2,1)S(1)}, u32[]{:S(2)}) copy-start(bf16[2048,256]{1,0:T(8,128)(2,1)S(1)} %add_convert_fusion) | copy-start | bytes 3145732
  92.8 3.8 %copy-start.5 = (bf16[1,16,128,256]{3,2,1,0:T(8,128)(2,1)S(1)}, bf16[1,16,128,256]{3,2,1,0:T(8,128)(2,1)}, u32[]{:S(2)}) copy-start(bf16[1,16,128,256]{3,2,1,0:T(8,128)(2,1)} %param.11) | copy-start | bytes 3145732
  92.8 3.8 %copy-start.7 = (bf16[1,16,128,256]{3,2,1,0:T(8,128)(2,1)S(1)}, bf16[1,16,128,256]{3,2,1,0:T(8,128)(2,1)}, u32[]{:S(2)}) copy-start(bf16[1,16,128,256]{3,2,1,0:T(8,128)(2,1)} %param.12) | copy-start | bytes 3145732
  92.8 3.8 %copy-start.14 = (bf16[1024,256]{1,0:T(8,128)(2,1)S(1)}, bf16[1024,256]{1,0:T(8,128)(2,1)}, u32[]{:S(2)}) copy-start(bf16[1024,256]{1,0:T(8,128)(2,1)} %param.19) | copy-start | bytes 1572868
  92.9 3.8 %copy-start.16 = (f32[256]{0:T(256)S(1)}, f32[256]{0:T(256)}, u32[]{:S(2)}) copy-start(f32[256]{0:T(256)} %param.20) | copy-start | bytes 3076
  96.6 3.2 copy-start.18
  99.8 7.0 %copy-start.20 = (bf16[2048,256]{1,0:T(8,128)(2,1)}, bf16[2048,256]{1,0:T(8,128)(2,1)S(1)}, u32[]{:S(2)}) copy-start(bf16[2048,256]{1,0:T(8,128)(2,1)S(1)} %get-tuple-element.127) | copy-start | bytes 3145732
  106.8 2.3 copy-start.17
  111.9 18.7 %all-to-all-start.2 = ((bf16[1,16,128,256]{3,1,0,2:T(8,128)(2,1)}), bf16[1,16,128,256]{3,1,0,2:T(8,128)(2,1)}, u32[]{:S(2)}, u32[]{:S(2)}) async-start(bf16[1,16,128,256]{3,1,0,2:T(8,128)(2,1)} %copy.31), calls=%async_computation.2 | async-start | bytes 2097152 | tf_op jit(solution)/shard_map/all_to_all | solution.py:158
  116.2 108.3 %all-reduce.11.cloned.1.call-start = ((), (), s32[]{:S(2)}) async-start(), calls=%async_computation.5 | async-start | bytes 4194304 | tf_op jit(solution)/shard_map/psum | solution.py:182
  116.4 5.0 %copy-start.19 = (bf16[2048,1024]{1,0:T(8,128)(2,1)S(1)}, bf16[2048,1024]{1,0:T(8,128)(2,1)}, u32[]{:S(2)}) copy-start(bf16[2048,1024]{1,0:T(8,128)(2,1)} %copy-done.18) | copy-start | bytes 12582916
  116.4 5.0 %copy-start.21 = (bf16[2048,256]{1,0:T(8,128)(2,1)S(1)}, bf16[2048,256]{1,0:T(8,128)(2,1)}, u32[]{:S(2)}) copy-start(bf16[2048,256]{1,0:T(8,128)(2,1)} %copy-done.20) | copy-start | bytes 3145732
  132.4 2.3 copy-start.2
  132.5 11.2 %copy-start.3 = (f32[1,4,16,32,256]{4,3,2,1,0:T(8,128)}, f32[1,4,16,32,256]{4,3,2,1,0:T(8,128)S(1)}, u32[]{:S(2)}) copy-start(f32[1,4,16,32,256]{4,3,2,1,0:T(8,128)S(1)} %copy.33) | copy-start | bytes 6291460
  161.2 66.8 %all-to-all-start.3 = ((bf16[1,64,32,256]{3,2,0,1:T(8,128)(2,1)}), bf16[1,64,32,256]{3,2,0,1:T(8,128)(2,1)}, u32[]{:S(2)}, u32[]{:S(2)}) async-start(bf16[1,64,32,256]{3,2,0,1:T(8,128)(2,1)} %fusion.270), calls=%async_computation.3 | async-start | bytes 2097152 | tf_op jit(solution)/shard_map/all_to_all | solution.py:164
  165.4 170.8 %all-reduce.9.cloned.1.call-start = ((), (), s32[]{:S(2)}) async-start(), calls=%async_computation.4 | async-start | bytes 245760 | tf_op jit(solution)/shard_map/psum | solution.py:182
  224.5 2.4 copy-start.9
  229.3 13.5 %copy-start.4 = (bf16[1,16,4,32,256]{4,3,2,1,0:T(8,128)(2,1)}, bf16[1,16,4,32,256]{4,3,2,1,0:T(8,128)(2,1)S(1)}, u32[]{:S(2)}) copy-start(bf16[1,16,4,32,256]{4,3,2,1,0:T(8,128)(2,1)S(1)} %copy.35) | copy-start | bytes 3145732
  233.9 4.8 %copy-start.6 = (bf16[1,16,128,256]{3,2,1,0:T(8,128)(2,1)S(1)}, bf16[1,16,128,256]{3,2,1,0:T(8,128)(2,1)}, u32[]{:S(2)}) copy-start(bf16[1,16,128,256]{3,2,1,0:T(8,128)(2,1)} %param.11) | copy-start | bytes 3145732
Sparse Core Ops, SparseCore 0:
  123.8 100.5 all-reduce.10
  247.3 88.8 all-reduce.8
where the time goes:
time: 354 us; the launch traced here: 352 us
  waiting for transfers between devices  145 us (41%)
  other arithmetic  129 us (36%)
  matrix products  23.4 us (7%)
  local copies, waits for them, and re-layouts  22.6 us (6%)
  starting transfers between devices  17.7 us (5%)
  between operations  14.5 us (4%)
    psum x2, waiting for transfers between devices, per_device(): lax.psum((row_part, col_part, scale_part, down_bias_part, down_part, up_b...  111 us
    reduce_sum x7, other arithmetic, tap_sums(): jnp.sum(cot_field * lax.slice_in_dim(padded, offset, offset + length, axi...  37.1 us
    convert_element_type x1, other arithmetic, per_device(): image_grad = (cotangent.astype(jnp.float32) + slide_padded(pad_along(row_...  18 us
    convert_element_type x1, other arithmetic, per_device(): row_local = slide_padded(pad_along(grad_float, 1, half_reach), col_taps[:...  17.4 us
    convert_element_type x1, other arithmetic, per_device(): slide_padded(mix_padded, col_taps, 1, mix_columns.shape[1])  17.2 us
    convert_element_type x1, other arithmetic, per_device(): slide_padded(image_padded, row_taps, 2, columns).astype(jnp.bfloat16)  16.8 us
    all_to_all x1, waiting for transfers between devices, per_device(): lax.all_to_all(row_mix, 'rows', split_axis=2, concat_axis=1, tiled=True)  15 us
    all_to_all x1, waiting for transfers between devices, per_device(): lax.all_to_all(col_local, 'rows', split_axis=1, concat_axis=2, tiled=True)  12.2 us
  transfers between devices with their start and end apart: 6, of which 5 were waited for; matrix products, arithmetic and copies ran while one was open for 22% of the time, Pallas kernels for 0%

commit v1 on v0

--- a/solution.py
+++ b/solution.py
@@ -169,7 +169,17 @@
         cotangent.astype(jnp.float32)
         + slide_padded(pad_along(row_float, 2, half_reach), row_taps[::-1], 2, columns)
     ).astype(jnp.bfloat16)
-    (
+    early = (scale_part, down_bias_part, down_part, up_bias_part, up_part, gain_part, shift_part)
+    flat = lax.psum(
+        jnp.concatenate([part.reshape(-1) for part in early]) * pixel_scale, ("rows", "rep")
+    )
+    scale_total, down_bias_total, down_total, up_bias_total, up_total, gain_total, shift_total = (
+        split_like(flat, early)
+    )
+    row_total, col_total = exchange_sum((row_part * pixel_scale, col_part * pixel_scale), ("rows", "rep"))
+    return (
+        block_out,
+        image_grad,
         row_total,
         col_total,
         scale_total,
@@ -179,33 +189,29 @@
         up_total,
         gain_total,
         shift_total,
-    ) = lax.psum(
-        (
-            row_part,
-            col_part,
-            scale_part,
-            down_bias_part,
-            down_part,
-            up_bias_part,
-            up_part,
-            gain_part,
-            shift_part,
-        ),
-        ("rows", "rep"),
-    )
-    return (
-        block_out,
-        image_grad,
-        row_total * pixel_scale,
-        col_total * pixel_scale,
-        scale_total * pixel_scale,
-        down_bias_total * pixel_scale,
-        down_total * pixel_scale,
-        up_bias_total * pixel_scale,
-        up_total * pixel_scale,
-        gain_total * pixel_scale,
-        shift_total * pixel_scale,
-    )
+    )
+
+
+def exchange_sum(parts, axes):
+    count = 1
+    for axis in axes:
+        count *= lax.axis_size(axis)
+    flat = jnp.concatenate([part.reshape(-1) for part in parts])
+    piece = -(-flat.shape[0] // (count * 128)) * 128
+    flat = jnp.pad(flat, (0, piece * count - flat.shape[0]))
+    spread = lax.all_to_all(flat.reshape(count, piece), axes, 0, 0, tiled=True)
+    mine = jnp.sum(spread, axis=0, keepdims=True)
+    whole = lax.all_to_all(jnp.broadcast_to(mine, (count, piece)), axes, 0, 0, tiled=True)
+    return split_like(whole.reshape(-1), parts)
+
+
+def split_like(flat, parts):
+    out = []
+    at = 0
+    for part in parts:
+        out.append(flat[at : at + part.size].reshape(part.shape))
+        at += part.size
+    return tuple(out)
 
 
 def solution(mesh):

time: 354 us -> 345 us (0.975); the launches traced: 352 us -> 339 us
  waiting for transfers between devices: 145 us -> 58.8 us
  other arithmetic: 129 us -> 183 us
  local copies, waits for them, and re-layouts: 22.6 us -> 39.5 us
  starting transfers between devices: 17.7 us -> 25.7 us
  matrix products: 23.4 us -> 17.1 us
    psum x2 -> x1, waiting for transfers between devices: 111 us -> 27.9 us  [per_device(): lax.psum(jnp.concatenate([part.reshape(-1) for part in early]) * pixel_sc...]
    convert_element_type x1, other arithmetic: 18 us -> 54.5 us  [per_device(): image_grad = (cotangent.astype(jnp.float32) + slide_padded(pad_along(row_...]
    convert_element_type x1, other arithmetic: 17.4 us -> 43 us  [per_device(): row_local = slide_padded(pad_along(grad_float, 1, half_reach), col_taps[:...]
    unnamed x44 -> x46, local copies, waits for them, and re-layouts: 3.68 us -> 14.4 us
    mul x9 -> x3, other arithmetic: 12.5 us -> 3.1 us  [the longest x1 3.08 us: per_device(): jnp.concatenate([part.reshape(-1) for part in early]) * pixel_scale]
    slice x0 -> x6, local copies, waits for them, and re-layouts: none -> 8.82 us  [split_like(): out.append(flat[at:at + part.size].reshape(part.shape))]
    another operation x2, local copies, waits for them, and re-layouts: 8.63 us -> 0.35 us  [tap_sums(): jnp.stack([jnp.sum(cot_field * lax.slice_in_dim(padded, offset, offset +...]
    all_to_all x0 -> x2, starting transfers between devices: none -> 7.65 us  [the longest x1 3.89 us: exchange_sum(): spread = lax.all_to_all(flat.reshape(count, piece), axes, 0, 0, tiled=True)]
  transfers between devices with their start and end apart: 6 -> 7, of which waited for: 5 -> 4; matrix products, arithmetic and copies ran while one was open for 22% -> 45% of each run, Pallas kernels for 0% -> 0%
where the time goes in v1:
time: 345 us; the launch traced here: 339 us
  other arithmetic  183 us (53%)
  waiting for transfers between devices  58.8 us (17%)
  local copies, waits for them, and re-layouts  39.5 us (11%)
  starting transfers between devices  25.7 us (7%)
  matrix products  17.1 us (5%)
  between operations  14.8 us (4%)
    convert_element_type x1, other arithmetic, per_device(): image_grad = (cotangent.astype(jnp.float32) + slide_padded(pad_along(row_...  54.5 us
    convert_element_type x1, other arithmetic, per_device(): row_local = slide_padded(pad_along(grad_float, 1, half_reach), col_taps[:...  43 us
    reduce_sum x7, other arithmetic, tap_sums(): jnp.sum(cot_field * lax.slice_in_dim(padded, offset, offset + length, axi...  35.5 us
    psum x1, waiting for transfers between devices, per_device(): lax.psum(jnp.concatenate([part.reshape(-1) for part in early]) * pixel_sc...  27.9 us
    convert_element_type x1, other arithmetic, per_device(): slide_padded(mix_padded, col_taps, 1, mix_columns.shape[1])  17.2 us
    convert_element_type x1, other arithmetic, per_device(): slide_padded(image_padded, row_taps, 2, columns).astype(jnp.bfloat16)  16.8 us
    all_to_all x1, waiting for transfers between devices, per_device(): lax.all_to_all(row_mix, 'rows', split_axis=2, concat_axis=1, tiled=True)  15.1 us
    unnamed x46, local copies, waits for them, and re-layouts  14.4 us
  transfers between devices with their start and end apart: 7, of which 4 were waited for; matrix products, arithmetic and copies ran while one was open for 45% of the time, Pallas kernels for 0%

profile of v1, /device:TPU:0, one launch (start us, length us, event | category | flops | bytes accessed | tf_op | source)
XLA Modules:
  0.0 338.9 jit_solution(16590017630585937112)
XLA Ops:
  11.6 16.8 %add_convert_fusion.2 = bf16[1,16,128,256]{3,2,1,0:T(8,128)(2,1)} fusion(f32[1,16,128,256]{3,2,1,0:T(8,128)S(1)} %convert_element_type.160, f32[256]{0:T(256)S(1)} %bitcast.495, f32[256]{0:T(256)S(1)} %bitcast.497, f32[256]{0:T(256)S(1)} %bitcast.437, f32[256]{0:T(256)S(1)} %bitcast.439, f32[256]{0:T(256)S(1)} %bitcast.441, f32[256]{0:T(256)S(1)} %bitcast.443, ...), kind=kLoop, calls=%fused_computation.587 | loop fusion | flops 53477376 | bytes 3197952 | tf_op jit(solution)/shard_map/convert_element_type | solution.py:135
  28.5 2.8 copy.46
  31.2 4.3 %all-to-all-start = ((bf16[1,16,128,256]{3,1,0,2:T(8,128)(2,1)}), bf16[1,16,128,256]{3,1,0,2:T(8,128)(2,1)}, u32[]{:S(2)}, u32[]{:S(2)}) async-start(bf16[1,16,128,256]{3,1,0,2:T(8,128)(2,1)} %copy.46), calls=%async_computation | async-start | bytes 2097152 | tf_op jit(solution)/shard_map/all_to_all | solution.py:137
  35.6 15.1 %all-to-all-done = bf16[1,16,128,256]{3,1,0,2:T(8,128)(2,1)} async-done(((bf16[1,16,128,256]{3,1,0,2:T(8,128)(2,1)}), bf16[1,16,128,256]{3,1,0,2:T(8,128)(2,1)}, u32[]{:S(2)}, u32[]{:S(2)}) %all-to-all-start) | async-done | bytes 1048608 | tf_op jit(solution)/shard_map/all_to_all | solution.py:137
  53.7 17.2 %fusion.272 = bf16[1,64,32,256]{3,2,0,1:T(8,128)(2,1)} fusion(f32[1,64,32,256]{3,2,1,0:T(8,128)S(1)} %bitcast.272, f32[256]{0:T(256)S(1)} %bitcast.393, f32[256]{0:T(256)S(1)} %bitcast.395, f32[256]{0:T(256)S(1)} %bitcast.297, f32[256]{0:T(256)S(1)} %bitcast.299, f32[256]{0:T(256)S(1)} %bitcast.301, f32[256]{0:T(256)S(1)} %bitcast.303, ...), kind=kLoop, calls=%fused_computation.595 | loop fusion | flops 53477376 | bytes 3197952 | tf_op jit(solution)/shard_map/convert_element_type | solution.py:139
  70.9 4.8 %all-to-all-start.1 = ((bf16[1,64,32,256]{3,2,0,1:T(8,128)(2,1)}), bf16[1,64,32,256]{3,2,0,1:T(8,128)(2,1)}, u32[]{:S(2)}, u32[]{:S(2)}) async-start(bf16[1,64,32,256]{3,2,0,1:T(8,128)(2,1)} %fusion.272), calls=%async_computation.1 | async-start | bytes 2097152 | tf_op jit(solution)/shard_map/all_to_all | solution.py:140
  77.2 12.9 %all-to-all-done.1 = bf16[1,64,32,256]{3,2,0,1:T(8,128)(2,1)} async-done(((bf16[1,64,32,256]{3,2,0,1:T(8,128)(2,1)}), bf16[1,64,32,256]{3,2,0,1:T(8,128)(2,1)}, u32[]{:S(2)}, u32[]{:S(2)}) %all-to-all-start.1) | async-done | bytes 1048608 | tf_op jit(solution)/shard_map/all_to_all | solution.py:140
  93.3 3.7 %multiply_convert_fusion = (bf16[2048,1024]{1,0:T(8,128)(2,1)S(1)}, f32[2048,1024]{1,0:T(8,128)S(1)}) fusion(f32[1024]{0:T(1024)S(1)} %copy-done.17, bf16[2048,256]{1,0:T(8,128)(2,1)S(1)} %add_convert_fusion, bf16[256,1024]{1,0:T(8,128)(2,1)S(1)} %copy-done), kind=kOutput, calls=%fused_computation.260 | convolution fusion | flops 1094713344 | bytes 14159872 | tf_op jit(solution)/shard_map/dot_general | solution.py:75
  97.1 2.6 fusion.262
  100.9 6.4 %fusion.284 = (f32[1024]{0:T(1024)S(1)}, bf16[2048,1024]{1,0:T(8,128)(2,1)S(1)}) fusion(f32[2048,1024]{1,0:T(8,128)S(1)} %get-tuple-element.232, f32[1024]{0:T(1024)S(1)} %copy-done.17, bf16[2048,256]{1,0:T(8,128)(2,1)S(1)} %get-tuple-element.124, bf16[1024,256]{1,0:T(8,128)(2,1)S(1)} %copy-done.16), kind=kOutput, calls=%fused_computation.622 | convolution fusion | flops 1117780992 | bytes 14163968 | tf_op jit(solution)/shard_map/dot_general | solution.py:82
  116.0 4.2 %all-to-all-start.2 = ((bf16[1,16,128,256]{3,1,0,2:T(8,128)(2,1)}), bf16[1,16,128,256]{3,1,0,2:T(8,128)(2,1)}, u32[]{:S(2)}, u32[]{:S(2)}) async-start(bf16[1,16,128,256]{3,1,0,2:T(8,128)(2,1)} %copy.51), calls=%async_computation.2 | async-start | bytes 2097152 | tf_op jit(solution)/shard_map/all_to_all | solution.py:158
  123.1 2.6 constant_dynamic-update-slice_fusion.4
  127.1 2.4 constant_dynamic-update-slice_fusion.2
  132.0 3.1 broadcast_multiply_fusion
  138.2 43.0 %fusion.273 = bf16[1,64,32,256]{3,2,0,1:T(8,128)(2,1)} fusion(f32[1,64,32,256]{3,2,1,0:T(8,128)} %bitcast.276, f32[256]{0:T(256)S(1)} %bitcast.296, f32[256]{0:T(256)S(1)} %bitcast.334, f32[256]{0:T(256)S(1)} %bitcast.372, f32[256]{0:T(256)S(1)} %bitcast.392, f32[256]{0:T(256)S(1)} %bitcast.390, f32[256]{0:T(256)S(1)} %bitcast.388, f32[256]{0:T(256)S(1)} %bitcast.386, ...), kind=kLoop, calls=%fused_computation.596 | loop fusion | flops 53477376 | bytes 3197952 | tf_op jit(solution)/shard_map/convert_element_type | solution.py:163
  181.2 5.3 %multiply_reduce_fusion.1 = (f32[256]{0:T(256)S(1)}, f32[256]{0:T(256)S(1)}, f32[256]{0:T(256)S(1)}, f32[256]{0:T(256)S(1)}, f32[256]{0:T(256)S(1)}, /*index=5*/...) fusion(f32[1,64,32,256]{3,2,1,0:T(8,128)} %bitcast.277, ...), kind=kLoop, calls=%fused_computation.527 | loop fusion | flops 18869760 | bytes 4212736 | tf_op jit(solution)/shard_map/reduce_sum | solution.py:49
  186.6 4.9 %multiply_reduce_fusion.19 = (f32[256]{0:T(256)S(1)}, f32[256]{0:T(256)S(1)}, f32[256]{0:T(256)S(1)}, f32[256]{0:T(256)S(1)}, f32[256]{0:T(256)S(1)}, /*index=5*...) fusion(f32[1,64,32,256]{3,2,1,0:T(8,128)S(1)} %bitcast.279, ...), kind=kLoop, calls=%fused_computation.545 | loop fusion | flops 18869760 | bytes 4212736 | tf_op jit(solution)/shard_map/reduce_sum | solution.py:49
  191.5 4.5 %all-to-all-start.3 = ((bf16[1,64,32,256]{3,2,0,1:T(8,128)(2,1)}), bf16[1,64,32,256]{3,2,0,1:T(8,128)(2,1)}, u32[]{:S(2)}, u32[]{:S(2)}) async-start(bf16[1,64,32,256]{3,2,0,1:T(8,128)(2,1)} %fusion.273), calls=%async_computation.3 | async-start | bytes 2097152 | tf_op jit(solution)/shard_map/all_to_all | solution.py:164
  196.0 2.3 multiply_reduce_fusion.26
  198.2 9.8 %multiply_reduce_fusion.38 = (f32[256]{0:T(256)S(1)}, f32[256]{0:T(256)S(1)}, f32[256]{0:T(256)S(1)}, f32[256]{0:T(256)S(1)}, f32[256]{0:T(256)S(1)}, /*index=5*...) fusion(f32[1,64,32,256]{3,2,1,0:T(8,128)} %bitcast.278, ...), kind=kLoop, calls=%fused_computation.564 | loop fusion | flops 14676480 | bytes 4208640 | tf_op jit(solution)/shard_map/reduce_sum | solution.py:49
  208.2 27.9 %all-reduce.7.cloned.1.call-done = f32[526336]{0:T(1024)} async-done(((f32[526336]{0:T(1024)}), f32[526336]{0:T(1024)}) %all-reduce.7.cloned.1.call-update) | async-done | bytes 2105360 | tf_op jit(solution)/shard_map/psum | solution.py:173
  236.1 3.0 fusion.276
  239.1 2.4 reshape.802
  241.5 2.5 slice.1565
  246.6 4.6 %fusion.158 = (f32[256]{0:T(256)S(1)}, f32[256]{0:T(256)S(1)}, f32[256]{0:T(256)S(1)}, f32[256]{0:T(256)S(1)}, f32[256]{0:T(256)S(1)}, /*index=5*/f32[256]{0:T(2...) fusion(bf16[1,16,128,256]{3,2,1,0:T(8,128)(2,1)S(1)} %bitcast.2, ...), kind=kLoop, calls=%fused_computation.414 | loop fusion | flops 19394048 | bytes 3164160 | tf_op jit(solution)/shard_map/reduce_sum | solution.py:49
  251.2 4.8 %fusion.157 = (f32[256]{0:T(256)S(1)}, f32[256]{0:T(256)S(1)}, f32[256]{0:T(256)S(1)}, f32[256]{0:T(256)S(1)}, f32[256]{0:T(256)S(1)}, /*index=5*/f32[256]{0:T(2...) fusion(bf16[1,16,128,256]{3,2,1,0:T(8,128)(2,1)S(1)} %bitcast.2, ...), kind=kLoop, calls=%fused_computation.413 | loop fusion | flops 19394048 | bytes 3164160 | tf_op jit(solution)/shard_map/reduce_sum | solution.py:49
  256.0 3.9 %fusion.156 = (f32[256]{0:T(256)S(1)}, f32[256]{0:T(256)S(1)}, f32[256]{0:T(256)S(1)}, f32[256]{0:T(256)S(1)}, f32[256]{0:T(256)S(1)}, /*index=5*/f32[256]{0:T(2...) fusion(bf16[1,16,128,256]{3,2,1,0:T(8,128)(2,1)S(1)} %bitcast.2, ...), kind=kLoop, calls=%fused_computation.412 | loop fusion | flops 16773376 | bytes 4209664 | tf_op jit(solution)/shard_map/reduce_sum | solution.py:49
  260.8 3.9 %all-to-all-start.4 = ((f32[16,1,1664]{2,1,0:T(1,128)}), f32[16,1,1664]{2,1,0:T(1,128)S(1)}, u32[]{:S(2)}, u32[]{:S(2)}) async-start(f32[16,1,1664]{2,1,0:T(1,128)} %bitcast.225), calls=%async_computation.4 | async-start | bytes 212992 | tf_op jit(solution)/shard_map/all_to_all | solution.py:202
  266.0 2.8 convert_element_type.156
  268.8 2.9 all-to-all-done.4
  272.5 3.8 %all-to-all-start.5 = ((f32[16,1,1664]{2,1,0:T(1,128)}), f32[16,1,1664]{2,1,0:T(1,128)S(1)}, u32[]{:S(2)}, u32[]{:S(2)}) async-start(f32[16,1,1664]{2,1,0:T(1,128)} %broadcast_in_dim.2), calls=%async_computation.5 | async-start | bytes 212992 | tf_op jit(solution)/shard_map/all_to_all | solution.py:204
  276.3 54.5 %fusion.102 = bf16[1,16,128,256]{3,2,1,0:T(8,128)(2,1)} fusion(f32[1,16,128,256]{3,2,1,0:T(8,128)} %convert_element_type.156, bf16[1,16,128,256]{3,2,1,0:T(8,128)(2,1)S(1)} %copy-done.11, bf16[1,16,128,256]{3,2,1,0:T(8,128)(2,1)S(1)} %bitcast.284, f32[256]{0:T(256)S(1)} %bitcast.496, f32[256]{0:T(256)S(1)} %bitcast.498, f32[256]{0:T(256)S(1)} %bitcast.438, ...), kind=kLoop, calls=%fused_computation.358 | loop fusion | flops 55050240 | bytes 5295104 | tf_op jit(solution)/shard_map/convert_element_type | solution.py:171
  (90 shorter events, 38.5 us)
Async XLA Ops:
  7.2 86.1 %copy-start = (bf16[256,1024]{1,0:T(8,128)(2,1)S(1)}, bf16[256,1024]{1,0:T(8,128)(2,1)}, u32[]{:S(2)}) copy-start(bf16[256,1024]{1,0:T(8,128)(2,1)} %param.17) | copy-start | bytes 1572868
  28.4 7.1 %copy-start.12 = (f32[51,256]{1,0:T(8,128)S(1)}, f32[51,256]{1,0:T(8,128)}, u32[]{:S(2)}) copy-start(f32[51,256]{1,0:T(8,128)} %param.14) | copy-start | bytes 156676
  31.2 19.4 %all-to-all-start = ((bf16[1,16,128,256]{3,1,0,2:T(8,128)(2,1)}), bf16[1,16,128,256]{3,1,0,2:T(8,128)(2,1)}, u32[]{:S(2)}, u32[]{:S(2)}) async-start(bf16[1,16,128,256]{3,1,0,2:T(8,128)(2,1)} %copy.46), calls=%async_computation | async-start | bytes 2097152 | tf_op jit(solution)/shard_map/all_to_all | solution.py:137
  52.4 1.3 copy-start.1
  53.7 22.0 %copy-start.15 = (f32[256]{0:T(256)S(1)}, f32[256]{0:T(256)}, u32[]{:S(2)}) copy-start(f32[256]{0:T(256)} %param.21) | copy-start | bytes 3076
  70.9 19.3 %all-to-all-start.1 = ((bf16[1,64,32,256]{3,2,0,1:T(8,128)(2,1)}), bf16[1,64,32,256]{3,2,0,1:T(8,128)(2,1)}, u32[]{:S(2)}, u32[]{:S(2)}) async-start(bf16[1,64,32,256]{3,2,0,1:T(8,128)(2,1)} %fusion.272), calls=%async_computation.1 | async-start | bytes 2097152 | tf_op jit(solution)/shard_map/all_to_all | solution.py:140
  90.1 2.4 copy-start.13
  90.1 2.4 copy-start.14
  91.5 1.8 copy-start.17
  93.3 3.8 %copy-start.7 = (bf16[1,16,128,256]{3,2,1,0:T(8,128)(2,1)S(1)}, bf16[1,16,128,256]{3,2,1,0:T(8,128)(2,1)}, u32[]{:S(2)}) copy-start(bf16[1,16,128,256]{3,2,1,0:T(8,128)(2,1)} %param.11) | copy-start | bytes 3145732
  93.3 3.8 %copy-start.10 = (bf16[1,16,128,256]{3,2,1,0:T(8,128)(2,1)S(1)}, bf16[1,16,128,256]{3,2,1,0:T(8,128)(2,1)}, u32[]{:S(2)}) copy-start(bf16[1,16,128,256]{3,2,1,0:T(8,128)(2,1)} %param.12) | copy-start | bytes 3145732
  93.3 3.8 %copy-start.16 = (bf16[1024,256]{1,0:T(8,128)(2,1)S(1)}, bf16[1024,256]{1,0:T(8,128)(2,1)}, u32[]{:S(2)}) copy-start(bf16[1024,256]{1,0:T(8,128)(2,1)} %param.19) | copy-start | bytes 1572868
  93.3 3.8 %copy-start.18 = (f32[256]{0:T(256)S(1)}, f32[256]{0:T(256)}, u32[]{:S(2)}) copy-start(f32[256]{0:T(256)} %param.20) | copy-start | bytes 3076
  116.0 19.2 %all-to-all-start.2 = ((bf16[1,16,128,256]{3,1,0,2:T(8,128)(2,1)}), bf16[1,16,128,256]{3,1,0,2:T(8,128)(2,1)}, u32[]{:S(2)}, u32[]{:S(2)}) async-start(bf16[1,16,128,256]{3,1,0,2:T(8,128)(2,1)} %copy.51), calls=%async_computation.2 | async-start | bytes 2097152 | tf_op jit(solution)/shard_map/all_to_all | solution.py:158
  120.2 115.9 %all-reduce.7.cloned.1.call-start = ((), (), s32[]{:S(2)}) async-start(), calls=%async_computation.6 | async-start | bytes 4210688 | tf_op jit(solution)/shard_map/psum | solution.py:173
  120.4 6.6 %copy-start.9 = (f32[32,8,8,128]{3,1,2,0:T(8,128)S(1)}, f32[32,8,8,128]{3,1,2,0:T(8,128)}, u32[]{:S(2)}) copy-start(f32[32,8,8,128]{3,1,2,0:T(8,128)} %copy.59) | copy-start | bytes 3145732
  138.2 43.0 %copy-start.2 = (f32[1,4,16,32,256]{4,3,2,1,0:T(8,128)S(1)}, f32[1,4,16,32,256]{4,3,2,1,0:T(8,128)}, u32[]{:S(2)}) copy-start(f32[1,4,16,32,256]{4,3,2,1,0:T(8,128)} %copy-done.1) | copy-start | bytes 6291460
  181.2 5.4 %copy-start.4 = (f32[1,4,16,32,256]{4,3,2,1,0:T(8,128)S(1)}, f32[1,4,16,32,256]{4,3,2,1,0:T(8,128)}, u32[]{:S(2)}) copy-start(f32[1,4,16,32,256]{4,3,2,1,0:T(8,128)} %copy.53) | copy-start | bytes 6291460
  191.5 53.8 %all-to-all-start.3 = ((bf16[1,64,32,256]{3,2,0,1:T(8,128)(2,1)}), bf16[1,64,32,256]{3,2,0,1:T(8,128)(2,1)}, u32[]{:S(2)}, u32[]{:S(2)}) async-start(bf16[1,64,32,256]{3,2,0,1:T(8,128)(2,1)} %fusion.273), calls=%async_computation.3 | async-start | bytes 2097152 | tf_op jit(solution)/shard_map/all_to_all | solution.py:164
  196.0 2.3 copy-start.3
  246.6 9.4 %copy-start.5 = (bf16[1,16,4,32,256]{4,3,2,1,0:T(8,128)(2,1)}, bf16[1,16,4,32,256]{4,3,2,1,0:T(8,128)(2,1)S(1)}, u32[]{:S(2)}) copy-start(bf16[1,16,4,32,256]{4,3,2,1,0:T(8,128)(2,1)S(1)} %copy.55) | copy-start | bytes 3145732
  251.2 4.8 %copy-start.8 = (bf16[1,16,128,256]{3,2,1,0:T(8,128)(2,1)S(1)}, bf16[1,16,128,256]{3,2,1,0:T(8,128)(2,1)}, u32[]{:S(2)}) copy-start(bf16[1,16,128,256]{3,2,1,0:T(8,128)(2,1)} %param.11) | copy-start | bytes 3145732
  260.1 16.2 %copy-start.6 = (bf16[1,16,4,32,256]{4,3,2,1,0:T(8,128)(2,1)S(1)}, bf16[1,16,4,32,256]{4,3,2,1,0:T(8,128)(2,1)}, u32[]{:S(2)}) copy-start(bf16[1,16,4,32,256]{4,3,2,1,0:T(8,128)(2,1)} %copy-done.5) | copy-start | bytes 3145732
  260.1 16.2 %copy-start.11 = (bf16[1,16,128,256]{3,2,1,0:T(8,128)(2,1)S(1)}, bf16[1,16,128,256]{3,2,1,0:T(8,128)(2,1)}, u32[]{:S(2)}) copy-start(bf16[1,16,128,256]{3,2,1,0:T(8,128)(2,1)} %param.12) | copy-start | bytes 3145732
  260.8 11.0 %all-to-all-start.4 = ((f32[16,1,1664]{2,1,0:T(1,128)}), f32[16,1,1664]{2,1,0:T(1,128)S(1)}, u32[]{:S(2)}, u32[]{:S(2)}) async-start(f32[16,1,1664]{2,1,0:T(1,128)} %bitcast.225), calls=%async_computation.4 | async-start | bytes 212992 | tf_op jit(solution)/shard_map/all_to_all | solution.py:202
  272.5 58.3 %all-to-all-start.5 = ((f32[16,1,1664]{2,1,0:T(1,128)}), f32[16,1,1664]{2,1,0:T(1,128)S(1)}, u32[]{:S(2)}, u32[]{:S(2)}) async-start(f32[16,1,1664]{2,1,0:T(1,128)} %broadcast_in_dim.2), calls=%async_computation.5 | async-start | bytes 212992 | tf_op jit(solution)/shard_map/all_to_all | solution.py:204
Sparse Core Ops, SparseCore 0:
  135.2 100.7 all-reduce.6

commit v2 on v1

--- a/solution.py
+++ b/solution.py
@@ -169,14 +169,17 @@
         cotangent.astype(jnp.float32)
         + slide_padded(pad_along(row_float, 2, half_reach), row_taps[::-1], 2, columns)
     ).astype(jnp.bfloat16)
-    early = (scale_part, down_bias_part, down_part, up_bias_part, up_part, gain_part, shift_part)
-    flat = lax.psum(
-        jnp.concatenate([part.reshape(-1) for part in early]) * pixel_scale, ("rows", "rep")
-    )
-    scale_total, down_bias_total, down_total, up_bias_total, up_total, gain_total, shift_total = (
-        split_like(flat, early)
-    )
-    row_total, col_total = exchange_sum((row_part * pixel_scale, col_part * pixel_scale), ("rows", "rep"))
+    down_total, up_total = lax.psum((down_part * pixel_scale, up_part * pixel_scale), ("rows", "rep"))
+    small = (row_part, col_part, scale_part, down_bias_part, up_bias_part, gain_part, shift_part)
+    (
+        row_total,
+        col_total,
+        scale_total,
+        down_bias_total,
+        up_bias_total,
+        gain_total,
+        shift_total,
+    ) = exchange_sum(tuple(part * pixel_scale for part in small), ("rows", "rep"))
     return (
         block_out,
         image_grad,

time: 345 us -> 315 us (0.913); the launches traced: 339 us -> 314 us
  other arithmetic: 183 us -> 154 us
  local copies, waits for them, and re-layouts: 39.5 us -> 19.4 us
  blocking collectives: 0 us -> 16.9 us
  matrix products: 17.1 us -> 24.2 us
    convert_element_type x1, other arithmetic: 43 us -> 17.4 us  [per_device(): row_local = slide_padded(pad_along(grad_float, 1, half_reach), col_taps[:...]
    all_to_all x0 -> x1, blocking collectives: none -> 16.9 us  [per_device(): lax.all_to_all(col_local, 'rows', split_axis=1, concat_axis=2, tiled=True)]
    all_to_all x1 -> x0, waiting for transfers between devices: 12.9 us -> none  [per_device(): lax.all_to_all(col_local, 'rows', split_axis=1, concat_axis=2, tiled=True)]
    all_to_all x1, waiting for transfers between devices: 0.01 us -> 7.98 us  [per_device(): lax.all_to_all(col_grad, 'rows', split_axis=2, concat_axis=1, tiled=True)]
    unnamed x46 -> x48, local copies, waits for them, and re-layouts: 14.4 us -> 6.83 us
    psum x1, waiting for transfers between devices: 27.9 us -> 35.3 us  [per_device(): lax.psum((down_part * pixel_scale, up_part * pixel_scale), ('rows', 'rep'))]
    slice x6 -> x4, local copies, waits for them, and re-layouts: 8.82 us -> 1.84 us  [split_like(): out.append(flat[at:at + part.size].reshape(part.shape))]
    all_to_all x1 -> x0, starting transfers between devices: 4.79 us -> none  [per_device(): lax.all_to_all(col_local, 'rows', split_axis=1, concat_axis=2, tiled=True)]
  transfers between devices with their start and end apart: 7 -> 6, of which waited for: 4 -> 3; matrix products, arithmetic and copies ran while one was open for 45% -> 27% of each run, Pallas kernels for 0% -> 0%
where the time goes in v2:
time: 315 us; the launch traced here: 314 us
  other arithmetic  154 us (49%)
  waiting for transfers between devices  58.4 us (19%)
  starting transfers between devices  26.2 us (8%)
  matrix products  24.2 us (8%)
  local copies, waits for them, and re-layouts  19.4 us (6%)
  blocking collectives  16.9 us (5%)
  between operations  14.6 us (5%)
    convert_element_type x1, other arithmetic, per_device(): image_grad = (cotangent.astype(jnp.float32) + slide_padded(pad_along(row_...  54.5 us
    reduce_sum x7, other arithmetic, tap_sums(): jnp.sum(cot_field * lax.slice_in_dim(padded, offset, offset + length, axi...  37.4 us
    psum x1, waiting for transfers between devices, per_device(): lax.psum((down_part * pixel_scale, up_part * pixel_scale), ('rows', 'rep'))  35.3 us
    convert_element_type x1, other arithmetic, per_device(): row_local = slide_padded(pad_along(grad_float, 1, half_reach), col_taps[:...  17.4 us
    all_to_all x1, blocking collectives, per_device(): lax.all_to_all(col_local, 'rows', split_axis=1, concat_axis=2, tiled=True)  16.9 us
    convert_element_type x1, other arithmetic, per_device(): slide_padded(image_padded, row_taps, 2, columns).astype(jnp.bfloat16)  16.8 us
    convert_element_type x1, other arithmetic, per_device(): slide_padded(mix_padded, col_taps, 1, mix_columns.shape[1])  16.7 us
    all_to_all x1, waiting for transfers between devices, per_device(): lax.all_to_all(row_mix, 'rows', split_axis=2, concat_axis=1, tiled=True)  15.1 us
  transfers between devices with their start and end apart: 6, of which 3 were waited for; matrix products, arithmetic and copies ran while one was open for 27% of the time, Pallas kernels for 0%

profile of v2, /device:TPU:0, one launch (start us, length us, event | category | flops | bytes accessed | tf_op | source)
XLA Modules:
  0.0 313.5 jit_solution(4869303773970266542)
XLA Ops:
  11.6 16.8 %add_convert_fusion.2 = bf16[1,16,128,256]{3,2,1,0:T(8,128)(2,1)} fusion(f32[1,16,128,256]{3,2,1,0:T(8,128)S(1)} %convert_element_type.160, f32[256]{0:T(256)S(1)} %bitcast.491, f32[256]{0:T(256)S(1)} %bitcast.493, f32[256]{0:T(256)S(1)} %bitcast.433, f32[256]{0:T(256)S(1)} %bitcast.435, f32[256]{0:T(256)S(1)} %bitcast.437, f32[256]{0:T(256)S(1)} %bitcast.439, ...), kind=kLoop, calls=%fused_computation.587 | loop fusion | flops 53477376 | bytes 3197952 | tf_op jit(solution)/shard_map/convert_element_type | solution.py:135
  28.4 2.8 copy.46
  31.2 4.2 %all-to-all-start = ((bf16[1,16,128,256]{3,1,0,2:T(8,128)(2,1)}), bf16[1,16,128,256]{3,1,0,2:T(8,128)(2,1)}, u32[]{:S(2)}, u32[]{:S(2)}) async-start(bf16[1,16,128,256]{3,1,0,2:T(8,128)(2,1)} %copy.46), calls=%async_computation | async-start | bytes 2097152 | tf_op jit(solution)/shard_map/all_to_all | solution.py:137
  35.6 15.1 %all-to-all-done = bf16[1,16,128,256]{3,1,0,2:T(8,128)(2,1)} async-done(((bf16[1,16,128,256]{3,1,0,2:T(8,128)(2,1)}), bf16[1,16,128,256]{3,1,0,2:T(8,128)(2,1)}, u32[]{:S(2)}, u32[]{:S(2)}) %all-to-all-start) | async-done | bytes 1048608 | tf_op jit(solution)/shard_map/all_to_all | solution.py:137
  50.7 1.6 copy_convert_fusion.1
  52.4 16.7 %fusion.272 = bf16[1,64,32,256]{3,2,0,1:T(8,128)(2,1)S(1)} fusion(f32[1,64,32,256]{3,2,1,0:T(8,128)S(1)} %bitcast.267, f32[256]{0:T(256)S(1)} %bitcast.389, f32[256]{0:T(256)S(1)} %bitcast.391, f32[256]{0:T(256)S(1)} %bitcast.293, f32[256]{0:T(256)S(1)} %bitcast.295, f32[256]{0:T(256)S(1)} %bitcast.297, f32[256]{0:T(256)S(1)} %bitcast.299, ...), kind=kLoop, calls=%fused_computation.594 | loop fusion | flops 53477376 | bytes 3197952 | tf_op jit(solution)/shard_map/convert_element_type | solution.py:139
  69.0 16.9 %all_to_all.69 = bf16[1,64,32,256]{3,2,0,1:T(8,128)(2,1)S(1)} all-to-all(bf16[1,64,32,256]{3,2,0,1:T(8,128)(2,1)S(1)} %fusion.272), channel_id=1, replica_groups=mesh['groups'=2,'rows'=4,'rep'=4] {'rows'}, dimensions={1} | all-to-all | bytes 2097152 | tf_op jit(solution)/shard_map/all_to_all | solution.py:140
  87.9 3.7 %multiply_convert_fusion = (bf16[2048,1024]{1,0:T(8,128)(2,1)S(1)}, f32[2048,1024]{1,0:T(8,128)S(1)}) fusion(f32[1024]{0:T(1024)S(1)} %copy-done.17, bf16[2048,256]{1,0:T(8,128)(2,1)S(1)} %add_convert_fusion, bf16[256,1024]{1,0:T(8,128)(2,1)S(1)} %copy-done), kind=kOutput, calls=%fused_computation.260 | convolution fusion | flops 1094713344 | bytes 14159872 | tf_op jit(solution)/shard_map/dot_general | solution.py:75
  91.7 2.6 fusion.262
  94.3 6.4 %fusion.283 = (f32[1024]{0:T(1024)S(1)}, bf16[2048,1024]{1,0:T(8,128)(2,1)S(1)}) fusion(f32[2048,1024]{1,0:T(8,128)S(1)} %get-tuple-element.232, f32[1024]{0:T(1024)S(1)} %copy-done.17, bf16[2048,256]{1,0:T(8,128)(2,1)S(1)} %get-tuple-element.120, bf16[1024,256]{1,0:T(8,128)(2,1)S(1)} %copy-done.16), kind=kOutput, calls=%fused_computation.618 | convolution fusion | flops 1117780992 | bytes 14163968 | tf_op jit(solution)/shard_map/dot_general | solution.py:82
  100.7 1.9 multiply_reduce_fusion
  105.5 4.5 %all-to-all-start.2 = ((bf16[1,16,128,256]{3,1,0,2:T(8,128)(2,1)}), bf16[1,16,128,256]{3,1,0,2:T(8,128)(2,1)}, u32[]{:S(2)}, u32[]{:S(2)}) async-start(bf16[1,16,128,256]{3,1,0,2:T(8,128)(2,1)} %copy.51), calls=%async_computation.2 | async-start | bytes 2097152 | tf_op jit(solution)/shard_map/all_to_all | solution.py:158
  111.5 4.7 %convolution_multiply_fusion = f32[1024,256]{1,0:T(8,128)} fusion(bf16[2048,1024]{1,0:T(8,128)(2,1)} %copy-done.20, bf16[2048,256]{1,0:T(8,128)(2,1)} %copy-done.21), kind=kOutput, calls=%fused_computation.590 | convolution fusion | flops 1074003968 | bytes 6291456 | tf_op jit(solution)/shard_map/dot_general | solution.py:102
  116.3 8.0 %all-to-all-done.2 = bf16[1,16,128,256]{3,1,0,2:T(8,128)(2,1)} async-done(((bf16[1,16,128,256]{3,1,0,2:T(8,128)(2,1)}), bf16[1,16,128,256]{3,1,0,2:T(8,128)(2,1)}, u32[]{:S(2)}, u32[]{:S(2)}) %all-to-all-start.2) | async-done | bytes 1048608 | tf_op jit(solution)/shard_map/all_to_all | solution.py:158
  124.3 1.6 copy_convert_fusion
  126.0 2.2 copy-done.2
  128.2 4.1 %multiply_reduce_fusion.1 = (f32[256]{0:T(256)S(1)}, f32[256]{0:T(256)S(1)}, f32[256]{0:T(256)S(1)}, f32[256]{0:T(256)S(1)}, f32[256]{0:T(256)S(1)}, /*index=5*/...) fusion(f32[1,64,32,256]{3,2,1,0:T(8,128)S(1)} %bitcast.271, ...), kind=kLoop, calls=%fused_computation.527 | loop fusion | flops 18869760 | bytes 4212736 | tf_op jit(solution)/shard_map/reduce_sum | solution.py:49
  132.3 4.9 %multiply_reduce_fusion.19 = (f32[256]{0:T(256)S(1)}, f32[256]{0:T(256)S(1)}, f32[256]{0:T(256)S(1)}, f32[256]{0:T(256)S(1)}, f32[256]{0:T(256)S(1)}, /*index=5*...) fusion(f32[1,64,32,256]{3,2,1,0:T(8,128)S(1)} %bitcast.272, ...), kind=kLoop, calls=%fused_computation.545 | loop fusion | flops 18869760 | bytes 4212736 | tf_op jit(solution)/shard_map/reduce_sum | solution.py:49
  137.2 17.4 %fusion.273 = bf16[1,64,32,256]{3,2,0,1:T(8,128)(2,1)} fusion(f32[1,64,32,256]{3,2,1,0:T(8,128)S(1)} %bitcast.273, f32[256]{0:T(256)S(1)} %bitcast.292, f32[256]{0:T(256)S(1)} %bitcast.330, f32[256]{0:T(256)S(1)} %bitcast.368, f32[256]{0:T(256)S(1)} %bitcast.388, f32[256]{0:T(256)S(1)} %bitcast.386, f32[256]{0:T(256)S(1)} %bitcast.384, ...), kind=kLoop, calls=%fused_computation.595 | loop fusion | flops 53477376 | bytes 3197952 | tf_op jit(solution)/shard_map/convert_element_type | solution.py:163
  154.6 4.5 %all-to-all-start.3 = ((bf16[1,64,32,256]{3,2,0,1:T(8,128)(2,1)}), bf16[1,64,32,256]{3,2,0,1:T(8,128)(2,1)}, u32[]{:S(2)}, u32[]{:S(2)}) async-start(bf16[1,64,32,256]{3,2,0,1:T(8,128)(2,1)} %fusion.273), calls=%async_computation.3 | async-start | bytes 2097152 | tf_op jit(solution)/shard_map/all_to_all | solution.py:164
  159.1 13.0 %multiply_reduce_fusion.38 = (f32[256]{0:T(256)S(1)}, f32[256]{0:T(256)S(1)}, f32[256]{0:T(256)S(1)}, f32[256]{0:T(256)S(1)}, f32[256]{0:T(256)S(1)}, /*index=5*...) fusion(f32[1,64,32,256]{3,2,1,0:T(8,128)} %bitcast.274, ...), kind=kLoop, calls=%fused_computation.564 | loop fusion | flops 14676480 | bytes 4208640 | tf_op jit(solution)/shard_map/reduce_sum | solution.py:49
  172.1 2.1 multiply_reduce_fusion.26
  175.8 4.6 %fusion.158 = (f32[256]{0:T(256)S(1)}, f32[256]{0:T(256)S(1)}, f32[256]{0:T(256)S(1)}, f32[256]{0:T(256)S(1)}, f32[256]{0:T(256)S(1)}, /*index=5*/f32[256]{0:T(2...) fusion(bf16[1,16,128,256]{3,2,1,0:T(8,128)(2,1)S(1)} %bitcast.2, ...), kind=kLoop, calls=%fused_computation.414 | loop fusion | flops 19394048 | bytes 3164160 | tf_op jit(solution)/shard_map/reduce_sum | solution.py:49
  180.4 4.8 %fusion.157 = (f32[256]{0:T(256)S(1)}, f32[256]{0:T(256)S(1)}, f32[256]{0:T(256)S(1)}, f32[256]{0:T(256)S(1)}, f32[256]{0:T(256)S(1)}, /*index=5*/f32[256]{0:T(2...) fusion(bf16[1,16,128,256]{3,2,1,0:T(8,128)(2,1)S(1)} %bitcast.2, ...), kind=kLoop, calls=%fused_computation.413 | loop fusion | flops 19394048 | bytes 3164160 | tf_op jit(solution)/shard_map/reduce_sum | solution.py:49
  185.2 3.9 %fusion.156 = (f32[256]{0:T(256)S(1)}, f32[256]{0:T(256)S(1)}, f32[256]{0:T(256)S(1)}, f32[256]{0:T(256)S(1)}, f32[256]{0:T(256)S(1)}, /*index=5*/f32[256]{0:T(2...) fusion(bf16[1,16,128,256]{3,2,1,0:T(8,128)(2,1)S(1)} %bitcast.2, ...), kind=kLoop, calls=%fused_computation.412 | loop fusion | flops 16773376 | bytes 4209664 | tf_op jit(solution)/shard_map/reduce_sum | solution.py:49
  190.0 6.9 %all-to-all-start.4 = ((f32[16,1,1792]{2,1,0:T(1,128)}), f32[16,1,1792]{2,1,0:T(1,128)S(1)}, u32[]{:S(2)}, u32[]{:S(2)}) async-start(f32[16,1,1792]{2,1,0:T(1,128)} %bitcast.225), calls=%async_computation.4 | async-start | bytes 229376 | tf_op jit(solution)/shard_map/all_to_all | solution.py:205
  197.0 4.8 %fusion.269 = f32[256,1024]{1,0:T(8,128)} fusion(bf16[2048,256]{1,0:T(8,128)(2,1)} %copy-done.10, bf16[2048,1024]{1,0:T(8,128)(2,1)} %copy-done.19), kind=kOutput, calls=%fused_computation.589 | convolution fusion | flops 1074003968 | bytes 6291456 | tf_op jit(solution)/shard_map/dot_general | solution.py:106
  203.0 1.6 convert_element_type.156
  205.4 6.0 %all-to-all-start.5 = ((f32[16,1,1792]{2,1,0:T(1,128)}), f32[16,1,1792]{2,1,0:T(1,128)S(1)}, u32[]{:S(2)}, u32[]{:S(2)}) async-start(f32[16,1,1792]{2,1,0:T(1,128)} %broadcast_in_dim.2), calls=%async_computation.5 | async-start | bytes 229376 | tf_op jit(solution)/shard_map/all_to_all | solution.py:207
  211.4 54.5 %fusion.102 = bf16[1,16,128,256]{3,2,1,0:T(8,128)(2,1)} fusion(f32[1,16,128,256]{3,2,1,0:T(8,128)} %convert_element_type.156, bf16[1,16,128,256]{3,2,1,0:T(8,128)(2,1)S(1)} %copy-done.9, bf16[1,16,128,256]{3,2,1,0:T(8,128)(2,1)S(1)} %bitcast.279, f32[256]{0:T(256)S(1)} %bitcast.492, f32[256]{0:T(256)S(1)} %bitcast.494, f32[256]{0:T(256)S(1)} %bitcast.434, ...), kind=kLoop, calls=%fused_computation.358 | loop fusion | flops 55050240 | bytes 5295104 | tf_op jit(solution)/shard_map/convert_element_type | solution.py:171
  268.0 35.3 %all-reduce.8.cloned.1.call-done = (f32[1024,256]{1,0:T(8,128)}, f32[256,1024]{1,0:T(8,128)}) async-done(((f32[1024,256]{1,0:T(8,128)}, f32[256,1024]{1,0:T(8,128)}), (f32[1024,256]{1,0:T(8,128)}, f32[256,1024]{1,0:T(8,128)})) %all-reduce.8.cloned.1.call-update) | async-done | bytes 2097168 | tf_op jit(solution)/shard_map/psum | solution.py:172
  303.3 2.4 copy.73
  (91 shorter events, 18.5 us)
Async XLA Ops:
  7.2 80.6 %copy-start = (bf16[256,1024]{1,0:T(8,128)(2,1)S(1)}, bf16[256,1024]{1,0:T(8,128)(2,1)}, u32[]{:S(2)}) copy-start(bf16[256,1024]{1,0:T(8,128)(2,1)} %param.17) | copy-start | bytes 1572868
  28.4 7.0 %copy-start.12 = (f32[51,256]{1,0:T(8,128)S(1)}, f32[51,256]{1,0:T(8,128)}, u32[]{:S(2)}) copy-start(f32[51,256]{1,0:T(8,128)} %param.14) | copy-start | bytes 156676
  31.2 19.4 %all-to-all-start = ((bf16[1,16,128,256]{3,1,0,2:T(8,128)(2,1)}), bf16[1,16,128,256]{3,1,0,2:T(8,128)(2,1)}, u32[]{:S(2)}, u32[]{:S(2)}) async-start(bf16[1,16,128,256]{3,1,0,2:T(8,128)(2,1)} %copy.46), calls=%async_computation | async-start | bytes 2097152 | tf_op jit(solution)/shard_map/all_to_all | solution.py:137
  52.4 33.5 %copy-start.1 = (f32[1,4,16,32,256]{4,3,2,1,0:T(8,128)}, f32[1,4,16,32,256]{4,3,2,1,0:T(8,128)S(1)}, u32[]{:S(2)}) copy-start(f32[1,4,16,32,256]{4,3,2,1,0:T(8,128)S(1)} %copy.48) | copy-start | bytes 6291460
  85.9 1.1 copy-start.13
  85.9 1.1 copy-start.14
  86.0 1.8 copy-start.17
  87.8 3.8 %copy-start.10 = (bf16[2048,256]{1,0:T(8,128)(2,1)}, bf16[2048,256]{1,0:T(8,128)(2,1)S(1)}, u32[]{:S(2)}) copy-start(bf16[2048,256]{1,0:T(8,128)(2,1)S(1)} %add_convert_fusion) | copy-start | bytes 3145732
  87.8 3.8 %copy-start.6 = (bf16[1,16,128,256]{3,2,1,0:T(8,128)(2,1)S(1)}, bf16[1,16,128,256]{3,2,1,0:T(8,128)(2,1)}, u32[]{:S(2)}) copy-start(bf16[1,16,128,256]{3,2,1,0:T(8,128)(2,1)} %param.11) | copy-start | bytes 3145732
  87.8 3.8 %copy-start.8 = (bf16[1,16,128,256]{3,2,1,0:T(8,128)(2,1)S(1)}, bf16[1,16,128,256]{3,2,1,0:T(8,128)(2,1)}, u32[]{:S(2)}) copy-start(bf16[1,16,128,256]{3,2,1,0:T(8,128)(2,1)} %param.12) | copy-start | bytes 3145732
  87.8 3.8 %copy-start.15 = (f32[256]{0:T(256)S(1)}, f32[256]{0:T(256)}, u32[]{:S(2)}) copy-start(f32[256]{0:T(256)} %param.21) | copy-start | bytes 3076
  87.9 3.8 %copy-start.16 = (bf16[1024,256]{1,0:T(8,128)(2,1)S(1)}, bf16[1024,256]{1,0:T(8,128)(2,1)}, u32[]{:S(2)}) copy-start(bf16[1024,256]{1,0:T(8,128)(2,1)} %param.19) | copy-start | bytes 1572868
  87.9 3.8 %copy-start.18 = (f32[256]{0:T(256)S(1)}, f32[256]{0:T(256)}, u32[]{:S(2)}) copy-start(f32[256]{0:T(256)} %param.20) | copy-start | bytes 3076
  91.6 2.7 copy-start.20
  94.3 6.4 %copy-start.21 = (bf16[2048,256]{1,0:T(8,128)(2,1)}, bf16[2048,256]{1,0:T(8,128)(2,1)S(1)}, u32[]{:S(2)}) copy-start(bf16[2048,256]{1,0:T(8,128)(2,1)S(1)} %get-tuple-element.120) | copy-start | bytes 3145732
  100.7 1.9 copy-start.19
  105.5 18.8 %all-to-all-start.2 = ((bf16[1,16,128,256]{3,1,0,2:T(8,128)(2,1)}), bf16[1,16,128,256]{3,1,0,2:T(8,128)(2,1)}, u32[]{:S(2)}, u32[]{:S(2)}) async-start(bf16[1,16,128,256]{3,1,0,2:T(8,128)(2,1)} %copy.51), calls=%async_computation.2 | async-start | bytes 2097152 | tf_op jit(solution)/shard_map/all_to_all | solution.py:158
  125.8 2.3 copy-start.2
  126.0 11.2 %copy-start.3 = (f32[1,4,16,32,256]{4,3,2,1,0:T(8,128)}, f32[1,4,16,32,256]{4,3,2,1,0:T(8,128)S(1)}, u32[]{:S(2)}) copy-start(f32[1,4,16,32,256]{4,3,2,1,0:T(8,128)S(1)} %copy.53) | copy-start | bytes 6291460
  154.6 19.8 %all-to-all-start.3 = ((bf16[1,64,32,256]{3,2,0,1:T(8,128)(2,1)}), bf16[1,64,32,256]{3,2,0,1:T(8,128)(2,1)}, u32[]{:S(2)}, u32[]{:S(2)}) async-start(bf16[1,64,32,256]{3,2,0,1:T(8,128)(2,1)} %fusion.273), calls=%async_computation.3 | async-start | bytes 2097152 | tf_op jit(solution)/shard_map/all_to_all | solution.py:164
  175.8 9.4 %copy-start.4 = (bf16[1,16,4,32,256]{4,3,2,1,0:T(8,128)(2,1)}, bf16[1,16,4,32,256]{4,3,2,1,0:T(8,128)(2,1)S(1)}, u32[]{:S(2)}) copy-start(bf16[1,16,4,32,256]{4,3,2,1,0:T(8,128)(2,1)S(1)} %copy.55) | copy-start | bytes 3145732
  180.4 4.8 %copy-start.7 = (bf16[1,16,128,256]{3,2,1,0:T(8,128)(2,1)S(1)}, bf16[1,16,128,256]{3,2,1,0:T(8,128)(2,1)}, u32[]{:S(2)}) copy-start(bf16[1,16,128,256]{3,2,1,0:T(8,128)(2,1)} %param.11) | copy-start | bytes 3145732
  190.0 14.6 %all-to-all-start.4 = ((f32[16,1,1792]{2,1,0:T(1,128)}), f32[16,1,1792]{2,1,0:T(1,128)S(1)}, u32[]{:S(2)}, u32[]{:S(2)}) async-start(f32[16,1,1792]{2,1,0:T(1,128)} %bitcast.225), calls=%async_computation.4 | async-start | bytes 229376 | tf_op jit(solution)/shard_map/all_to_all | solution.py:205
  197.0 106.4 %all-reduce.8.cloned.1.call-start = ((), (), s32[]{:S(2)}) async-start(), calls=%async_computation.6 | async-start | bytes 4194304 | tf_op jit(solution)/shard_map/psum | solution.py:172
  201.8 1.2 copy-start.5
  203.0 8.4 %copy-start.9 = (bf16[1,16,128,256]{3,2,1,0:T(8,128)(2,1)S(1)}, bf16[1,16,128,256]{3,2,1,0:T(8,128)(2,1)}, u32[]{:S(2)}) copy-start(bf16[1,16,128,256]{3,2,1,0:T(8,128)(2,1)} %param.12) | copy-start | bytes 3145732
  205.4 60.5 %all-to-all-start.5 = ((f32[16,1,1792]{2,1,0:T(1,128)}), f32[16,1,1792]{2,1,0:T(1,128)S(1)}, u32[]{:S(2)}, u32[]{:S(2)}) async-start(f32[16,1,1792]{2,1,0:T(1,128)} %broadcast_in_dim.2), calls=%async_computation.5 | async-start | bytes 229376 | tf_op jit(solution)/shard_map/all_to_all | solution.py:207
  303.3 2.4 copy-start.11
Sparse Core Ops, SparseCore 0:
  202.0 101.3 all-reduce.7

commit v3 on v2

--- a/solution.py
+++ b/solution.py
@@ -131,18 +131,19 @@
     pixel_scale = 1.0 / math.sqrt(
         tiles_here * lax.axis_size("rep") * band_rows * lax.axis_size("rows") * columns
     )
+    image_columns = lax.all_to_all(images, "rows", split_axis=2, concat_axis=1, tiled=True)
+    cot_columns = lax.all_to_all(cotangent, "rows", split_axis=2, concat_axis=1, tiled=True)
     image_padded = pad_along(images.astype(jnp.float32), 2, half_reach)
     row_mix = slide_padded(image_padded, row_taps, 2, columns).astype(jnp.bfloat16)
     row_mix = lax.optimization_barrier(row_mix)
     mix_columns = lax.all_to_all(row_mix, "rows", split_axis=2, concat_axis=1, tiled=True)
     mix_padded = pad_along(mix_columns.astype(jnp.float32), 1, half_reach)
-    col_local = slide_padded(mix_padded, col_taps, 1, mix_columns.shape[1]).astype(jnp.bfloat16)
-    col_mix = lax.all_to_all(col_local, "rows", split_axis=1, concat_axis=2, tiled=True)
+    col_mix = slide_padded(mix_padded, col_taps, 1, mix_columns.shape[1]).astype(jnp.bfloat16)
     col_mix = lax.optimization_barrier(col_mix)
     block_rows, grad_rows, partials = pointwise(
         col_mix.reshape(-1, channels),
-        images.reshape(-1, channels),
-        cotangent.reshape(-1, channels),
+        image_columns.reshape(-1, channels),
+        cot_columns.reshape(-1, channels),
         norm_gain,
         norm_shift,
         up_weight,
@@ -152,14 +153,14 @@
         layer_scale,
     )
     scale_part, down_bias_part, down_part, up_bias_part, up_part, gain_part, shift_part = partials
-    block_out = block_rows.reshape(images.shape)
+    block_out = lax.all_to_all(
+        block_rows.reshape(mix_columns.shape), "rows", split_axis=1, concat_axis=2, tiled=True
+    )
     grad_rows = lax.optimization_barrier(grad_rows)
-    col_grad = grad_rows.reshape(images.shape)
-    grad_columns = lax.all_to_all(col_grad, "rows", split_axis=2, concat_axis=1, tiled=True)
-    grad_float = grad_columns.astype(jnp.float32)
+    grad_float = grad_rows.reshape(mix_columns.shape).astype(jnp.float32)
     col_part = tap_sums(grad_float, mix_padded, taps_count, 1)
     row_local = slide_padded(
-        pad_along(grad_float, 1, half_reach), col_taps[::-1], 1, grad_columns.shape[1]
+        pad_along(grad_float, 1, half_reach), col_taps[::-1], 1, mix_columns.shape[1]
     ).astype(jnp.bfloat16)
     row_grad = lax.all_to_all(row_local, "rows", split_axis=1, concat_axis=2, tiled=True)
     row_grad = lax.optimization_barrier(row_grad)

time: 315 us -> 352 us (1.12); the launches traced: 314 us -> 345 us
  other arithmetic: 154 us -> 178 us
  waiting for transfers between devices: 58.4 us -> 67 us
  local copies, waits for them, and re-layouts: 19.4 us -> 25.7 us
  blocking collectives: 16.9 us -> 12.7 us
    convert_element_type x1, other arithmetic: 16.8 us -> 39 us  [per_device(): slide_padded(image_padded, row_taps, 2, columns).astype(jnp.bfloat16)]
    all_to_all x2 -> x3, waiting for transfers between devices: 7.99 us -> 17.9 us  [the longest x1 12.8 us: per_device(): lax.all_to_all(cotangent, 'rows', split_axis=2, concat_axis=1, tiled=True)]
    reduce_sum x7, other arithmetic: 37.4 us -> 44.1 us  [tap_sums(): jnp.sum(cot_field * lax.slice_in_dim(padded, offset, offset + length, axi...]
    convert_element_type x1 -> x2, local copies, waits for them, and re-layouts: 0.14 us -> 6.23 us  [the longest x1 3.29 us: pointwise(): cot_float = cot_rows.astype(jnp.float32)]
    convert_element_type x1, other arithmetic: 54.5 us -> 48.8 us  [per_device(): image_grad = (cotangent.astype(jnp.float32) + slide_padded(pad_along(row_...]
    all_to_all x1, blocking collectives: 16.9 us -> 12.7 us  [exchange_sum(): spread = lax.all_to_all(flat.reshape(count, piece), axes, 0, 0, tiled=True)]
    all_to_all x1, waiting for transfers between devices: 0.01 us -> 3.75 us  [per_device(): lax.all_to_all(row_local, 'rows', split_axis=1, concat_axis=2, tiled=True)]
    unnamed x48 -> x58, local copies, waits for them, and re-layouts: 6.83 us -> 8.79 us
  transfers between devices with their start and end apart: 6 -> 7, of which waited for: 3 -> 5; matrix products, arithmetic and copies ran while one was open for 27% -> 29% of each run, Pallas kernels for 0% -> 0%
where the time goes in v3:
time: 352 us; the launch traced here: 345 us
  other arithmetic  178 us (51%)
  waiting for transfers between devices  67 us (19%)
  local copies, waits for them, and re-layouts  25.7 us (7%)
  starting transfers between devices  24.8 us (7%)
  matrix products  21.9 us (6%)
  between operations  15.2 us (4%)
  blocking collectives  12.7 us (4%)
    convert_element_type x1, other arithmetic, per_device(): image_grad = (cotangent.astype(jnp.float32) + slide_padded(pad_along(row_...  48.8 us
    reduce_sum x7, other arithmetic, tap_sums(): jnp.sum(cot_field * lax.slice_in_dim(padded, offset, offset + length, axi...  44.1 us
    convert_element_type x1, other arithmetic, per_device(): slide_padded(image_padded, row_taps, 2, columns).astype(jnp.bfloat16)  39 us
    psum x1, waiting for transfers between devices, per_device(): lax.psum((down_part * pixel_scale, up_part * pixel_scale), ('rows', 'rep'))  33 us
    convert_element_type x1, other arithmetic, per_device(): row_local = slide_padded(pad_along(grad_float, 1, half_reach), col_taps[:...  17.5 us
    convert_element_type x1, other arithmetic, per_device(): slide_padded(mix_padded, col_taps, 1, mix_columns.shape[1])  16.7 us
    all_to_all x1, waiting for transfers between devices, per_device(): lax.all_to_all(cotangent, 'rows', split_axis=2, concat_axis=1, tiled=True)  12.8 us
    all_to_all x1, blocking collectives, exchange_sum(): spread = lax.all_to_all(flat.reshape(count, piece), axes, 0, 0, tiled=True)  12.7 us
  transfers between devices with their start and end apart: 7, of which 5 were waited for; matrix products, arithmetic and copies ran while one was open for 29% of the time, Pallas kernels for 0%

profile of v3, /device:TPU:0, one launch (start us, length us, event | category | flops | bytes accessed | tf_op | source)
XLA Modules:
  0.0 345.4 jit_solution(125824079591626709)
XLA Ops:
  10.2 2.9 copy_convert_fusion
  13.1 39.0 %add_convert_fusion.2 = bf16[1,16,128,256]{3,1,0,2:T(8,128)(2,1)} fusion(f32[1,16,128,256]{3,1,0,2:T(8,128)S(1)} %get-tuple-element.154, f32[256]{0:T(256)S(1)} %bitcast.591, f32[256]{0:T(256)S(1)} %bitcast.593, f32[256]{0:T(256)S(1)} %bitcast.495, f32[256]{0:T(256)S(1)} %bitcast.497, f32[256]{0:T(256)S(1)} %bitcast.499, f32[256]{0:T(256)S(1)} %bitcast.501, ...), kind=kLoop, calls=%fused_computation.587 | loop fusion | flops 53477376 | bytes 3197952 | tf_op jit(solution)/shard_map/convert_element_type | solution.py:137
  52.1 4.2 %all-to-all-start.1 = ((bf16[1,16,128,256]{3,1,0,2:T(8,128)(2,1)}), bf16[1,16,128,256]{3,1,0,2:T(8,128)(2,1)}, u32[]{:S(2)}, u32[]{:S(2)}) async-start(bf16[1,16,128,256]{3,1,0,2:T(8,128)(2,1)} %add_convert_fusion.2), calls=%async_computation.1 | async-start | bytes 2097152 | tf_op jit(solution)/shard_map/all_to_all | solution.py:139
  56.3 2.8 copy.164
  59.1 12.4 %all-to-all-done.1 = bf16[1,16,128,256]{3,1,0,2:T(8,128)(2,1)} async-done(((bf16[1,16,128,256]{3,1,0,2:T(8,128)(2,1)}), bf16[1,16,128,256]{3,1,0,2:T(8,128)(2,1)}, u32[]{:S(2)}, u32[]{:S(2)}) %all-to-all-start.1) | async-done | bytes 1048608 | tf_op jit(solution)/shard_map/all_to_all | solution.py:139
  71.5 4.3 %all-to-all-start.3 = ((bf16[1,16,128,256]{3,1,0,2:T(8,128)(2,1)}), bf16[1,16,128,256]{3,1,0,2:T(8,128)(2,1)}, u32[]{:S(2)}, u32[]{:S(2)}) async-start(bf16[1,16,128,256]{3,1,0,2:T(8,128)(2,1)} %copy.164), calls=%async_computation.3 | async-start | bytes 2097152 | tf_op jit(solution)/shard_map/all_to_all | solution.py:135
  77.5 12.8 %all-to-all-done.3 = bf16[1,16,128,256]{3,1,0,2:T(8,128)(2,1)} async-done(((bf16[1,16,128,256]{3,1,0,2:T(8,128)(2,1)}), bf16[1,16,128,256]{3,1,0,2:T(8,128)(2,1)}, u32[]{:S(2)}, u32[]{:S(2)}) %all-to-all-start.3) | async-done | bytes 1048608 | tf_op jit(solution)/shard_map/all_to_all | solution.py:135
  90.3 4.4 %all-to-all-start = ((bf16[1,16,128,256]{3,1,0,2:T(8,128)(2,1)}), bf16[1,16,128,256]{3,1,0,2:T(8,128)(2,1)}, u32[]{:S(2)}, u32[]{:S(2)}) async-start(bf16[1,16,128,256]{3,1,0,2:T(8,128)(2,1)} %get-tuple-element.155), calls=%async_computation | async-start | bytes 2097152 | tf_op jit(solution)/shard_map/all_to_all | solution.py:134
  94.7 16.7 %add_convert_fusion.1 = bf16[1,64,32,256]{3,2,0,1:T(8,128)(2,1)S(1)} fusion(f32[1,64,32,256]{3,2,0,1:T(8,128)S(1)} %bitcast.375, f32[256]{0:T(256)S(1)} %bitcast.489, f32[256]{0:T(256)S(1)} %bitcast.491, f32[256]{0:T(256)S(1)} %bitcast.393, f32[256]{0:T(256)S(1)} %bitcast.395, f32[256]{0:T(256)S(1)} %bitcast.397, f32[256]{0:T(256)S(1)} %bitcast.399, ...), kind=kLoop, calls=%fused_computation.586 | loop fusion | flops 53477376 | bytes 3197952 | tf_op jit(solution)/shard_map/convert_element_type | solution.py:141
  111.4 3.3 copy.166
  117.0 2.9 copy.159
  121.9 3.7 %multiply_convert_fusion = (bf16[2048,1024]{1,0:T(8,128)(2,1)S(1)}, f32[2048,1024]{1,0:T(8,128)S(1)}) fusion(f32[1024]{0:T(1024)S(1)} %copy-done.24, bf16[2048,256]{1,0:T(8,128)(2,1)S(1)} %add_convert_fusion, bf16[256,1024]{1,0:T(8,128)(2,1)S(1)} %copy-done), kind=kOutput, calls=%fused_computation.260 | convolution fusion | flops 1094713344 | bytes 14159872 | tf_op jit(solution)/shard_map/dot_general | solution.py:75
  125.7 2.5 fusion.263
  128.3 6.4 %fusion.280 = (f32[1024]{0:T(1024)S(1)}, bf16[2048,1024]{1,0:T(8,128)(2,1)S(1)}) fusion(f32[2048,1024]{1,0:T(8,128)S(1)} %get-tuple-element.265, f32[1024]{0:T(1024)S(1)} %copy-done.24, bf16[2048,256]{1,0:T(8,128)(2,1)S(1)} %get-tuple-element.152, bf16[1024,256]{1,0:T(8,128)(2,1)S(1)} %copy-done.18), kind=kOutput, calls=%fused_computation.614 | convolution fusion | flops 1117780992 | bytes 14163968 | tf_op jit(solution)/shard_map/dot_general | solution.py:82
  138.0 10.4 %multiply_reduce_fusion.3 = (f32[256]{0:T(256)S(1)}, f32[256]{0:T(256)S(1)}, f32[256]{0:T(256)S(1)}, f32[256]{0:T(256)S(1)}, f32[256]{0:T(256)S(1)}, /*index=5*/...) fusion(f32[1,64,32,256]{3,2,0,1:T(8,128)S(1)} %bitcast.376, ...), kind=kLoop, calls=%fused_computation.529 | loop fusion | flops 19394048 | bytes 3164160 | tf_op jit(solution)/shard_map/reduce_sum | solution.py:49
  148.3 11.3 %multiply_reduce_fusion.2 = (f32[256]{0:T(256)S(1)}, f32[256]{0:T(256)S(1)}, f32[256]{0:T(256)S(1)}, f32[256]{0:T(256)S(1)}, f32[256]{0:T(256)S(1)}, /*index=5*/...) fusion(f32[1,64,32,256]{3,2,0,1:T(8,128)S(1)} %bitcast.377, ...), kind=kLoop, calls=%fused_computation.528 | loop fusion | flops 19394048 | bytes 3164160 | tf_op jit(solution)/shard_map/reduce_sum | solution.py:49
  159.9 17.5 %fusion.254 = bf16[1,64,32,256]{3,2,0,1:T(8,128)(2,1)} fusion(f32[1,64,32,256]{3,2,0,1:T(8,128)S(1)} %convert.19, f32[256]{0:T(256)S(1)} %bitcast.490, f32[256]{0:T(256)S(1)} %bitcast.492, f32[256]{0:T(256)S(1)} %bitcast.394, f32[256]{0:T(256)S(1)} %bitcast.396, f32[256]{0:T(256)S(1)} %bitcast.398, f32[256]{0:T(256)S(1)} %bitcast.400, f32[256]{0:T(256)S(1)} %bitcast.402, ...), kind=kLoop, calls=%fused_computation.510 | loop fusion | flops 53477376 | bytes 3197952 | tf_op jit(solution)/shard_map/convert_element_type | solution.py:164
  177.4 4.5 %all-to-all-start.4 = ((bf16[1,64,32,256]{3,2,0,1:T(8,128)(2,1)}), bf16[1,64,32,256]{3,2,0,1:T(8,128)(2,1)}, u32[]{:S(2)}, u32[]{:S(2)}) async-start(bf16[1,64,32,256]{3,2,0,1:T(8,128)(2,1)} %fusion.254), calls=%async_computation.4 | async-start | bytes 2097152 | tf_op jit(solution)/shard_map/all_to_all | solution.py:165
  181.9 8.5 %multiply_reduce_fusion.4 = (f32[256]{0:T(256)S(1)}, f32[256]{0:T(256)S(1)}, f32[256]{0:T(256)S(1)}, f32[256]{0:T(256)S(1)}, f32[256]{0:T(256)S(1)}, /*index=5*/...) fusion(f32[1,64,32,256]{3,2,0,1:T(8,128)S(1)} %bitcast.378, ...), kind=kLoop, calls=%fused_computation.530 | loop fusion | flops 15200768 | bytes 3160064 | tf_op jit(solution)/shard_map/reduce_sum | solution.py:49
  192.6 3.7 %all-to-all-done.4 = bf16[1,64,32,256]{3,2,0,1:T(8,128)(2,1)} async-done(((bf16[1,64,32,256]{3,2,0,1:T(8,128)(2,1)}), bf16[1,64,32,256]{3,2,0,1:T(8,128)(2,1)}, u32[]{:S(2)}, u32[]{:S(2)}) %all-to-all-start.4) | async-done | bytes 1048608 | tf_op jit(solution)/shard_map/all_to_all | solution.py:165
  198.3 4.1 %fusion.156 = (f32[256]{0:T(256)S(1)}, f32[256]{0:T(256)S(1)}, f32[256]{0:T(256)S(1)}, f32[256]{0:T(256)S(1)}, f32[256]{0:T(256)S(1)}, /*index=5*/f32[256]{0:T(2...) fusion(bf16[1,16,128,256]{3,1,0,2:T(8,128)(2,1)S(1)} %bitcast.3, ...), kind=kLoop, calls=%fused_computation.412 | loop fusion | flops 16773376 | bytes 4209664 | tf_op jit(solution)/shard_map/reduce_sum | solution.py:49
  202.4 4.9 %fusion.157 = (f32[256]{0:T(256)S(1)}, f32[256]{0:T(256)S(1)}, f32[256]{0:T(256)S(1)}, f32[256]{0:T(256)S(1)}, f32[256]{0:T(256)S(1)}, /*index=5*/f32[256]{0:T(2...) fusion(bf16[1,16,128,256]{3,1,0,2:T(8,128)(2,1)S(1)} %bitcast.3, ...), kind=kLoop, calls=%fused_computation.413 | loop fusion | flops 19394048 | bytes 3164160 | tf_op jit(solution)/shard_map/reduce_sum | solution.py:49
  207.4 4.5 %fusion.158 = (f32[256]{0:T(256)S(1)}, f32[256]{0:T(256)S(1)}, f32[256]{0:T(256)S(1)}, f32[256]{0:T(256)S(1)}, f32[256]{0:T(256)S(1)}, /*index=5*/f32[256]{0:T(2...) fusion(bf16[1,16,128,256]{3,1,0,2:T(8,128)(2,1)S(1)} %bitcast.3, ...), kind=kLoop, calls=%fused_computation.414 | loop fusion | flops 19394048 | bytes 3164160 | tf_op jit(solution)/shard_map/reduce_sum | solution.py:49
  212.2 12.7 %all_to_all.78 = f32[16,1,1792]{2,1,0:T(1,128)S(1)} all-to-all(f32[16,1,1792]{2,1,0:T(1,128)S(1)} %bitcast.390), channel_id=1, replica_groups=mesh['groups'=2,'rows'=4,'rep'=4] {'rows','rep'}, dimensions={0} | all-to-all | bytes 229376 | tf_op jit(solution)/shard_map/all_to_all | solution.py:206
  224.9 3.5 %all-to-all-start.2 = ((bf16[1,64,32,256]{3,2,0,1:T(8,128)(2,1)}), bf16[1,64,32,256]{3,2,0,1:T(8,128)(2,1)S(1)}, u32[]{:S(2)}, u32[]{:S(2)}) async-start(bf16[1,64,32,256]{3,2,0,1:T(8,128)(2,1)} %bitcast.385), calls=%async_computation.2 | async-start | bytes 2097152 | tf_op jit(solution)/shard_map/all_to_all | solution.py:156
  228.5 5.0 %fusion.269 = f32[256,1024]{1,0:T(8,128)} fusion(bf16[2048,256]{1,0:T(8,128)(2,1)} %copy-done.16, bf16[2048,1024]{1,0:T(8,128)(2,1)} %copy-done.25), kind=kOutput, calls=%fused_computation.589 | convolution fusion | flops 1074003968 | bytes 6291456 | tf_op jit(solution)/shard_map/dot_general | solution.py:106
  233.5 2.3 convolution_multiply_fusion
  238.8 5.1 %all-to-all-done.2 = bf16[1,64,32,256]{3,2,0,1:T(8,128)(2,1)S(1)} async-done(((bf16[1,64,32,256]{3,2,0,1:T(8,128)(2,1)}), bf16[1,64,32,256]{3,2,0,1:T(8,128)(2,1)S(1)}, u32[]{:S(2)}, u32[]{:S(2)}) %all-to-all-start.2) | async-done | bytes 1048608 | tf_op jit(solution)/shard_map/all_to_all | solution.py:156
  244.6 3.8 %all-to-all-start.6 = ((f32[16,1,1792]{2,1,0:T(1,128)}), f32[16,1,1792]{2,1,0:T(1,128)S(1)}, u32[]{:S(2)}, u32[]{:S(2)}) async-start(f32[16,1,1792]{2,1,0:T(1,128)} %broadcast_in_dim.2), calls=%async_computation.6 | async-start | bytes 229376 | tf_op jit(solution)/shard_map/all_to_all | solution.py:208
  248.4 48.8 %fusion.102 = bf16[1,16,128,256]{3,1,0,2:T(8,128)(2,1)S(1)} fusion(f32[1,16,128,256]{3,1,0,2:T(8,128)} %convert_element_type.169, bf16[1,16,128,256]{3,1,0,2:T(8,128)(2,1)S(1)} %bitcast.384, f32[256]{0:T(256)S(1)} %bitcast.592, f32[256]{0:T(256)S(1)} %bitcast.594, f32[256]{0:T(256)S(1)} %bitcast.496, f32[256]{0:T(256)S(1)} %bitcast.498, ...), kind=kLoop, calls=%fused_computation.358 | loop fusion | flops 55050240 | bytes 5295104 | tf_op jit(solution)/shard_map/convert_element_type | solution.py:172
  301.7 33.0 %all-reduce.8.cloned.1.call-done = (f32[1024,256]{1,0:T(8,128)}, f32[256,1024]{1,0:T(8,128)}) async-done(((f32[1024,256]{1,0:T(8,128)}, f32[256,1024]{1,0:T(8,128)}), (f32[1024,256]{1,0:T(8,128)}, f32[256,1024]{1,0:T(8,128)})) %all-reduce.8.cloned.1.call-update) | async-done | bytes 2097168 | tf_op jit(solution)/shard_map/psum | solution.py:173
  334.7 2.4 copy.236
  (103 shorter events, 25.9 us)
Async XLA Ops:
  7.2 114.6 %copy-start = (bf16[256,1024]{1,0:T(8,128)(2,1)S(1)}, bf16[256,1024]{1,0:T(8,128)(2,1)}, u32[]{:S(2)}) copy-start(bf16[256,1024]{1,0:T(8,128)(2,1)} %param.17) | copy-start | bytes 1572868
  13.1 39.0 %copy-start.1 = (f32[1,16,128,256]{3,1,0,2:T(8,128)}, f32[1,16,128,256]{3,1,0,2:T(8,128)S(1)}, u32[]{:S(2)}) copy-start(f32[1,16,128,256]{3,1,0,2:T(8,128)S(1)} %get-tuple-element.154) | copy-start | bytes 6291460
  52.1 19.4 %all-to-all-start.1 = ((bf16[1,16,128,256]{3,1,0,2:T(8,128)(2,1)}), bf16[1,16,128,256]{3,1,0,2:T(8,128)(2,1)}, u32[]{:S(2)}, u32[]{:S(2)}) async-start(bf16[1,16,128,256]{3,1,0,2:T(8,128)(2,1)} %add_convert_fusion.2), calls=%async_computation.1 | async-start | bytes 2097152 | tf_op jit(solution)/shard_map/all_to_all | solution.py:139
  56.3 19.5 %copy-start.19 = (f32[51,256]{1,0:T(8,128)S(1)}, f32[51,256]{1,0:T(8,128)}, u32[]{:S(2)}) copy-start(f32[51,256]{1,0:T(8,128)} %param.14) | copy-start | bytes 156676
  71.5 18.8 %all-to-all-start.3 = ((bf16[1,16,128,256]{3,1,0,2:T(8,128)(2,1)}), bf16[1,16,128,256]{3,1,0,2:T(8,128)(2,1)}, u32[]{:S(2)}, u32[]{:S(2)}) async-start(bf16[1,16,128,256]{3,1,0,2:T(8,128)(2,1)} %copy.164), calls=%async_computation.3 | async-start | bytes 2097152 | tf_op jit(solution)/shard_map/all_to_all | solution.py:135
  90.3 26.7 %all-to-all-start = ((bf16[1,16,128,256]{3,1,0,2:T(8,128)(2,1)}), bf16[1,16,128,256]{3,1,0,2:T(8,128)(2,1)}, u32[]{:S(2)}, u32[]{:S(2)}) async-start(bf16[1,16,128,256]{3,1,0,2:T(8,128)(2,1)} %get-tuple-element.155), calls=%async_computation | async-start | bytes 2097152 | tf_op jit(solution)/shard_map/all_to_all | solution.py:134
  111.4 3.7 %copy-start.7 = (bf16[1,64,32,256]{3,2,0,1:T(8,128)(2,1)}, bf16[1,64,32,256]{3,2,0,1:T(8,128)(2,1)S(1)}, u32[]{:S(2)}) copy-start(bf16[1,64,32,256]{3,2,0,1:T(8,128)(2,1)S(1)} %add_convert_fusion.1) | copy-start | bytes 3145732
  115.1 4.9 %copy-start.21 = (f32[256]{0:T(256)S(1)}, f32[256]{0:T(256)}, u32[]{:S(2)}) copy-start(f32[256]{0:T(256)} %param.15) | copy-start | bytes 3076
  115.1 4.9 %copy-start.23 = (f32[256]{0:T(256)S(1)}, f32[256]{0:T(256)}, u32[]{:S(2)}) copy-start(f32[256]{0:T(256)} %param.16) | copy-start | bytes 3076
  117.0 4.8 %copy-start.24 = (f32[1024]{0:T(1024)S(1)}, f32[1024]{0:T(1024)}, u32[]{:S(2)}) copy-start(f32[1024]{0:T(1024)} %param.18) | copy-start | bytes 12292
  121.8 3.8 %copy-start.16 = (bf16[2048,256]{1,0:T(8,128)(2,1)}, bf16[2048,256]{1,0:T(8,128)(2,1)S(1)}, u32[]{:S(2)}) copy-start(bf16[2048,256]{1,0:T(8,128)(2,1)S(1)} %add_convert_fusion) | copy-start | bytes 3145732
  121.9 3.8 %copy-start.9 = (f32[1,16,4,32,256]{4,3,1,2,0:T(8,128)S(1)}, f32[1,16,4,32,256]{4,3,1,2,0:T(8,128)}, u32[]{:S(2)}) copy-start(f32[1,16,4,32,256]{4,3,1,2,0:T(8,128)} %copy.166) | copy-start | bytes 6291460
  121.9 3.8 %copy-start.10 = (f32[1,16,4,32,256]{4,3,1,2,0:T(8,128)S(1)}, f32[1,16,4,32,256]{4,3,1,2,0:T(8,128)}, u32[]{:S(2)}) copy-start(f32[1,16,4,32,256]{4,3,1,2,0:T(8,128)} %copy.159) | copy-start | bytes 6291460
  121.9 3.8 %copy-start.18 = (bf16[1024,256]{1,0:T(8,128)(2,1)S(1)}, bf16[1024,256]{1,0:T(8,128)(2,1)}, u32[]{:S(2)}) copy-start(bf16[1024,256]{1,0:T(8,128)(2,1)} %param.19) | copy-start | bytes 1572868
  121.9 3.8 %copy-start.20 = (f32[256]{0:T(256)S(1)}, f32[256]{0:T(256)}, u32[]{:S(2)}) copy-start(f32[256]{0:T(256)} %param.21) | copy-start | bytes 3076
  121.9 3.8 %copy-start.22 = (f32[256]{0:T(256)S(1)}, f32[256]{0:T(256)}, u32[]{:S(2)}) copy-start(f32[256]{0:T(256)} %param.20) | copy-start | bytes 3076
  125.7 2.6 copy-start.11
  128.3 6.4 %copy-start.14 = (bf16[2048,256]{1,0:T(8,128)(2,1)}, bf16[2048,256]{1,0:T(8,128)(2,1)S(1)}, u32[]{:S(2)}) copy-start(bf16[2048,256]{1,0:T(8,128)(2,1)S(1)} %get-tuple-element.152) | copy-start | bytes 3145732
  128.3 6.4 %copy-start.8 = (bf16[1,64,32,256]{3,2,0,1:T(8,128)(2,1)S(1)}, bf16[1,64,32,256]{3,2,0,1:T(8,128)(2,1)}, u32[]{:S(2)}) copy-start(bf16[1,64,32,256]{3,2,0,1:T(8,128)(2,1)} %copy-done.7) | copy-start | bytes 3145732
  134.7 2.0 copy-start.25
  138.0 21.7 %copy-start.3 = (bf16[2048,256]{1,0:T(8,128)(2,1)}, bf16[2048,256]{1,0:T(8,128)(2,1)S(1)}, u32[]{:S(2)}) copy-start(bf16[2048,256]{1,0:T(8,128)(2,1)S(1)} %multiply_convert_fusion.1) | copy-start | bytes 3145732
  177.4 19.0 %all-to-all-start.4 = ((bf16[1,64,32,256]{3,2,0,1:T(8,128)(2,1)}), bf16[1,64,32,256]{3,2,0,1:T(8,128)(2,1)}, u32[]{:S(2)}, u32[]{:S(2)}) async-start(bf16[1,64,32,256]{3,2,0,1:T(8,128)(2,1)} %fusion.254), calls=%async_computation.4 | async-start | bytes 2097152 | tf_op jit(solution)/shard_map/all_to_all | solution.py:165
  181.9 8.5 %copy-start.4 = (bf16[2048,256]{1,0:T(8,128)(2,1)S(1)}, bf16[2048,256]{1,0:T(8,128)(2,1)}, u32[]{:S(2)}) copy-start(bf16[2048,256]{1,0:T(8,128)(2,1)} %copy-done.3) | copy-start | bytes 3145732
  190.8 7.5 %copy-start.2 = (f32[1,16,128,256]{3,1,0,2:T(8,128)S(1)}, f32[1,16,128,256]{3,1,0,2:T(8,128)}, u32[]{:S(2)}) copy-start(f32[1,16,128,256]{3,1,0,2:T(8,128)} %copy-done.1) | copy-start | bytes 6291460
  196.4 1.9 copy-start.13
  198.3 9.1 %copy-start.5 = (bf16[1,4,16,32,256]{4,2,3,1,0:T(8,128)(2,1)}, bf16[1,4,16,32,256]{4,2,3,1,0:T(8,128)(2,1)S(1)}, u32[]{:S(2)}) copy-start(bf16[1,4,16,32,256]{4,2,3,1,0:T(8,128)(2,1)S(1)} %copy.169) | copy-start | bytes 3145732
  224.9 18.9 %all-to-all-start.2 = ((bf16[1,64,32,256]{3,2,0,1:T(8,128)(2,1)}), bf16[1,64,32,256]{3,2,0,1:T(8,128)(2,1)S(1)}, u32[]{:S(2)}, u32[]{:S(2)}) async-start(bf16[1,64,32,256]{3,2,0,1:T(8,128)(2,1)} %bitcast.385), calls=%async_computation.2 | async-start | bytes 2097152 | tf_op jit(solution)/shard_map/all_to_all | solution.py:156
  228.5 5.1 %copy-start.15 = (bf16[2048,256]{1,0:T(8,128)(2,1)S(1)}, bf16[2048,256]{1,0:T(8,128)(2,1)}, u32[]{:S(2)}) copy-start(bf16[2048,256]{1,0:T(8,128)(2,1)} %copy-done.14) | copy-start | bytes 3145732
  228.5 106.2 %all-reduce.8.cloned.1.call-start = ((), (), s32[]{:S(2)}) async-start(), calls=%async_computation.7 | async-start | bytes 4194304 | tf_op jit(solution)/shard_map/psum | solution.py:173
  228.5 5.0 %copy-start.12 = (bf16[2048,1024]{1,0:T(8,128)(2,1)S(1)}, bf16[2048,1024]{1,0:T(8,128)(2,1)}, u32[]{:S(2)}) copy-start(bf16[2048,1024]{1,0:T(8,128)(2,1)} %copy-done.11) | copy-start | bytes 12582916
  244.6 55.0 %all-to-all-start.6 = ((f32[16,1,1792]{2,1,0:T(1,128)}), f32[16,1,1792]{2,1,0:T(1,128)S(1)}, u32[]{:S(2)}, u32[]{:S(2)}) async-start(f32[16,1,1792]{2,1,0:T(1,128)} %broadcast_in_dim.2), calls=%async_computation.6 | async-start | bytes 229376 | tf_op jit(solution)/shard_map/all_to_all | solution.py:208
  334.7 2.4 copy-start.17
  (1 other events, 1.2 us)
Sparse Core Ops, SparseCore 0:
  236.0 98.6 all-reduce.7

commit v4 on v2

--- a/solution.py
+++ b/solution.py
@@ -37,7 +37,7 @@
     for offset in range(taps_table.shape[0]):
         result = result + taps_table[offset] * lax.slice_in_dim(
             padded, offset, offset + length, axis=direction
-        )
+        ).astype(jnp.float32)
     return result
 
 
@@ -47,7 +47,10 @@
     return jnp.stack(
         [
             jnp.sum(
-                cot_field * lax.slice_in_dim(padded, offset, offset + length, axis=direction),
+                cot_field.astype(jnp.float32)
+                * lax.slice_in_dim(padded, offset, offset + length, axis=direction).astype(
+                    jnp.float32
+                ),
                 axis=lead_axes,
             )
             for offset in range(taps_count)
@@ -131,11 +134,11 @@
     pixel_scale = 1.0 / math.sqrt(
         tiles_here * lax.axis_size("rep") * band_rows * lax.axis_size("rows") * columns
     )
-    image_padded = pad_along(images.astype(jnp.float32), 2, half_reach)
+    image_padded = pad_along(images, 2, half_reach)
     row_mix = slide_padded(image_padded, row_taps, 2, columns).astype(jnp.bfloat16)
     row_mix = lax.optimization_barrier(row_mix)
     mix_columns = lax.all_to_all(row_mix, "rows", split_axis=2, concat_axis=1, tiled=True)
-    mix_padded = pad_along(mix_columns.astype(jnp.float32), 1, half_reach)
+    mix_padded = pad_along(mix_columns, 1, half_reach)
     col_local = slide_padded(mix_padded, col_taps, 1, mix_columns.shape[1]).astype(jnp.bfloat16)
     col_mix = lax.all_to_all(col_local, "rows", split_axis=1, concat_axis=2, tiled=True)
     col_mix = lax.optimization_barrier(col_mix)
@@ -156,18 +159,16 @@
     grad_rows = lax.optimization_barrier(grad_rows)
     col_grad = grad_rows.reshape(images.shape)
     grad_columns = lax.all_to_all(col_grad, "rows", split_axis=2, concat_axis=1, tiled=True)
-    grad_float = grad_columns.astype(jnp.float32)
-    col_part = tap_sums(grad_float, mix_padded, taps_count, 1)
+    col_part = tap_sums(grad_columns, mix_padded, taps_count, 1)
     row_local = slide_padded(
-        pad_along(grad_float, 1, half_reach), col_taps[::-1], 1, grad_columns.shape[1]
+        pad_along(grad_columns, 1, half_reach), col_taps[::-1], 1, grad_columns.shape[1]
     ).astype(jnp.bfloat16)
     row_grad = lax.all_to_all(row_local, "rows", split_axis=1, concat_axis=2, tiled=True)
     row_grad = lax.optimization_barrier(row_grad)
-    row_float = row_grad.astype(jnp.float32)
-    row_part = tap_sums(row_float, image_padded, taps_count, 2)
+    row_part = tap_sums(row_grad, image_padded, taps_count, 2)
     image_grad = (
         cotangent.astype(jnp.float32)
-        + slide_padded(pad_along(row_float, 2, half_reach), row_taps[::-1], 2, columns)
+        + slide_padded(pad_along(row_grad, 2, half_reach), row_taps[::-1], 2, columns)
     ).astype(jnp.bfloat16)
     down_total, up_total = lax.psum((down_part * pixel_scale, up_part * pixel_scale), ("rows", "rep"))
     small = (row_part, col_part, scale_part, down_bias_part, up_bias_part, gain_part, shift_part)
@@ -199,12 +200,12 @@
     count = 1
     for axis in axes:
         count *= lax.axis_size(axis)
-    flat = jnp.concatenate([part.reshape(-1) for part in parts])
-    piece = -(-flat.shape[0] // (count * 128)) * 128
-    flat = jnp.pad(flat, (0, piece * count - flat.shape[0]))
-    spread = lax.all_to_all(flat.reshape(count, piece), axes, 0, 0, tiled=True)
+    stacked = jnp.concatenate([part.reshape(-1, 128) for part in parts])
+    piece = -(-stacked.shape[0] // count)
+    stacked = jnp.pad(stacked, ((0, piece * count - stacked.shape[0]), (0, 0)))
+    spread = lax.all_to_all(stacked.reshape(count, piece, 128), axes, 0, 0, tiled=True)
     mine = jnp.sum(spread, axis=0, keepdims=True)
-    whole = lax.all_to_all(jnp.broadcast_to(mine, (count, piece)), axes, 0, 0, tiled=True)
+    whole = lax.all_to_all(jnp.broadcast_to(mine, (count, piece, 128)), axes, 0, 0, tiled=True)
     return split_like(whole.reshape(-1), parts)
 
 

time: 315 us -> 336 us (1.067)
  waiting for transfers between devices: 58.4 us -> 128 us
  other arithmetic: 154 us -> 125 us
  blocking collectives: 16.9 us -> 0 us
    psum x1, waiting for transfers between devices: 35.3 us -> 76.6 us  [per_device(): lax.psum((down_part * pixel_scale, up_part * pixel_scale), ('rows', 'rep'))]
    convert_element_type x1, other arithmetic: 54.5 us -> 16.5 us  [per_device(): image_grad = (cotangent.astype(jnp.float32) + slide_padded(pad_along(row_...]
    convert_element_type x1, other arithmetic: 16.8 us -> 41.6 us  [per_device(): slide_padded(image_padded, row_taps, 2, columns).astype(jnp.bfloat16)]
    all_to_all x1 -> x0, blocking collectives: 16.9 us -> none  [per_device(): lax.all_to_all(col_local, 'rows', split_axis=1, concat_axis=2, tiled=True)]
    all_to_all x2 -> x3, waiting for transfers between devices: 0.01 us -> 16.5 us  [the longest x1 14 us: per_device(): lax.all_to_all(col_local, 'rows', split_axis=1, concat_axis=2, tiled=True)]
    all_to_all x1, waiting for transfers between devices: 0.01 us -> 10.8 us  [per_device(): lax.all_to_all(row_local, 'rows', split_axis=1, concat_axis=2, tiled=True)]
    reduce_sum x7, other arithmetic: 37.4 us -> 26.7 us  [tap_sums(): jnp.sum(cot_field.astype(jnp.float32) * lax.slice_in_dim(padded, offset,...]
    convert_element_type x5 -> x1, other arithmetic: 23.5 us -> 18.6 us  [per_device(): row_local = slide_padded(pad_along(grad_columns, 1, half_reach), col_taps...]
  transfers between devices with their start and end apart: 6 -> 7, of which waited for: 3 -> 6; matrix products, arithmetic and copies ran while one was open for 27% -> 10% of each run, Pallas kernels for 0% -> 0%
where the time goes in v4:
time: 336 us
  waiting for transfers between devices  128 us (38%)
  other arithmetic  125 us (37%)
  starting transfers between devices  26.2 us (8%)
  matrix products  24.1 us (7%)
  local copies, waits for them, and re-layouts  17.9 us (5%)
  between operations  14.5 us (4%)
    psum x1, waiting for transfers between devices, per_device(): lax.psum((down_part * pixel_scale, up_part * pixel_scale), ('rows', 'rep'))  76.6 us
    convert_element_type x1, other arithmetic, per_device(): slide_padded(image_padded, row_taps, 2, columns).astype(jnp.bfloat16)  41.6 us
    reduce_sum x7, other arithmetic, tap_sums(): jnp.sum(cot_field.astype(jnp.float32) * lax.slice_in_dim(padded, offset,...  26.7 us
    convert_element_type x1, other arithmetic, per_device(): slide_padded(mix_padded, col_taps, 1, mix_columns.shape[1])  18.6 us
    convert_element_type x1, other arithmetic, per_device(): row_local = slide_padded(pad_along(grad_columns, 1, half_reach), col_taps...  18.6 us
    convert_element_type x1, other arithmetic, per_device(): image_grad = (cotangent.astype(jnp.float32) + slide_padded(pad_along(row_...  16.5 us
    all_to_all x1, waiting for transfers between devices, per_device(): lax.all_to_all(row_mix, 'rows', split_axis=2, concat_axis=1, tiled=True)  14.4 us
    all_to_all x1, waiting for transfers between devices, per_device(): lax.all_to_all(col_local, 'rows', split_axis=1, concat_axis=2, tiled=True)  14 us
  transfers between devices with their start and end apart: 7, of which 6 were waited for; matrix products, arithmetic and copies ran while one was open for 10% of the time, Pallas kernels for 0%

profile of v4, /device:TPU:0, one launch (start us, length us, event | category | flops | bytes accessed | tf_op | source)
XLA Modules:
  0.0 335.6 jit_solution(11380142096445996244)
XLA Ops:
  10.2 41.6 %fusion.268 = bf16[1,16,128,256]{3,2,1,0:T(8,128)(2,1)S(1)} fusion(bf16[1,16,128,256]{3,2,1,0:T(8,128)(2,1)} %param.11, f32[256]{0:T(256)S(1)} %bitcast.395, f32[256]{0:T(256)S(1)} %bitcast.397, f32[256]{0:T(256)S(1)} %bitcast.337, f32[256]{0:T(256)S(1)} %bitcast.339, f32[256]{0:T(256)S(1)} %bitcast.341, f32[256]{0:T(256)S(1)} %bitcast.343, ...), kind=kLoop, calls=%fused_computation.688 | loop fusion | flops 80216064 | bytes 2149376 | tf_op jit(solution)/shard_map/convert_element_type | solution.py:138
  51.8 1.6 copy.26
  53.4 4.2 %all-to-all-start = ((bf16[1,16,128,256]{3,1,0,2:T(8,128)(2,1)}), bf16[1,16,128,256]{3,1,0,2:T(8,128)(2,1)S(1)}, u32[]{:S(2)}, u32[]{:S(2)}) async-start(bf16[1,16,128,256]{3,1,0,2:T(8,128)(2,1)} %copy.26), calls=%async_computation | async-start | bytes 2097152 | tf_op jit(solution)/shard_map/all_to_all | solution.py:140
  57.7 14.4 %all-to-all-done = bf16[1,16,128,256]{3,1,0,2:T(8,128)(2,1)S(1)} async-done(((bf16[1,16,128,256]{3,1,0,2:T(8,128)(2,1)}), bf16[1,16,128,256]{3,1,0,2:T(8,128)(2,1)S(1)}, u32[]{:S(2)}, u32[]{:S(2)}) %all-to-all-start) | async-done | bytes 1048608 | tf_op jit(solution)/shard_map/all_to_all | solution.py:140
  73.5 18.6 %fusion.272 = bf16[1,64,32,256]{3,2,0,1:T(8,128)(2,1)} fusion(f32[256]{0:T(256)S(1)} %bitcast.497, f32[256]{0:T(256)S(1)} %bitcast.499, f32[256]{0:T(256)S(1)} %bitcast.401, f32[256]{0:T(256)S(1)} %bitcast.403, f32[256]{0:T(256)S(1)} %bitcast.405, f32[256]{0:T(256)S(1)} %bitcast.407, f32[256]{0:T(256)S(1)} %bitcast.409, f32[256]{0:T(256)S(1)} %bitcast.411, ...), kind=kLoop, calls=%fused_computation.693 | loop fusion | flops 80216064 | bytes 2149376 | tf_op jit(solution)/shard_map/convert_element_type | solution.py:142
  92.1 4.4 %all-to-all-start.1 = ((bf16[1,64,32,256]{3,2,0,1:T(8,128)(2,1)}), bf16[1,64,32,256]{3,2,0,1:T(8,128)(2,1)}, u32[]{:S(2)}, u32[]{:S(2)}) async-start(bf16[1,64,32,256]{3,2,0,1:T(8,128)(2,1)} %fusion.272), calls=%async_computation.1 | async-start | bytes 2097152 | tf_op jit(solution)/shard_map/all_to_all | solution.py:143
  96.8 14.0 %all-to-all-done.1 = bf16[1,64,32,256]{3,2,0,1:T(8,128)(2,1)} async-done(((bf16[1,64,32,256]{3,2,0,1:T(8,128)(2,1)}), bf16[1,64,32,256]{3,2,0,1:T(8,128)(2,1)}, u32[]{:S(2)}, u32[]{:S(2)}) %all-to-all-start.1) | async-done | bytes 1048608 | tf_op jit(solution)/shard_map/all_to_all | solution.py:143
  110.8 1.3 copy.30
  114.0 3.7 %multiply_convert_fusion = (bf16[2048,1024]{1,0:T(8,128)(2,1)S(1)}, f32[2048,1024]{1,0:T(8,128)S(1)}) fusion(f32[1024]{0:T(1024)S(1)} %copy-done.14, bf16[2048,256]{1,0:T(8,128)(2,1)S(1)} %add_convert_fusion.1, bf16[256,1024]{1,0:T(8,128)(2,1)S(1)} %copy-done), kind=kOutput, calls=%fused_computation.211 | convolution fusion | flops 1094713344 | bytes 14159872 | tf_op jit(solution)/shard_map/dot_general | solution.py:78
  117.8 2.5 fusion.260
  120.3 6.4 %fusion.283 = (f32[1024]{0:T(1024)S(1)}, bf16[2048,1024]{1,0:T(8,128)(2,1)S(1)}) fusion(f32[2048,1024]{1,0:T(8,128)S(1)} %get-tuple-element.232, f32[1024]{0:T(1024)S(1)} %copy-done.14, bf16[2048,256]{1,0:T(8,128)(2,1)S(1)} %get-tuple-element.120, bf16[1024,256]{1,0:T(8,128)(2,1)S(1)} %copy-done.13), kind=kOutput, calls=%fused_computation.715 | convolution fusion | flops 1117780992 | bytes 14163968 | tf_op jit(solution)/shard_map/dot_general | solution.py:85
  126.8 1.8 multiply_reduce_fusion
  129.9 1.6 copy.31
  131.5 3.7 %all-to-all-start.2 = ((bf16[1,16,128,256]{3,1,0,2:T(8,128)(2,1)}), bf16[1,16,128,256]{3,1,0,2:T(8,128)(2,1)S(1)}, u32[]{:S(2)}, u32[]{:S(2)}) async-start(bf16[1,16,128,256]{3,1,0,2:T(8,128)(2,1)} %copy.31), calls=%async_computation.2 | async-start | bytes 2097152 | tf_op jit(solution)/shard_map/all_to_all | solution.py:161
  135.3 4.8 %convolution_multiply_fusion = f32[1024,256]{1,0:T(8,128)} fusion(bf16[2048,1024]{1,0:T(8,128)(2,1)} %copy-done.17, bf16[2048,256]{1,0:T(8,128)(2,1)} %copy-done.18), kind=kOutput, calls=%fused_computation.691 | convolution fusion | flops 1074003968 | bytes 6291456 | tf_op jit(solution)/shard_map/dot_general | solution.py:105
  140.1 9.3 %all-to-all-done.2 = bf16[1,16,128,256]{3,1,0,2:T(8,128)(2,1)S(1)} async-done(((bf16[1,16,128,256]{3,1,0,2:T(8,128)(2,1)}), bf16[1,16,128,256]{3,1,0,2:T(8,128)(2,1)S(1)}, u32[]{:S(2)}, u32[]{:S(2)}) %all-to-all-start.2) | async-done | bytes 1048608 | tf_op jit(solution)/shard_map/all_to_all | solution.py:161
  149.8 4.8 %fusion.179 = (f32[256]{0:T(256)S(1)}, f32[256]{0:T(256)S(1)}, f32[256]{0:T(256)S(1)}, f32[256]{0:T(256)S(1)}, f32[256]{0:T(256)S(1)}, /*index=5*/f32[256]{0:T(2...) fusion(bf16[1,64,32,256]{3,2,1,0:T(8,128)(2,1)S(1)} %bitcast.28, ...), kind=kLoop, calls=%fused_computation.586 | loop fusion | flops 28831232 | bytes 2115584 | tf_op jit(solution)/shard_map/reduce_sum | solution.py:49
  154.7 4.1 %fusion.180 = (f32[256]{0:T(256)S(1)}, f32[256]{0:T(256)S(1)}, f32[256]{0:T(256)S(1)}, f32[256]{0:T(256)S(1)}, f32[256]{0:T(256)S(1)}, /*index=5*/f32[256]{0:T(2...) fusion(bf16[1,64,32,256]{3,2,1,0:T(8,128)(2,1)S(1)} %bitcast.28, ...), kind=kLoop, calls=%fused_computation.587 | loop fusion | flops 28831232 | bytes 2115584 | tf_op jit(solution)/shard_map/reduce_sum | solution.py:49
  159.3 18.6 %fusion.273 = bf16[1,64,32,256]{3,2,0,1:T(8,128)(2,1)} fusion(bf16[1,64,32,256]{3,2,1,0:T(8,128)(2,1)S(1)} %bitcast.285, f32[256]{0:T(256)S(1)} %bitcast.400, f32[256]{0:T(256)S(1)} %bitcast.438, f32[256]{0:T(256)S(1)} %bitcast.476, f32[256]{0:T(256)S(1)} %bitcast.496, f32[256]{0:T(256)S(1)} %bitcast.494, f32[256]{0:T(256)S(1)} %bitcast.492, ...), kind=kLoop, calls=%fused_computation.694 | loop fusion | flops 80216064 | bytes 2149376 | tf_op jit(solution)/shard_map/convert_element_type | solution.py:165
  177.8 4.5 %all-to-all-start.3 = ((bf16[1,64,32,256]{3,2,0,1:T(8,128)(2,1)}), bf16[1,64,32,256]{3,2,0,1:T(8,128)(2,1)}, u32[]{:S(2)}, u32[]{:S(2)}) async-start(bf16[1,64,32,256]{3,2,0,1:T(8,128)(2,1)} %fusion.273), calls=%async_computation.3 | async-start | bytes 2097152 | tf_op jit(solution)/shard_map/all_to_all | solution.py:166
  182.3 3.3 fusion.178
  185.8 10.8 %all-to-all-done.3 = bf16[1,64,32,256]{3,2,0,1:T(8,128)(2,1)} async-done(((bf16[1,64,32,256]{3,2,0,1:T(8,128)(2,1)}), bf16[1,64,32,256]{3,2,0,1:T(8,128)(2,1)}, u32[]{:S(2)}, u32[]{:S(2)}) %all-to-all-start.3) | async-done | bytes 1048608 | tf_op jit(solution)/shard_map/all_to_all | solution.py:166
  197.9 4.8 %fusion.256 = (f32[256]{0:T(256)S(1)}, f32[256]{0:T(256)S(1)}, f32[256]{0:T(256)S(1)}, f32[256]{0:T(256)S(1)}, f32[256]{0:T(256)S(1)}, /*index=5*/f32[256]{0:T(2...) fusion(bf16[1,16,128,256]{3,2,1,0:T(8,128)(2,1)S(1)} %bitcast.2, ...), kind=kLoop, calls=%fused_computation.663 | loop fusion | flops 28831232 | bytes 2115584 | tf_op jit(solution)/shard_map/reduce_sum | solution.py:49
  202.7 5.1 %fusion.255 = (f32[256]{0:T(256)S(1)}, f32[256]{0:T(256)S(1)}, f32[256]{0:T(256)S(1)}, f32[256]{0:T(256)S(1)}, f32[256]{0:T(256)S(1)}, /*index=5*/f32[256]{0:T(2...) fusion(bf16[1,16,128,256]{3,2,1,0:T(8,128)(2,1)S(1)} %bitcast.2, ...), kind=kLoop, calls=%fused_computation.662 | loop fusion | flops 28831232 | bytes 2115584 | tf_op jit(solution)/shard_map/reduce_sum | solution.py:49
  207.8 4.2 %fusion.254 = (f32[256]{0:T(256)S(1)}, f32[256]{0:T(256)S(1)}, f32[256]{0:T(256)S(1)}, f32[256]{0:T(256)S(1)}, f32[256]{0:T(256)S(1)}, /*index=5*/f32[256]{0:T(2...) fusion(bf16[1,16,128,256]{3,2,1,0:T(8,128)(2,1)S(1)} %bitcast.2, ...), kind=kLoop, calls=%fused_computation.661 | loop fusion | flops 24113408 | bytes 2112512 | tf_op jit(solution)/shard_map/reduce_sum | solution.py:49
  213.1 5.7 %all-to-all-start.4 = ((f32[16,14,128]{2,1,0:T(8,128)}), f32[16,14,128]{2,1,0:T(8,128)S(1)}, u32[]{:S(2)}, u32[]{:S(2)}) async-start(f32[16,14,128]{2,1,0:T(8,128)} %reshape.784), calls=%async_computation.4 | async-start | bytes 262144 | tf_op jit(solution)/shard_map/all_to_all | solution.py:206
  218.9 4.8 %fusion.269 = f32[256,1024]{1,0:T(8,128)} fusion(bf16[2048,256]{1,0:T(8,128)(2,1)} %copy-done.7, bf16[2048,1024]{1,0:T(8,128)(2,1)} %copy-done.16), kind=kOutput, calls=%fused_computation.690 | convolution fusion | flops 1074003968 | bytes 6291456 | tf_op jit(solution)/shard_map/dot_general | solution.py:109
  223.7 2.5 all-to-all-done.4
  226.9 3.5 %all-to-all-start.5 = ((f32[16,14,128]{2,1,0:T(8,128)}), f32[16,14,128]{2,1,0:T(8,128)S(1)}, u32[]{:S(2)}, u32[]{:S(2)}) async-start(f32[16,14,128]{2,1,0:T(8,128)} %broadcast_in_dim.2), calls=%async_computation.5 | async-start | bytes 262144 | tf_op jit(solution)/shard_map/all_to_all | solution.py:208
  230.4 16.5 %fusion.257 = bf16[1,16,128,256]{3,2,1,0:T(8,128)(2,1)} fusion(bf16[1,16,128,256]{3,2,1,0:T(8,128)(2,1)S(1)} %copy-done.6, bf16[1,16,128,256]{3,2,1,0:T(8,128)(2,1)S(1)} %bitcast.278, f32[256]{0:T(256)S(1)} %bitcast.396, f32[256]{0:T(256)S(1)} %bitcast.398, f32[256]{0:T(256)S(1)} %bitcast.338, f32[256]{0:T(256)S(1)} %bitcast.340, f32[256]{0:T(256)S(1)} %bitcast.342, ...), kind=kLoop, calls=%fused_computation.668 | loop fusion | flops 81264640 | bytes 3197952 | tf_op jit(solution)/shard_map/convert_element_type | solution.py:172
  248.8 76.6 %all-reduce.8.cloned.1.call-done = (f32[1024,256]{1,0:T(8,128)}, f32[256,1024]{1,0:T(8,128)}) async-done(((f32[1024,256]{1,0:T(8,128)}, f32[256,1024]{1,0:T(8,128)}), (f32[1024,256]{1,0:T(8,128)}, f32[256,1024]{1,0:T(8,128)})) %all-reduce.8.cloned.1.call-update) | async-done | bytes 2097168 | tf_op jit(solution)/shard_map/psum | solution.py:173
  325.5 2.4 copy.38
  (81 shorter events, 14.9 us)
Async XLA Ops:
  7.2 106.8 %copy-start = (bf16[256,1024]{1,0:T(8,128)(2,1)S(1)}, bf16[256,1024]{1,0:T(8,128)(2,1)}, u32[]{:S(2)}) copy-start(bf16[256,1024]{1,0:T(8,128)(2,1)} %param.17) | copy-start | bytes 1572868
  51.8 5.8 %copy-start.9 = (f32[51,256]{1,0:T(8,128)S(1)}, f32[51,256]{1,0:T(8,128)}, u32[]{:S(2)}) copy-start(f32[51,256]{1,0:T(8,128)} %param.14) | copy-start | bytes 156676
  53.4 18.7 %all-to-all-start = ((bf16[1,16,128,256]{3,1,0,2:T(8,128)(2,1)}), bf16[1,16,128,256]{3,1,0,2:T(8,128)(2,1)S(1)}, u32[]{:S(2)}, u32[]{:S(2)}) async-start(bf16[1,16,128,256]{3,1,0,2:T(8,128)(2,1)} %copy.26), calls=%async_computation | async-start | bytes 2097152 | tf_op jit(solution)/shard_map/all_to_all | solution.py:140
  72.4 1.0 copy-start.3
  73.4 23.1 %copy-start.5 = (bf16[1,16,128,256]{3,2,1,0:T(8,128)(2,1)S(1)}, bf16[1,16,128,256]{3,2,1,0:T(8,128)(2,1)}, u32[]{:S(2)}) copy-start(bf16[1,16,128,256]{3,2,1,0:T(8,128)(2,1)} %param.12) | copy-start | bytes 3145732
  73.4 23.1 %copy-start.12 = (f32[256]{0:T(256)S(1)}, f32[256]{0:T(256)}, u32[]{:S(2)}) copy-start(f32[256]{0:T(256)} %param.21) | copy-start | bytes 3076
  92.1 18.7 %all-to-all-start.1 = ((bf16[1,64,32,256]{3,2,0,1:T(8,128)(2,1)}), bf16[1,64,32,256]{3,2,0,1:T(8,128)(2,1)}, u32[]{:S(2)}, u32[]{:S(2)}) async-start(bf16[1,64,32,256]{3,2,0,1:T(8,128)(2,1)} %fusion.272), calls=%async_computation.1 | async-start | bytes 2097152 | tf_op jit(solution)/shard_map/all_to_all | solution.py:143
  110.8 2.4 copy-start.10
  110.8 2.4 copy-start.11
  112.2 1.8 copy-start.14
  114.0 3.8 %copy-start.7 = (bf16[2048,256]{1,0:T(8,128)(2,1)}, bf16[2048,256]{1,0:T(8,128)(2,1)S(1)}, u32[]{:S(2)}) copy-start(bf16[2048,256]{1,0:T(8,128)(2,1)S(1)} %add_convert_fusion.1) | copy-start | bytes 3145732
  114.0 3.8 %copy-start.1 = (bf16[1,16,128,256]{3,2,1,0:T(8,128)(2,1)S(1)}, bf16[1,16,128,256]{3,2,1,0:T(8,128)(2,1)}, u32[]{:S(2)}) copy-start(bf16[1,16,128,256]{3,2,1,0:T(8,128)(2,1)} %param.11) | copy-start | bytes 3145732
  114.0 3.8 %copy-start.13 = (bf16[1024,256]{1,0:T(8,128)(2,1)S(1)}, bf16[1024,256]{1,0:T(8,128)(2,1)}, u32[]{:S(2)}) copy-start(bf16[1024,256]{1,0:T(8,128)(2,1)} %param.19) | copy-start | bytes 1572868
  114.0 3.8 %copy-start.15 = (f32[256]{0:T(256)S(1)}, f32[256]{0:T(256)}, u32[]{:S(2)}) copy-start(f32[256]{0:T(256)} %param.20) | copy-start | bytes 3076
  117.7 2.6 copy-start.17
  120.3 6.4 %copy-start.18 = (bf16[2048,256]{1,0:T(8,128)(2,1)}, bf16[2048,256]{1,0:T(8,128)(2,1)S(1)}, u32[]{:S(2)}) copy-start(bf16[2048,256]{1,0:T(8,128)(2,1)S(1)} %get-tuple-element.120) | copy-start | bytes 3145732
  126.7 1.9 copy-start.16
  131.5 17.9 %all-to-all-start.2 = ((bf16[1,16,128,256]{3,1,0,2:T(8,128)(2,1)}), bf16[1,16,128,256]{3,1,0,2:T(8,128)(2,1)S(1)}, u32[]{:S(2)}, u32[]{:S(2)}) async-start(bf16[1,16,128,256]{3,1,0,2:T(8,128)(2,1)} %copy.31), calls=%async_computation.2 | async-start | bytes 2097152 | tf_op jit(solution)/shard_map/all_to_all | solution.py:161
  149.8 9.0 %copy-start.4 = (bf16[1,16,128,256]{3,2,1,0:T(8,128)(2,1)S(1)}, bf16[1,16,128,256]{3,2,1,0:T(8,128)(2,1)}, u32[]{:S(2)}) copy-start(bf16[1,16,128,256]{3,2,1,0:T(8,128)(2,1)} %copy-done.3) | copy-start | bytes 3145732
  177.8 18.7 %all-to-all-start.3 = ((bf16[1,64,32,256]{3,2,0,1:T(8,128)(2,1)}), bf16[1,64,32,256]{3,2,0,1:T(8,128)(2,1)}, u32[]{:S(2)}, u32[]{:S(2)}) async-start(bf16[1,64,32,256]{3,2,0,1:T(8,128)(2,1)} %fusion.273), calls=%async_computation.3 | async-start | bytes 2097152 | tf_op jit(solution)/shard_map/all_to_all | solution.py:166
  185.6 12.3 %copy-start.2 = (bf16[1,16,128,256]{3,2,1,0:T(8,128)(2,1)S(1)}, bf16[1,16,128,256]{3,2,1,0:T(8,128)(2,1)}, u32[]{:S(2)}) copy-start(bf16[1,16,128,256]{3,2,1,0:T(8,128)(2,1)} %param.11) | copy-start | bytes 3145732
  213.1 13.1 %all-to-all-start.4 = ((f32[16,14,128]{2,1,0:T(8,128)}), f32[16,14,128]{2,1,0:T(8,128)S(1)}, u32[]{:S(2)}, u32[]{:S(2)}) async-start(f32[16,14,128]{2,1,0:T(8,128)} %reshape.784), calls=%async_computation.4 | async-start | bytes 262144 | tf_op jit(solution)/shard_map/all_to_all | solution.py:206
  218.8 106.6 %all-reduce.8.cloned.1.call-start = ((), (), s32[]{:S(2)}) async-start(), calls=%async_computation.6 | async-start | bytes 4194304 | tf_op jit(solution)/shard_map/psum | solution.py:173
  223.6 6.8 %copy-start.6 = (bf16[1,16,128,256]{3,2,1,0:T(8,128)(2,1)S(1)}, bf16[1,16,128,256]{3,2,1,0:T(8,128)(2,1)}, u32[]{:S(2)}) copy-start(bf16[1,16,128,256]{3,2,1,0:T(8,128)(2,1)} %param.12) | copy-start | bytes 3145732
  226.9 20.1 %all-to-all-start.5 = ((f32[16,14,128]{2,1,0:T(8,128)}), f32[16,14,128]{2,1,0:T(8,128)S(1)}, u32[]{:S(2)}, u32[]{:S(2)}) async-start(f32[16,14,128]{2,1,0:T(8,128)} %broadcast_in_dim.2), calls=%async_computation.5 | async-start | bytes 262144 | tf_op jit(solution)/shard_map/all_to_all | solution.py:208
  325.5 2.4 copy-start.8
Sparse Core Ops, SparseCore 0:
  223.8 101.5 all-reduce.7

commit v5 on v4

--- a/solution.py
+++ b/solution.py
@@ -134,11 +134,11 @@
     pixel_scale = 1.0 / math.sqrt(
         tiles_here * lax.axis_size("rep") * band_rows * lax.axis_size("rows") * columns
     )
-    image_padded = pad_along(images, 2, half_reach)
+    image_padded = pad_along(images.astype(jnp.float32), 2, half_reach)
     row_mix = slide_padded(image_padded, row_taps, 2, columns).astype(jnp.bfloat16)
     row_mix = lax.optimization_barrier(row_mix)
     mix_columns = lax.all_to_all(row_mix, "rows", split_axis=2, concat_axis=1, tiled=True)
-    mix_padded = pad_along(mix_columns, 1, half_reach)
+    mix_padded = pad_along(mix_columns.astype(jnp.float32), 1, half_reach)
     col_local = slide_padded(mix_padded, col_taps, 1, mix_columns.shape[1]).astype(jnp.bfloat16)
     col_mix = lax.all_to_all(col_local, "rows", split_axis=1, concat_axis=2, tiled=True)
     col_mix = lax.optimization_barrier(col_mix)
@@ -159,18 +159,21 @@
     grad_rows = lax.optimization_barrier(grad_rows)
     col_grad = grad_rows.reshape(images.shape)
     grad_columns = lax.all_to_all(col_grad, "rows", split_axis=2, concat_axis=1, tiled=True)
-    col_part = tap_sums(grad_columns, mix_padded, taps_count, 1)
+    grad_float = grad_columns.astype(jnp.float32)
+    col_part = tap_sums(grad_float, mix_padded, taps_count, 1)
     row_local = slide_padded(
-        pad_along(grad_columns, 1, half_reach), col_taps[::-1], 1, grad_columns.shape[1]
+        pad_along(grad_float, 1, half_reach), col_taps[::-1], 1, grad_columns.shape[1]
     ).astype(jnp.bfloat16)
     row_grad = lax.all_to_all(row_local, "rows", split_axis=1, concat_axis=2, tiled=True)
     row_grad = lax.optimization_barrier(row_grad)
-    row_part = tap_sums(row_grad, image_padded, taps_count, 2)
+    row_part = tap_sums(row_grad, pad_along(images, 2, half_reach), taps_count, 2)
     image_grad = (
         cotangent.astype(jnp.float32)
         + slide_padded(pad_along(row_grad, 2, half_reach), row_taps[::-1], 2, columns)
     ).astype(jnp.bfloat16)
-    down_total, up_total = lax.psum((down_part * pixel_scale, up_part * pixel_scale), ("rows", "rep"))
+    down_total, up_total = lax.optimization_barrier(
+        lax.psum((down_part * pixel_scale, up_part * pixel_scale), ("rows", "rep"))
+    )
     small = (row_part, col_part, scale_part, down_bias_part, up_bias_part, gain_part, shift_part)
     (
         row_total,

time: 336 us -> 256 us (0.76)
  waiting for transfers between devices: 128 us -> 61.3 us
  other arithmetic: 125 us -> 111 us
    psum x1, waiting for transfers between devices: 76.6 us -> 22.7 us  [per_device(): lax.psum((down_part * pixel_scale, up_part * pixel_scale), ('rows', 'rep'))]
    convert_element_type x1, other arithmetic: 41.6 us -> 16.8 us  [per_device(): slide_padded(image_padded, row_taps, 2, columns).astype(jnp.bfloat16)]
    all_to_all x1, waiting for transfers between devices: 10.8 us -> 2.02 us  [per_device(): lax.all_to_all(row_local, 'rows', split_axis=1, concat_axis=2, tiled=True)]
    reduce_sum x7, other arithmetic: 26.7 us -> 35.1 us  [tap_sums(): jnp.sum(cot_field.astype(jnp.float32) * lax.slice_in_dim(padded, offset,...]
    convert_element_type x1 -> x4, other arithmetic: 18.6 us -> 20.7 us  [the longest x1 17.4 us: per_device(): row_local = slide_padded(pad_along(grad_float, 1, half_reach), col_taps[:...]
  transfers between devices with their start and end apart: 7 -> 7, of which waited for: 6 -> 5; matrix products, arithmetic and copies ran while one was open for 10% -> 31% of each run, Pallas kernels for 0% -> 0%
where the time goes in v5:
time: 256 us; the launch traced here: 255 us
  other arithmetic  111 us (43%)
  waiting for transfers between devices  61.3 us (24%)
  starting transfers between devices  28.3 us (11%)
  matrix products  21.7 us (8%)
  local copies, waits for them, and re-layouts  18.1 us (7%)
  between operations  14.5 us (6%)
    reduce_sum x7, other arithmetic, tap_sums(): jnp.sum(cot_field.astype(jnp.float32) * lax.slice_in_dim(padded, offset,...  35.1 us
    psum x1, waiting for transfers between devices, per_device(): lax.psum((down_part * pixel_scale, up_part * pixel_scale), ('rows', 'rep'))  22.7 us
    convert_element_type x1, other arithmetic, per_device(): slide_padded(mix_padded, col_taps, 1, mix_columns.shape[1])  17.4 us
    convert_element_type x1, other arithmetic, per_device(): row_local = slide_padded(pad_along(grad_float, 1, half_reach), col_taps[:...  17.4 us
    convert_element_type x1, other arithmetic, per_device(): slide_padded(image_padded, row_taps, 2, columns).astype(jnp.bfloat16)  16.8 us
    convert_element_type x1, other arithmetic, per_device(): image_grad = (cotangent.astype(jnp.float32) + slide_padded(pad_along(row_...  16.5 us
    all_to_all x1, waiting for transfers between devices, per_device(): lax.all_to_all(row_mix, 'rows', split_axis=2, concat_axis=1, tiled=True)  14.4 us
    all_to_all x1, waiting for transfers between devices, per_device(): lax.all_to_all(col_local, 'rows', split_axis=1, concat_axis=2, tiled=True)  12.8 us
  transfers between devices with their start and end apart: 7, of which 5 were waited for; matrix products, arithmetic and copies ran while one was open for 31% of the time, Pallas kernels for 0%

profile of v5, /device:TPU:0, one launch (start us, length us, event | category | flops | bytes accessed | tf_op | source)
XLA Modules:
  0.0 254.9 jit_solution(10180881011786007776)
XLA Ops:
  11.7 16.8 %fusion.101 = bf16[1,16,128,256]{3,2,1,0:T(8,128)(2,1)} fusion(f32[1,16,128,256]{3,2,1,0:T(8,128)S(1)} %convert_element_type.614, f32[256]{0:T(256)S(1)} %bitcast.469, f32[256]{0:T(256)S(1)} %bitcast.471, f32[256]{0:T(256)S(1)} %bitcast.335, f32[256]{0:T(256)S(1)} %bitcast.337, f32[256]{0:T(256)S(1)} %bitcast.339, f32[256]{0:T(256)S(1)} %bitcast.341, ...), kind=kLoop, calls=%fused_computation.407 | loop fusion | flops 53477376 | bytes 3197952 | tf_op jit(solution)/shard_map/convert_element_type | solution.py:138
  28.4 2.8 %copy.26 = bf16[1,16,128,256]{3,1,0,2:T(8,128)(2,1)} copy(bf16[1,16,128,256]{3,2,1,0:T(8,128)(2,1)} %fusion.101) | data formatting | bytes 2097152 | tf_op jit(solution)/shard_map/optimization_barrier | solution.py:139
  31.2 4.2 %all-to-all-start = ((bf16[1,16,128,256]{3,1,0,2:T(8,128)(2,1)}), bf16[1,16,128,256]{3,1,0,2:T(8,128)(2,1)S(1)}, u32[]{:S(2)}, u32[]{:S(2)}) async-start(bf16[1,16,128,256]{3,1,0,2:T(8,128)(2,1)} %copy.26), calls=%async_computation | async-start | bytes 2097152 | tf_op jit(solution)/shard_map/all_to_all | solution.py:140
  35.5 14.4 %all-to-all-done = bf16[1,16,128,256]{3,1,0,2:T(8,128)(2,1)S(1)} async-done(((bf16[1,16,128,256]{3,1,0,2:T(8,128)(2,1)}), bf16[1,16,128,256]{3,1,0,2:T(8,128)(2,1)S(1)}, u32[]{:S(2)}, u32[]{:S(2)}) %all-to-all-start) | async-done | bytes 1048608 | tf_op jit(solution)/shard_map/all_to_all | solution.py:140
  51.0 17.4 %fusion.297 = bf16[1,64,32,256]{3,2,0,1:T(8,128)(2,1)} fusion(f32[1,64,32,256]{3,2,1,0:T(8,128)S(1)} %bitcast.275, f32[256]{0:T(256)S(1)} %bitcast.495, f32[256]{0:T(256)S(1)} %bitcast.497, f32[256]{0:T(256)S(1)} %bitcast.373, f32[256]{0:T(256)S(1)} %bitcast.375, f32[256]{0:T(256)S(1)} %bitcast.377, f32[256]{0:T(256)S(1)} %bitcast.379, ...), kind=kLoop, calls=%fused_computation.669 | loop fusion | flops 53477376 | bytes 3197952 | tf_op jit(solution)/shard_map/convert_element_type | solution.py:142
  68.4 4.4 %all-to-all-start.1 = ((bf16[1,64,32,256]{3,2,0,1:T(8,128)(2,1)}), bf16[1,64,32,256]{3,2,0,1:T(8,128)(2,1)}, u32[]{:S(2)}, u32[]{:S(2)}) async-start(bf16[1,64,32,256]{3,2,0,1:T(8,128)(2,1)} %fusion.297), calls=%async_computation.1 | async-start | bytes 2097152 | tf_op jit(solution)/shard_map/all_to_all | solution.py:143
  74.3 12.8 %all-to-all-done.1 = bf16[1,64,32,256]{3,2,0,1:T(8,128)(2,1)} async-done(((bf16[1,64,32,256]{3,2,0,1:T(8,128)(2,1)}), bf16[1,64,32,256]{3,2,0,1:T(8,128)(2,1)}, u32[]{:S(2)}, u32[]{:S(2)}) %all-to-all-start.1) | async-done | bytes 1048608 | tf_op jit(solution)/shard_map/all_to_all | solution.py:143
  90.3 3.7 %multiply_convert_fusion = (bf16[2048,1024]{1,0:T(8,128)(2,1)S(1)}, f32[2048,1024]{1,0:T(8,128)S(1)}) fusion(f32[1024]{0:T(1024)S(1)} %copy-done.15, bf16[2048,256]{1,0:T(8,128)(2,1)S(1)} %add_convert_fusion, bf16[256,1024]{1,0:T(8,128)(2,1)S(1)} %copy-done), kind=kOutput, calls=%fused_computation.210 | convolution fusion | flops 1094713344 | bytes 14159872 | tf_op jit(solution)/shard_map/dot_general | solution.py:78
  94.1 2.6 %fusion.287 = (f32[256]{0:T(256)S(1)}, bf16[2048,256]{1,0:T(8,128)(2,1)}, bf16[2048,256]{1,0:T(8,128)(2,1)S(1)}) fusion(bf16[1,16,128,256]{3,2,1,0:T(8,128)(2,1)S(1)} %copy-done.6, f32[256]{0:T(256)S(1)} %copy-done.13, bf16[1,16,128,256]{3,2,1,0:T(8,128)(2,1)S(1)} %copy-done.2, f32[256]{0:T(256)S(1)} %copy-done.16, ...), kind=kOutput, calls=%fused_computation.597 | convolution fusion | flops 1078984448 | bytes 8915968 | tf_op jit(solution)/shard_map/dot_general | solution.py:80
  96.7 2.3 convolution_multiply_fusion
  99.0 6.4 %fusion.308 = (f32[1024]{0:T(1024)S(1)}, bf16[2048,1024]{1,0:T(8,128)(2,1)S(1)}) fusion(f32[2048,1024]{1,0:T(8,128)S(1)} %get-tuple-element.236, f32[1024]{0:T(1024)S(1)} %copy-done.15, bf16[2048,256]{1,0:T(8,128)(2,1)S(1)} %get-tuple-element.124, bf16[1024,256]{1,0:T(8,128)(2,1)S(1)} %copy-done.14), kind=kOutput, calls=%fused_computation.691 | convolution fusion | flops 1117780992 | bytes 14163968 | tf_op jit(solution)/shard_map/dot_general | solution.py:85
  105.4 1.9 multiply_reduce_fusion
  108.6 1.6 copy.31
  110.2 4.3 %all-to-all-start.2 = ((bf16[1,16,128,256]{3,1,0,2:T(8,128)(2,1)}), bf16[1,16,128,256]{3,1,0,2:T(8,128)(2,1)}, u32[]{:S(2)}, u32[]{:S(2)}) async-start(bf16[1,16,128,256]{3,1,0,2:T(8,128)(2,1)} %copy.31), calls=%async_computation.2 | async-start | bytes 2097152 | tf_op jit(solution)/shard_map/all_to_all | solution.py:161
  114.7 4.8 %fusion.294 = f32[256,1024]{1,0:T(8,128)} fusion(bf16[2048,256]{1,0:T(8,128)(2,1)} %copy-done.8, bf16[2048,1024]{1,0:T(8,128)(2,1)} %copy-done.17), kind=kOutput, calls=%fused_computation.664 | convolution fusion | flops 1074003968 | bytes 6291456 | tf_op jit(solution)/shard_map/dot_general | solution.py:109
  119.5 9.4 %all-to-all-done.2 = bf16[1,16,128,256]{3,1,0,2:T(8,128)(2,1)} async-done(((bf16[1,16,128,256]{3,1,0,2:T(8,128)(2,1)}), bf16[1,16,128,256]{3,1,0,2:T(8,128)(2,1)}, u32[]{:S(2)}, u32[]{:S(2)}) %all-to-all-start.2) | async-done | bytes 1048608 | tf_op jit(solution)/shard_map/all_to_all | solution.py:161
  128.9 1.6 copy_convert_fusion
  130.6 4.2 %multiply_reduce_fusion.1 = (f32[256]{0:T(256)S(1)}, f32[256]{0:T(256)S(1)}, f32[256]{0:T(256)S(1)}, f32[256]{0:T(256)S(1)}, f32[256]{0:T(256)S(1)}, /*index=5*/...) fusion(f32[1,64,32,256]{3,2,1,0:T(8,128)S(1)} %bitcast.279, ...), kind=kLoop, calls=%fused_computation.603 | loop fusion | flops 18869760 | bytes 4212736 | tf_op jit(solution)/shard_map/reduce_sum | solution.py:49
  134.8 4.9 %multiply_reduce_fusion.19 = (f32[256]{0:T(256)S(1)}, f32[256]{0:T(256)S(1)}, f32[256]{0:T(256)S(1)}, f32[256]{0:T(256)S(1)}, f32[256]{0:T(256)S(1)}, /*index=5*...) fusion(f32[1,64,32,256]{3,2,1,0:T(8,128)S(1)} %bitcast.280, ...), kind=kLoop, calls=%fused_computation.621 | loop fusion | flops 18869760 | bytes 4212736 | tf_op jit(solution)/shard_map/reduce_sum | solution.py:49
  139.7 17.4 %fusion.298 = bf16[1,64,32,256]{3,2,0,1:T(8,128)(2,1)} fusion(f32[1,64,32,256]{3,2,1,0:T(8,128)S(1)} %bitcast.281, f32[256]{0:T(256)S(1)} %bitcast.372, f32[256]{0:T(256)S(1)} %bitcast.410, f32[256]{0:T(256)S(1)} %bitcast.474, f32[256]{0:T(256)S(1)} %bitcast.494, f32[256]{0:T(256)S(1)} %bitcast.492, f32[256]{0:T(256)S(1)} %bitcast.490, ...), kind=kLoop, calls=%fused_computation.670 | loop fusion | flops 53477376 | bytes 3197952 | tf_op jit(solution)/shard_map/convert_element_type | solution.py:166
  157.1 4.5 %all-to-all-start.3 = ((bf16[1,64,32,256]{3,2,0,1:T(8,128)(2,1)}), bf16[1,64,32,256]{3,2,0,1:T(8,128)(2,1)}, u32[]{:S(2)}, u32[]{:S(2)}) async-start(bf16[1,64,32,256]{3,2,0,1:T(8,128)(2,1)} %fusion.298), calls=%async_computation.3 | async-start | bytes 2097152 | tf_op jit(solution)/shard_map/all_to_all | solution.py:167
  161.6 9.8 %multiply_reduce_fusion.38 = (f32[256]{0:T(256)S(1)}, f32[256]{0:T(256)S(1)}, f32[256]{0:T(256)S(1)}, f32[256]{0:T(256)S(1)}, f32[256]{0:T(256)S(1)}, /*index=5*...) fusion(f32[1,64,32,256]{3,2,1,0:T(8,128)} %bitcast.282, ...), kind=kLoop, calls=%fused_computation.640 | loop fusion | flops 14676480 | bytes 4208640 | tf_op jit(solution)/shard_map/reduce_sum | solution.py:49
  171.5 2.1 multiply_reduce_fusion.26
  173.8 2.0 all-to-all-done.3
  177.2 4.8 %fusion.182 = (f32[256]{0:T(256)S(1)}, f32[256]{0:T(256)S(1)}, f32[256]{0:T(256)S(1)}, f32[256]{0:T(256)S(1)}, f32[256]{0:T(256)S(1)}, /*index=5*/f32[256]{0:T(2...) fusion(bf16[1,16,128,256]{3,2,1,0:T(8,128)(2,1)S(1)} %bitcast.2, ...), kind=kLoop, calls=%fused_computation.488 | loop fusion | flops 28831232 | bytes 2115584 | tf_op jit(solution)/shard_map/reduce_sum | solution.py:49
  182.0 5.1 %fusion.181 = (f32[256]{0:T(256)S(1)}, f32[256]{0:T(256)S(1)}, f32[256]{0:T(256)S(1)}, f32[256]{0:T(256)S(1)}, f32[256]{0:T(256)S(1)}, /*index=5*/f32[256]{0:T(2...) fusion(bf16[1,16,128,256]{3,2,1,0:T(8,128)(2,1)S(1)} %bitcast.2, ...), kind=kLoop, calls=%fused_computation.487 | loop fusion | flops 28831232 | bytes 2115584 | tf_op jit(solution)/shard_map/reduce_sum | solution.py:49
  187.1 4.2 %fusion.180 = (f32[256]{0:T(256)S(1)}, f32[256]{0:T(256)S(1)}, f32[256]{0:T(256)S(1)}, f32[256]{0:T(256)S(1)}, f32[256]{0:T(256)S(1)}, /*index=5*/f32[256]{0:T(2...) fusion(bf16[1,16,128,256]{3,2,1,0:T(8,128)(2,1)S(1)} %bitcast.2, ...), kind=kLoop, calls=%fused_computation.486 | loop fusion | flops 24113408 | bytes 2112512 | tf_op jit(solution)/shard_map/reduce_sum | solution.py:49
  192.4 6.6 %all-to-all-start.4 = ((f32[16,14,128]{2,1,0:T(8,128)}), f32[16,14,128]{2,1,0:T(8,128)S(1)}, u32[]{:S(2)}, u32[]{:S(2)}) async-start(f32[16,14,128]{2,1,0:T(8,128)} %reshape.797), calls=%async_computation.4 | async-start | bytes 262144 | tf_op jit(solution)/shard_map/all_to_all | solution.py:209
  199.0 22.7 %all-reduce.9.cloned.1.call-done = (f32[1024,256]{1,0:T(8,128)}, f32[256,1024]{1,0:T(8,128)}) async-done(((f32[1024,256]{1,0:T(8,128)}, f32[256,1024]{1,0:T(8,128)}), (f32[1024,256]{1,0:T(8,128)}, f32[256,1024]{1,0:T(8,128)})) %all-reduce.9.cloned.1.call-update) | async-done | bytes 2097168 | tf_op jit(solution)/shard_map/psum | solution.py:175
  222.4 4.0 %all-to-all-start.5 = ((f32[16,14,128]{2,1,0:T(8,128)}), f32[16,14,128]{2,1,0:T(8,128)S(1)}, u32[]{:S(2)}, u32[]{:S(2)}) async-start(f32[16,14,128]{2,1,0:T(8,128)} %broadcast_in_dim.2), calls=%async_computation.5 | async-start | bytes 262144 | tf_op jit(solution)/shard_map/all_to_all | solution.py:211
  226.5 16.5 %fusion.284 = bf16[1,16,128,256]{3,2,1,0:T(8,128)(2,1)} fusion(bf16[1,16,128,256]{3,2,1,0:T(8,128)(2,1)S(1)} %copy-done.7, bf16[1,16,128,256]{3,2,1,0:T(8,128)(2,1)S(1)} %bitcast.286, f32[256]{0:T(256)S(1)} %bitcast.470, f32[256]{0:T(256)S(1)} %bitcast.472, f32[256]{0:T(256)S(1)} %bitcast.336, f32[256]{0:T(256)S(1)} %bitcast.338, f32[256]{0:T(256)S(1)} %bitcast.340, ...), kind=kLoop, calls=%fused_computation.594 | loop fusion | flops 81264640 | bytes 3197952 | tf_op jit(solution)/shard_map/convert_element_type | solution.py:173
  244.9 2.3 copy.44
  (80 shorter events, 18.1 us)
Async XLA Ops:
  7.2 83.1 %copy-start = (bf16[256,1024]{1,0:T(8,128)(2,1)S(1)}, bf16[256,1024]{1,0:T(8,128)(2,1)}, u32[]{:S(2)}) copy-start(bf16[256,1024]{1,0:T(8,128)(2,1)} %param.17) | copy-start | bytes 1572868
  28.4 7.0 %copy-start.10 = (f32[51,256]{1,0:T(8,128)S(1)}, f32[51,256]{1,0:T(8,128)}, u32[]{:S(2)}) copy-start(f32[51,256]{1,0:T(8,128)} %param.14) | copy-start | bytes 156676
  31.2 18.7 %all-to-all-start = ((bf16[1,16,128,256]{3,1,0,2:T(8,128)(2,1)}), bf16[1,16,128,256]{3,1,0,2:T(8,128)(2,1)S(1)}, u32[]{:S(2)}, u32[]{:S(2)}) async-start(bf16[1,16,128,256]{3,1,0,2:T(8,128)(2,1)} %copy.26), calls=%async_computation | async-start | bytes 2097152 | tf_op jit(solution)/shard_map/all_to_all | solution.py:140
  49.9 1.0 copy-start.4
  51.0 21.8 %copy-start.13 = (f32[256]{0:T(256)S(1)}, f32[256]{0:T(256)}, u32[]{:S(2)}) copy-start(f32[256]{0:T(256)} %param.21) | copy-start | bytes 3076
  68.4 18.7 %all-to-all-start.1 = ((bf16[1,64,32,256]{3,2,0,1:T(8,128)(2,1)}), bf16[1,64,32,256]{3,2,0,1:T(8,128)(2,1)}, u32[]{:S(2)}, u32[]{:S(2)}) async-start(bf16[1,64,32,256]{3,2,0,1:T(8,128)(2,1)} %fusion.297), calls=%async_computation.1 | async-start | bytes 2097152 | tf_op jit(solution)/shard_map/all_to_all | solution.py:143
  87.1 2.4 copy-start.11
  87.1 2.4 copy-start.12
  88.4 1.8 copy-start.15
  90.2 3.8 %copy-start.8 = (bf16[2048,256]{1,0:T(8,128)(2,1)}, bf16[2048,256]{1,0:T(8,128)(2,1)S(1)}, u32[]{:S(2)}) copy-start(bf16[2048,256]{1,0:T(8,128)(2,1)S(1)} %add_convert_fusion) | copy-start | bytes 3145732
  90.3 3.8 %copy-start.2 = (bf16[1,16,128,256]{3,2,1,0:T(8,128)(2,1)S(1)}, bf16[1,16,128,256]{3,2,1,0:T(8,128)(2,1)}, u32[]{:S(2)}) copy-start(bf16[1,16,128,256]{3,2,1,0:T(8,128)(2,1)} %param.11) | copy-start | bytes 3145732
  90.3 3.8 %copy-start.6 = (bf16[1,16,128,256]{3,2,1,0:T(8,128)(2,1)S(1)}, bf16[1,16,128,256]{3,2,1,0:T(8,128)(2,1)}, u32[]{:S(2)}) copy-start(bf16[1,16,128,256]{3,2,1,0:T(8,128)(2,1)} %param.12) | copy-start | bytes 3145732
  90.3 3.8 %copy-start.14 = (bf16[1024,256]{1,0:T(8,128)(2,1)S(1)}, bf16[1024,256]{1,0:T(8,128)(2,1)}, u32[]{:S(2)}) copy-start(bf16[1024,256]{1,0:T(8,128)(2,1)} %param.19) | copy-start | bytes 1572868
  90.3 3.8 %copy-start.16 = (f32[256]{0:T(256)S(1)}, f32[256]{0:T(256)}, u32[]{:S(2)}) copy-start(f32[256]{0:T(256)} %param.20) | copy-start | bytes 3076
  105.4 1.9 copy-start.17
  110.2 18.8 %all-to-all-start.2 = ((bf16[1,16,128,256]{3,1,0,2:T(8,128)(2,1)}), bf16[1,16,128,256]{3,1,0,2:T(8,128)(2,1)}, u32[]{:S(2)}, u32[]{:S(2)}) async-start(bf16[1,16,128,256]{3,1,0,2:T(8,128)(2,1)} %copy.31), calls=%async_computation.2 | async-start | bytes 2097152 | tf_op jit(solution)/shard_map/all_to_all | solution.py:161
  114.4 107.3 %all-reduce.9.cloned.1.call-start = ((), (), s32[]{:S(2)}) async-start(), calls=%async_computation.6 | async-start | bytes 4194304 | tf_op jit(solution)/shard_map/psum | solution.py:175
  130.6 9.1 %copy-start.1 = (f32[1,4,16,32,256]{4,3,2,1,0:T(8,128)}, f32[1,4,16,32,256]{4,3,2,1,0:T(8,128)S(1)}, u32[]{:S(2)}) copy-start(f32[1,4,16,32,256]{4,3,2,1,0:T(8,128)S(1)} %copy.33) | copy-start | bytes 6291460
  157.1 18.8 %all-to-all-start.3 = ((bf16[1,64,32,256]{3,2,0,1:T(8,128)(2,1)}), bf16[1,64,32,256]{3,2,0,1:T(8,128)(2,1)}, u32[]{:S(2)}, u32[]{:S(2)}) async-start(bf16[1,64,32,256]{3,2,0,1:T(8,128)(2,1)} %fusion.298), calls=%async_computation.3 | async-start | bytes 2097152 | tf_op jit(solution)/shard_map/all_to_all | solution.py:167
  161.6 9.9 %copy-start.5 = (bf16[1,16,128,256]{3,1,0,2:T(8,128)(2,1)S(1)}, bf16[1,16,128,256]{3,1,0,2:T(8,128)(2,1)}, u32[]{:S(2)}) copy-start(bf16[1,16,128,256]{3,1,0,2:T(8,128)(2,1)} %copy-done.4) | copy-start | bytes 3145732
  171.5 5.7 %copy-start.3 = (bf16[1,16,128,256]{3,2,1,0:T(8,128)(2,1)S(1)}, bf16[1,16,128,256]{3,2,1,0:T(8,128)(2,1)}, u32[]{:S(2)}) copy-start(bf16[1,16,128,256]{3,2,1,0:T(8,128)(2,1)} %param.11) | copy-start | bytes 3145732
  191.3 35.2 %copy-start.7 = (bf16[1,16,128,256]{3,2,1,0:T(8,128)(2,1)S(1)}, bf16[1,16,128,256]{3,2,1,0:T(8,128)(2,1)}, u32[]{:S(2)}) copy-start(bf16[1,16,128,256]{3,2,1,0:T(8,128)(2,1)} %param.12) | copy-start | bytes 3145732
  192.4 29.3 %all-to-all-start.4 = ((f32[16,14,128]{2,1,0:T(8,128)}), f32[16,14,128]{2,1,0:T(8,128)S(1)}, u32[]{:S(2)}, u32[]{:S(2)}) async-start(f32[16,14,128]{2,1,0:T(8,128)} %reshape.797), calls=%async_computation.4 | async-start | bytes 262144 | tf_op jit(solution)/shard_map/all_to_all | solution.py:209
  222.4 20.6 %all-to-all-start.5 = ((f32[16,14,128]{2,1,0:T(8,128)}), f32[16,14,128]{2,1,0:T(8,128)S(1)}, u32[]{:S(2)}, u32[]{:S(2)}) async-start(f32[16,14,128]{2,1,0:T(8,128)} %broadcast_in_dim.2), calls=%async_computation.5 | async-start | bytes 262144 | tf_op jit(solution)/shard_map/all_to_all | solution.py:211
  243.0 4.1 %copy-start.9 = (f32[256,1024]{1,0:T(8,128)S(1)}, f32[256,1024]{1,0:T(8,128)}, u32[]{:S(2)}) copy-start(f32[256,1024]{1,0:T(8,128)} %get-tuple-element.256) | copy-start | bytes 3145732
Sparse Core Ops, SparseCore 0:
  119.6 102.0 all-reduce.8

commit v6 on v5

--- a/solution.py
+++ b/solution.py
@@ -175,6 +175,7 @@
         lax.psum((down_part * pixel_scale, up_part * pixel_scale), ("rows", "rep"))
     )
     small = (row_part, col_part, scale_part, down_bias_part, up_bias_part, gain_part, shift_part)
+    small, image_grad = lax.optimization_barrier((small, image_grad))
     (
         row_total,
         col_total,

time: 256 us -> 245 us (0.957)
  waiting for transfers between devices: 61.3 us -> 44.3 us
  blocking collectives: 0 us -> 13.8 us
  starting transfers between devices: 28.3 us -> 21.3 us
    psum x1, waiting for transfers between devices: 22.7 us -> 0.02 us  [per_device(): lax.psum((down_part * pixel_scale, up_part * pixel_scale), ('rows', 'rep'))]
    all_to_all x0 -> x1, blocking collectives: none -> 13.8 us  [exchange_sum(): lax.all_to_all(stacked.reshape(count, piece, 128), axes, 0, 0, tiled=True)]
    all_to_all x1, waiting for transfers between devices: 0.01 us -> 7.34 us  [exchange_sum(): lax.all_to_all(jnp.broadcast_to(mine, (count, piece, 128)), axes, 0, 0, t...]
    all_to_all x1 -> x0, starting transfers between devices: 6.62 us -> none  [exchange_sum(): lax.all_to_all(stacked.reshape(count, piece, 128), axes, 0, 0, tiled=True)]
  transfers between devices with their start and end apart: 7 -> 6, of which waited for: 5 -> 5; matrix products, arithmetic and copies ran while one was open for 31% -> 33% of each run, Pallas kernels for 0% -> 0%
where the time goes in v6:
time: 245 us; the launch traced here: 244 us
  other arithmetic  110 us (45%)
  waiting for transfers between devices  44.3 us (18%)
  matrix products  22 us (9%)
  starting transfers between devices  21.3 us (9%)
  local copies, waits for them, and re-layouts  17.4 us (7%)
  between operations  14.6 us (6%)
  blocking collectives  13.8 us (6%)
    reduce_sum x7, other arithmetic, tap_sums(): jnp.sum(cot_field.astype(jnp.float32) * lax.slice_in_dim(padded, offset,...  34.3 us
    convert_element_type x1, other arithmetic, per_device(): row_local = slide_padded(pad_along(grad_float, 1, half_reach), col_taps[:...  17.4 us
    convert_element_type x1, other arithmetic, per_device(): slide_padded(mix_padded, col_taps, 1, mix_columns.shape[1])  17.4 us
    convert_element_type x1, other arithmetic, per_device(): slide_padded(image_padded, row_taps, 2, columns).astype(jnp.bfloat16)  16.7 us
    convert_element_type x1, other arithmetic, per_device(): image_grad = (cotangent.astype(jnp.float32) + slide_padded(pad_along(row_...  16.5 us
    all_to_all x1, waiting for transfers between devices, per_device(): lax.all_to_all(row_mix, 'rows', split_axis=2, concat_axis=1, tiled=True)  14.4 us
    all_to_all x1, blocking collectives, exchange_sum(): lax.all_to_all(stacked.reshape(count, piece, 128), axes, 0, 0, tiled=True)  13.8 us
    all_to_all x1, waiting for transfers between devices, per_device(): lax.all_to_all(col_local, 'rows', split_axis=1, concat_axis=2, tiled=True)  12.8 us
  transfers between devices with their start and end apart: 6, of which 5 were waited for; matrix products, arithmetic and copies ran while one was open for 33% of the time, Pallas kernels for 0%

profile of v6, /device:TPU:0, one launch (start us, length us, event | category | flops | bytes accessed | tf_op | source)
XLA Modules:
  0.0 243.7 jit_solution(17853103843633569092)
XLA Ops:
  11.6 16.7 %fusion.101 = bf16[1,16,128,256]{3,2,1,0:T(8,128)(2,1)} fusion(f32[1,16,128,256]{3,2,1,0:T(8,128)S(1)} %convert_element_type.614, f32[256]{0:T(256)S(1)} %bitcast.469, f32[256]{0:T(256)S(1)} %bitcast.471, f32[256]{0:T(256)S(1)} %bitcast.335, f32[256]{0:T(256)S(1)} %bitcast.337, f32[256]{0:T(256)S(1)} %bitcast.339, f32[256]{0:T(256)S(1)} %bitcast.341, ...), kind=kLoop, calls=%fused_computation.407 | loop fusion | flops 53477376 | bytes 3197952 | tf_op jit(solution)/shard_map/convert_element_type | solution.py:138
  28.4 2.8 %copy.26 = bf16[1,16,128,256]{3,1,0,2:T(8,128)(2,1)} copy(bf16[1,16,128,256]{3,2,1,0:T(8,128)(2,1)} %fusion.101) | data formatting | bytes 2097152 | tf_op jit(solution)/shard_map/optimization_barrier | solution.py:139
  31.2 4.2 %all-to-all-start = ((bf16[1,16,128,256]{3,1,0,2:T(8,128)(2,1)}), bf16[1,16,128,256]{3,1,0,2:T(8,128)(2,1)S(1)}, u32[]{:S(2)}, u32[]{:S(2)}) async-start(bf16[1,16,128,256]{3,1,0,2:T(8,128)(2,1)} %copy.26), calls=%async_computation | async-start | bytes 2097152 | tf_op jit(solution)/shard_map/all_to_all | solution.py:140
  35.5 14.4 %all-to-all-done = bf16[1,16,128,256]{3,1,0,2:T(8,128)(2,1)S(1)} async-done(((bf16[1,16,128,256]{3,1,0,2:T(8,128)(2,1)}), bf16[1,16,128,256]{3,1,0,2:T(8,128)(2,1)S(1)}, u32[]{:S(2)}, u32[]{:S(2)}) %all-to-all-start) | async-done | bytes 1048608 | tf_op jit(solution)/shard_map/all_to_all | solution.py:140
  50.9 17.4 %fusion.297 = bf16[1,64,32,256]{3,2,0,1:T(8,128)(2,1)} fusion(f32[1,64,32,256]{3,2,1,0:T(8,128)S(1)} %bitcast.275, f32[256]{0:T(256)S(1)} %bitcast.495, f32[256]{0:T(256)S(1)} %bitcast.497, f32[256]{0:T(256)S(1)} %bitcast.373, f32[256]{0:T(256)S(1)} %bitcast.375, f32[256]{0:T(256)S(1)} %bitcast.377, f32[256]{0:T(256)S(1)} %bitcast.379, ...), kind=kLoop, calls=%fused_computation.669 | loop fusion | flops 53477376 | bytes 3197952 | tf_op jit(solution)/shard_map/convert_element_type | solution.py:142
  68.3 4.4 %all-to-all-start.1 = ((bf16[1,64,32,256]{3,2,0,1:T(8,128)(2,1)}), bf16[1,64,32,256]{3,2,0,1:T(8,128)(2,1)}, u32[]{:S(2)}, u32[]{:S(2)}) async-start(bf16[1,64,32,256]{3,2,0,1:T(8,128)(2,1)} %fusion.297), calls=%async_computation.1 | async-start | bytes 2097152 | tf_op jit(solution)/shard_map/all_to_all | solution.py:143
  74.3 12.8 %all-to-all-done.1 = bf16[1,64,32,256]{3,2,0,1:T(8,128)(2,1)} async-done(((bf16[1,64,32,256]{3,2,0,1:T(8,128)(2,1)}), bf16[1,64,32,256]{3,2,0,1:T(8,128)(2,1)}, u32[]{:S(2)}, u32[]{:S(2)}) %all-to-all-start.1) | async-done | bytes 1048608 | tf_op jit(solution)/shard_map/all_to_all | solution.py:143
  90.3 3.7 %multiply_convert_fusion = (bf16[2048,1024]{1,0:T(8,128)(2,1)S(1)}, f32[2048,1024]{1,0:T(8,128)S(1)}) fusion(f32[1024]{0:T(1024)S(1)} %copy-done.15, bf16[2048,256]{1,0:T(8,128)(2,1)S(1)} %add_convert_fusion, bf16[256,1024]{1,0:T(8,128)(2,1)S(1)} %copy-done), kind=kOutput, calls=%fused_computation.210 | convolution fusion | flops 1094713344 | bytes 14159872 | tf_op jit(solution)/shard_map/dot_general | solution.py:78
  94.1 2.6 %fusion.287 = (f32[256]{0:T(256)S(1)}, bf16[2048,256]{1,0:T(8,128)(2,1)}, bf16[2048,256]{1,0:T(8,128)(2,1)S(1)}) fusion(bf16[1,16,128,256]{3,2,1,0:T(8,128)(2,1)S(1)} %copy-done.6, f32[256]{0:T(256)S(1)} %copy-done.13, bf16[1,16,128,256]{3,2,1,0:T(8,128)(2,1)S(1)} %copy-done.3, f32[256]{0:T(256)S(1)} %copy-done.16, ...), kind=kOutput, calls=%fused_computation.597 | convolution fusion | flops 1078984448 | bytes 8915968 | tf_op jit(solution)/shard_map/dot_general | solution.py:80
  96.7 6.4 %fusion.308 = (f32[1024]{0:T(1024)S(1)}, bf16[2048,1024]{1,0:T(8,128)(2,1)S(1)}) fusion(f32[2048,1024]{1,0:T(8,128)S(1)} %get-tuple-element.252, f32[1024]{0:T(1024)S(1)} %copy-done.15, bf16[2048,256]{1,0:T(8,128)(2,1)S(1)} %get-tuple-element.140, bf16[1024,256]{1,0:T(8,128)(2,1)S(1)} %copy-done.14), kind=kOutput, calls=%fused_computation.691 | convolution fusion | flops 1117780992 | bytes 14163968 | tf_op jit(solution)/shard_map/dot_general | solution.py:85
  103.1 2.0 multiply_reduce_fusion
  106.3 1.6 copy.31
  107.9 4.2 %all-to-all-start.2 = ((bf16[1,16,128,256]{3,1,0,2:T(8,128)(2,1)}), bf16[1,16,128,256]{3,1,0,2:T(8,128)(2,1)}, u32[]{:S(2)}, u32[]{:S(2)}) async-start(bf16[1,16,128,256]{3,1,0,2:T(8,128)(2,1)} %copy.31), calls=%async_computation.2 | async-start | bytes 2097152 | tf_op jit(solution)/shard_map/all_to_all | solution.py:161
  112.5 5.0 %fusion.294 = f32[256,1024]{1,0:T(8,128)} fusion(bf16[2048,256]{1,0:T(8,128)(2,1)} %copy-done.8, bf16[2048,1024]{1,0:T(8,128)(2,1)} %copy-done.17), kind=kOutput, calls=%fused_computation.664 | convolution fusion | flops 1074003968 | bytes 6291456 | tf_op jit(solution)/shard_map/dot_general | solution.py:109
  117.5 2.3 convolution_multiply_fusion
  119.8 6.9 %all-to-all-done.2 = bf16[1,16,128,256]{3,1,0,2:T(8,128)(2,1)} async-done(((bf16[1,16,128,256]{3,1,0,2:T(8,128)(2,1)}), bf16[1,16,128,256]{3,1,0,2:T(8,128)(2,1)}, u32[]{:S(2)}, u32[]{:S(2)}) %all-to-all-start.2) | async-done | bytes 1048608 | tf_op jit(solution)/shard_map/all_to_all | solution.py:161
  126.7 1.7 copy_convert_fusion
  128.6 17.4 %fusion.298 = bf16[1,64,32,256]{3,2,0,1:T(8,128)(2,1)} fusion(f32[1,64,32,256]{3,2,1,0:T(8,128)S(1)} %bitcast.279, f32[256]{0:T(256)S(1)} %bitcast.372, f32[256]{0:T(256)S(1)} %bitcast.410, f32[256]{0:T(256)S(1)} %bitcast.474, f32[256]{0:T(256)S(1)} %bitcast.494, f32[256]{0:T(256)S(1)} %bitcast.492, f32[256]{0:T(256)S(1)} %bitcast.490, ...), kind=kLoop, calls=%fused_computation.670 | loop fusion | flops 53477376 | bytes 3197952 | tf_op jit(solution)/shard_map/convert_element_type | solution.py:166
  145.9 4.1 %multiply_reduce_fusion.1 = (f32[256]{0:T(256)S(1)}, f32[256]{0:T(256)S(1)}, f32[256]{0:T(256)S(1)}, f32[256]{0:T(256)S(1)}, f32[256]{0:T(256)S(1)}, /*index=5*/...) fusion(f32[1,64,32,256]{3,2,1,0:T(8,128)S(1)} %bitcast.280, ...), kind=kLoop, calls=%fused_computation.603 | loop fusion | flops 18869760 | bytes 4212736 | tf_op jit(solution)/shard_map/reduce_sum | solution.py:49
  150.1 4.9 %multiply_reduce_fusion.19 = (f32[256]{0:T(256)S(1)}, f32[256]{0:T(256)S(1)}, f32[256]{0:T(256)S(1)}, f32[256]{0:T(256)S(1)}, f32[256]{0:T(256)S(1)}, /*index=5*...) fusion(f32[1,64,32,256]{3,2,1,0:T(8,128)S(1)} %bitcast.281, ...), kind=kLoop, calls=%fused_computation.621 | loop fusion | flops 18869760 | bytes 4212736 | tf_op jit(solution)/shard_map/reduce_sum | solution.py:49
  155.0 4.5 %all-to-all-start.3 = ((bf16[1,64,32,256]{3,2,0,1:T(8,128)(2,1)}), bf16[1,64,32,256]{3,2,0,1:T(8,128)(2,1)}, u32[]{:S(2)}, u32[]{:S(2)}) async-start(bf16[1,64,32,256]{3,2,0,1:T(8,128)(2,1)} %fusion.298), calls=%async_computation.3 | async-start | bytes 2097152 | tf_op jit(solution)/shard_map/all_to_all | solution.py:167
  159.5 2.3 multiply_reduce_fusion.26
  161.8 8.9 %multiply_reduce_fusion.38 = (f32[256]{0:T(256)S(1)}, f32[256]{0:T(256)S(1)}, f32[256]{0:T(256)S(1)}, f32[256]{0:T(256)S(1)}, f32[256]{0:T(256)S(1)}, /*index=5*...) fusion(f32[1,64,32,256]{3,2,1,0:T(8,128)S(1)} %bitcast.282, ...), kind=kLoop, calls=%fused_computation.640 | loop fusion | flops 14676480 | bytes 4208640 | tf_op jit(solution)/shard_map/reduce_sum | solution.py:49
  170.8 2.9 %all-to-all-done.3 = bf16[1,64,32,256]{3,2,0,1:T(8,128)(2,1)} async-done(((bf16[1,64,32,256]{3,2,0,1:T(8,128)(2,1)}), bf16[1,64,32,256]{3,2,0,1:T(8,128)(2,1)}, u32[]{:S(2)}, u32[]{:S(2)}) %all-to-all-start.3) | async-done | bytes 1048608 | tf_op jit(solution)/shard_map/all_to_all | solution.py:167
  175.1 16.5 %fusion.285 = bf16[1,16,128,256]{3,2,1,0:T(8,128)(2,1)} fusion(bf16[1,16,128,256]{3,2,1,0:T(8,128)(2,1)S(1)} %copy-done.7, bf16[1,16,128,256]{3,2,1,0:T(8,128)(2,1)S(1)} %bitcast.283, f32[256]{0:T(256)S(1)} %bitcast.470, f32[256]{0:T(256)S(1)} %bitcast.472, f32[256]{0:T(256)S(1)} %bitcast.336, f32[256]{0:T(256)S(1)} %bitcast.338, f32[256]{0:T(256)S(1)} %bitcast.340, ...), kind=kLoop, calls=%fused_computation.595 | loop fusion | flops 81264640 | bytes 3197952 | tf_op jit(solution)/shard_map/convert_element_type | solution.py:173
  191.6 5.0 %fusion.157 = (f32[256]{0:T(256)S(1)}, f32[256]{0:T(256)S(1)}, f32[256]{0:T(256)S(1)}, f32[256]{0:T(256)S(1)}, f32[256]{0:T(256)S(1)}, /*index=5*/f32[256]{0:T(2...) fusion(bf16[1,16,128,256]{3,2,1,0:T(8,128)(2,1)S(1)} %bitcast.2, ...), kind=kLoop, calls=%fused_computation.463 | loop fusion | flops 28831232 | bytes 2115584 | tf_op jit(solution)/shard_map/reduce_sum | solution.py:49
  196.6 5.0 %fusion.156 = (f32[256]{0:T(256)S(1)}, f32[256]{0:T(256)S(1)}, f32[256]{0:T(256)S(1)}, f32[256]{0:T(256)S(1)}, f32[256]{0:T(256)S(1)}, /*index=5*/f32[256]{0:T(2...) fusion(bf16[1,16,128,256]{3,2,1,0:T(8,128)(2,1)S(1)} %bitcast.2, ...), kind=kLoop, calls=%fused_computation.462 | loop fusion | flops 28831232 | bytes 2115584 | tf_op jit(solution)/shard_map/reduce_sum | solution.py:49
  201.7 4.1 %fusion.155 = (f32[256]{0:T(256)S(1)}, f32[256]{0:T(256)S(1)}, f32[256]{0:T(256)S(1)}, f32[256]{0:T(256)S(1)}, f32[256]{0:T(256)S(1)}, /*index=5*/f32[256]{0:T(2...) fusion(bf16[1,16,128,256]{3,2,1,0:T(8,128)(2,1)S(1)} %bitcast.2, ...), kind=kLoop, calls=%fused_computation.461 | loop fusion | flops 24113408 | bytes 2112512 | tf_op jit(solution)/shard_map/reduce_sum | solution.py:49
  206.3 13.8 %all_to_all.64 = f32[16,14,128]{2,1,0:T(8,128)S(1)} all-to-all(f32[16,14,128]{2,1,0:T(8,128)S(1)} %reshape.797), channel_id=1, replica_groups=mesh['groups'=2,'rows'=4,'rep'=4] {'rows','rep'}, dimensions={0} | all-to-all | bytes 229376 | tf_op jit(solution)/shard_map/all_to_all | solution.py:210
  220.8 3.6 %all-to-all-start.5 = ((f32[16,14,128]{2,1,0:T(8,128)}), f32[16,14,128]{2,1,0:T(8,128)S(1)}, u32[]{:S(2)}, u32[]{:S(2)}) async-start(f32[16,14,128]{2,1,0:T(8,128)} %broadcast_in_dim.2), calls=%async_computation.5 | async-start | bytes 262144 | tf_op jit(solution)/shard_map/all_to_all | solution.py:212
  224.4 7.3 %all-to-all-done.5 = f32[16,14,128]{2,1,0:T(8,128)S(1)} async-done(((f32[16,14,128]{2,1,0:T(8,128)}), f32[16,14,128]{2,1,0:T(8,128)S(1)}, u32[]{:S(2)}, u32[]{:S(2)}) %all-to-all-start.5) | async-done | bytes 114720 | tf_op jit(solution)/shard_map/all_to_all | solution.py:212
  233.6 2.3 copy.44
  (89 shorter events, 17.5 us)
Async XLA Ops:
  7.2 83.0 %copy-start = (bf16[256,1024]{1,0:T(8,128)(2,1)S(1)}, bf16[256,1024]{1,0:T(8,128)(2,1)}, u32[]{:S(2)}) copy-start(bf16[256,1024]{1,0:T(8,128)(2,1)} %param.17) | copy-start | bytes 1572868
  28.4 7.0 %copy-start.10 = (f32[51,256]{1,0:T(8,128)S(1)}, f32[51,256]{1,0:T(8,128)}, u32[]{:S(2)}) copy-start(f32[51,256]{1,0:T(8,128)} %param.14) | copy-start | bytes 156676
  31.2 18.7 %all-to-all-start = ((bf16[1,16,128,256]{3,1,0,2:T(8,128)(2,1)}), bf16[1,16,128,256]{3,1,0,2:T(8,128)(2,1)S(1)}, u32[]{:S(2)}, u32[]{:S(2)}) async-start(bf16[1,16,128,256]{3,1,0,2:T(8,128)(2,1)} %copy.26), calls=%async_computation | async-start | bytes 2097152 | tf_op jit(solution)/shard_map/all_to_all | solution.py:140
  49.8 1.0 copy-start.5
  50.9 21.8 %copy-start.13 = (f32[256]{0:T(256)S(1)}, f32[256]{0:T(256)}, u32[]{:S(2)}) copy-start(f32[256]{0:T(256)} %param.21) | copy-start | bytes 3076
  68.3 18.7 %all-to-all-start.1 = ((bf16[1,64,32,256]{3,2,0,1:T(8,128)(2,1)}), bf16[1,64,32,256]{3,2,0,1:T(8,128)(2,1)}, u32[]{:S(2)}, u32[]{:S(2)}) async-start(bf16[1,64,32,256]{3,2,0,1:T(8,128)(2,1)} %fusion.297), calls=%async_computation.1 | async-start | bytes 2097152 | tf_op jit(solution)/shard_map/all_to_all | solution.py:143
  87.1 2.4 copy-start.11
  87.1 2.4 copy-start.12
  88.4 1.8 copy-start.15
  90.2 3.8 %copy-start.8 = (bf16[2048,256]{1,0:T(8,128)(2,1)}, bf16[2048,256]{1,0:T(8,128)(2,1)S(1)}, u32[]{:S(2)}) copy-start(bf16[2048,256]{1,0:T(8,128)(2,1)S(1)} %add_convert_fusion) | copy-start | bytes 3145732
  90.2 3.8 %copy-start.3 = (bf16[1,16,128,256]{3,2,1,0:T(8,128)(2,1)S(1)}, bf16[1,16,128,256]{3,2,1,0:T(8,128)(2,1)}, u32[]{:S(2)}) copy-start(bf16[1,16,128,256]{3,2,1,0:T(8,128)(2,1)} %param.11) | copy-start | bytes 3145732
  90.2 3.8 %copy-start.6 = (bf16[1,16,128,256]{3,2,1,0:T(8,128)(2,1)S(1)}, bf16[1,16,128,256]{3,2,1,0:T(8,128)(2,1)}, u32[]{:S(2)}) copy-start(bf16[1,16,128,256]{3,2,1,0:T(8,128)(2,1)} %param.12) | copy-start | bytes 3145732
  90.2 3.8 %copy-start.14 = (bf16[1024,256]{1,0:T(8,128)(2,1)S(1)}, bf16[1024,256]{1,0:T(8,128)(2,1)}, u32[]{:S(2)}) copy-start(bf16[1024,256]{1,0:T(8,128)(2,1)} %param.19) | copy-start | bytes 1572868
  90.3 3.8 %copy-start.16 = (f32[256]{0:T(256)S(1)}, f32[256]{0:T(256)}, u32[]{:S(2)}) copy-start(f32[256]{0:T(256)} %param.20) | copy-start | bytes 3076
  94.0 2.7 %copy-start.18 = (bf16[2048,1024]{1,0:T(8,128)(2,1)}, bf16[2048,1024]{1,0:T(8,128)(2,1)S(1)}, u32[]{:S(2)}) copy-start(bf16[2048,1024]{1,0:T(8,128)(2,1)S(1)} %get-tuple-element.251) | copy-start | bytes 12582916
  96.7 6.4 %copy-start.20 = (bf16[2048,256]{1,0:T(8,128)(2,1)}, bf16[2048,256]{1,0:T(8,128)(2,1)S(1)}, u32[]{:S(2)}) copy-start(bf16[2048,256]{1,0:T(8,128)(2,1)S(1)} %get-tuple-element.140) | copy-start | bytes 3145732
  103.1 2.0 copy-start.17
  107.9 18.7 %all-to-all-start.2 = ((bf16[1,16,128,256]{3,1,0,2:T(8,128)(2,1)}), bf16[1,16,128,256]{3,1,0,2:T(8,128)(2,1)}, u32[]{:S(2)}, u32[]{:S(2)}) async-start(bf16[1,16,128,256]{3,1,0,2:T(8,128)(2,1)} %copy.31), calls=%async_computation.2 | async-start | bytes 2097152 | tf_op jit(solution)/shard_map/all_to_all | solution.py:161
  112.2 112.2 %all-reduce.9.cloned.1.call-start = ((), (), s32[]{:S(2)}) async-start(), calls=%async_computation.6 | async-start | bytes 4194304 | tf_op jit(solution)/shard_map/psum | solution.py:175
  112.4 5.0 %copy-start.19 = (bf16[2048,1024]{1,0:T(8,128)(2,1)S(1)}, bf16[2048,1024]{1,0:T(8,128)(2,1)}, u32[]{:S(2)}) copy-start(bf16[2048,1024]{1,0:T(8,128)(2,1)} %copy-done.18) | copy-start | bytes 12582916
  112.4 5.0 %copy-start.21 = (bf16[2048,256]{1,0:T(8,128)(2,1)S(1)}, bf16[2048,256]{1,0:T(8,128)(2,1)}, u32[]{:S(2)}) copy-start(bf16[2048,256]{1,0:T(8,128)(2,1)} %copy-done.20) | copy-start | bytes 3145732
  128.5 21.5 %copy-start.1 = (f32[1,4,16,32,256]{4,3,2,1,0:T(8,128)}, f32[1,4,16,32,256]{4,3,2,1,0:T(8,128)S(1)}, u32[]{:S(2)}) copy-start(f32[1,4,16,32,256]{4,3,2,1,0:T(8,128)S(1)} %copy.33) | copy-start | bytes 6291460
  155.0 18.8 %all-to-all-start.3 = ((bf16[1,64,32,256]{3,2,0,1:T(8,128)(2,1)}), bf16[1,64,32,256]{3,2,0,1:T(8,128)(2,1)}, u32[]{:S(2)}, u32[]{:S(2)}) async-start(bf16[1,64,32,256]{3,2,0,1:T(8,128)(2,1)} %fusion.298), calls=%async_computation.3 | async-start | bytes 2097152 | tf_op jit(solution)/shard_map/all_to_all | solution.py:167
  159.5 2.3 copy-start.2
  170.6 4.4 %copy-start.7 = (bf16[1,16,128,256]{3,2,1,0:T(8,128)(2,1)S(1)}, bf16[1,16,128,256]{3,2,1,0:T(8,128)(2,1)}, u32[]{:S(2)}) copy-start(bf16[1,16,128,256]{3,2,1,0:T(8,128)(2,1)} %param.12) | copy-start | bytes 3145732
  175.1 16.5 %copy-start.4 = (bf16[1,16,128,256]{3,2,1,0:T(8,128)(2,1)S(1)}, bf16[1,16,128,256]{3,2,1,0:T(8,128)(2,1)}, u32[]{:S(2)}) copy-start(bf16[1,16,128,256]{3,2,1,0:T(8,128)(2,1)} %param.11) | copy-start | bytes 3145732
  220.8 11.0 %all-to-all-start.5 = ((f32[16,14,128]{2,1,0:T(8,128)}), f32[16,14,128]{2,1,0:T(8,128)S(1)}, u32[]{:S(2)}, u32[]{:S(2)}) async-start(f32[16,14,128]{2,1,0:T(8,128)} %broadcast_in_dim.2), calls=%async_computation.5 | async-start | bytes 262144 | tf_op jit(solution)/shard_map/all_to_all | solution.py:212
  224.4 11.5 %copy-start.9 = (f32[256,1024]{1,0:T(8,128)S(1)}, f32[256,1024]{1,0:T(8,128)}, u32[]{:S(2)}) copy-start(f32[256,1024]{1,0:T(8,128)} %get-tuple-element.268) | copy-start | bytes 3145732
Sparse Core Ops, SparseCore 0:
  119.9 101.8 all-reduce.8

commit v7 on v5

--- a/solution.py
+++ b/solution.py
@@ -167,6 +167,7 @@
     row_grad = lax.all_to_all(row_local, "rows", split_axis=1, concat_axis=2, tiled=True)
     row_grad = lax.optimization_barrier(row_grad)
     row_part = tap_sums(row_grad, pad_along(images, 2, half_reach), taps_count, 2)
+    row_part, row_grad = lax.optimization_barrier((row_part, row_grad))
     image_grad = (
         cotangent.astype(jnp.float32)
         + slide_padded(pad_along(row_grad, 2, half_reach), row_taps[::-1], 2, columns)
@@ -183,7 +184,7 @@
         up_bias_total,
         gain_total,
         shift_total,
-    ) = exchange_sum(tuple(part * pixel_scale for part in small), ("rows", "rep"))
+    ), image_grad = exchange_sum(tuple(part * pixel_scale for part in small), ("rows", "rep"), image_grad)
     return (
         block_out,
         image_grad,
@@ -199,7 +200,7 @@
     )
 
 
-def exchange_sum(parts, axes):
+def exchange_sum(parts, axes, companion):
     count = 1
     for axis in axes:
         count *= lax.axis_size(axis)
@@ -208,8 +209,9 @@
     stacked = jnp.pad(stacked, ((0, piece * count - stacked.shape[0]), (0, 0)))
     spread = lax.all_to_all(stacked.reshape(count, piece, 128), axes, 0, 0, tiled=True)
     mine = jnp.sum(spread, axis=0, keepdims=True)
+    mine, companion = lax.optimization_barrier((mine, companion))
     whole = lax.all_to_all(jnp.broadcast_to(mine, (count, piece, 128)), axes, 0, 0, tiled=True)
-    return split_like(whole.reshape(-1), parts)
+    return split_like(whole.reshape(-1), parts), companion
 
 
 def split_like(flat, parts):

time: 256 us -> 243 us (0.949)
  waiting for transfers between devices: 61.3 us -> 45.9 us
    psum x1, waiting for transfers between devices: 22.7 us -> 0.02 us  [per_device(): lax.psum((down_part * pixel_scale, up_part * pixel_scale), ('rows', 'rep'))]
    all_to_all x1, waiting for transfers between devices: 0.01 us -> 7.34 us  [exchange_sum(): lax.all_to_all(jnp.broadcast_to(mine, (count, piece, 128)), axes, 0, 0, t...]
  transfers between devices with their start and end apart: 7 -> 7, of which waited for: 5 -> 5; matrix products, arithmetic and copies ran while one was open for 31% -> 33% of each run, Pallas kernels for 0% -> 0%
where the time goes in v7:
time: 243 us; the launch traced here: 242 us
  other arithmetic  111 us (46%)
  waiting for transfers between devices  45.9 us (19%)
  starting transfers between devices  30.3 us (12%)
  matrix products  21.8 us (9%)
  local copies, waits for them, and re-layouts  18.1 us (7%)
  between operations  14.6 us (6%)
    reduce_sum x7, other arithmetic, tap_sums(): jnp.sum(cot_field.astype(jnp.float32) * lax.slice_in_dim(padded, offset,...  35.1 us
    convert_element_type x1, other arithmetic, per_device(): slide_padded(mix_padded, col_taps, 1, mix_columns.shape[1])  17.4 us
    convert_element_type x1, other arithmetic, per_device(): row_local = slide_padded(pad_along(grad_float, 1, half_reach), col_taps[:...  17.4 us
    convert_element_type x1, other arithmetic, per_device(): slide_padded(image_padded, row_taps, 2, columns).astype(jnp.bfloat16)  16.8 us
    convert_element_type x1, other arithmetic, per_device(): image_grad = (cotangent.astype(jnp.float32) + slide_padded(pad_along(row_...  16.5 us
    all_to_all x1, waiting for transfers between devices, per_device(): lax.all_to_all(row_mix, 'rows', split_axis=2, concat_axis=1, tiled=True)  14.4 us
    all_to_all x1, waiting for transfers between devices, per_device(): lax.all_to_all(col_local, 'rows', split_axis=1, concat_axis=2, tiled=True)  12.8 us
    all_to_all x1, waiting for transfers between devices, per_device(): lax.all_to_all(col_grad, 'rows', split_axis=2, concat_axis=1, tiled=True)  9.35 us
  transfers between devices with their start and end apart: 7, of which 5 were waited for; matrix products, arithmetic and copies ran while one was open for 33% of the time, Pallas kernels for 0%

profile of v7, /device:TPU:0, one launch (start us, length us, event | category | flops | bytes accessed | tf_op | source)
XLA Modules:
  0.0 241.6 jit_solution(10967108993711986160)
XLA Ops:
  11.6 16.8 %fusion.101 = bf16[1,16,128,256]{3,2,1,0:T(8,128)(2,1)} fusion(f32[1,16,128,256]{3,2,1,0:T(8,128)S(1)} %convert_element_type.617, f32[256]{0:T(256)S(1)} %bitcast.471, f32[256]{0:T(256)S(1)} %bitcast.473, f32[256]{0:T(256)S(1)} %bitcast.337, f32[256]{0:T(256)S(1)} %bitcast.339, f32[256]{0:T(256)S(1)} %bitcast.341, f32[256]{0:T(256)S(1)} %bitcast.343, ...), kind=kLoop, calls=%fused_computation.406 | loop fusion | flops 53477376 | bytes 3197952 | tf_op jit(solution)/shard_map/convert_element_type | solution.py:138
  28.4 2.8 %copy.26 = bf16[1,16,128,256]{3,1,0,2:T(8,128)(2,1)} copy(bf16[1,16,128,256]{3,2,1,0:T(8,128)(2,1)} %fusion.101) | data formatting | bytes 2097152 | tf_op jit(solution)/shard_map/optimization_barrier | solution.py:139
  31.2 4.2 %all-to-all-start = ((bf16[1,16,128,256]{3,1,0,2:T(8,128)(2,1)}), bf16[1,16,128,256]{3,1,0,2:T(8,128)(2,1)S(1)}, u32[]{:S(2)}, u32[]{:S(2)}) async-start(bf16[1,16,128,256]{3,1,0,2:T(8,128)(2,1)} %copy.26), calls=%async_computation | async-start | bytes 2097152 | tf_op jit(solution)/shard_map/all_to_all | solution.py:140
  35.5 14.4 %all-to-all-done = bf16[1,16,128,256]{3,1,0,2:T(8,128)(2,1)S(1)} async-done(((bf16[1,16,128,256]{3,1,0,2:T(8,128)(2,1)}), bf16[1,16,128,256]{3,1,0,2:T(8,128)(2,1)S(1)}, u32[]{:S(2)}, u32[]{:S(2)}) %all-to-all-start) | async-done | bytes 1048608 | tf_op jit(solution)/shard_map/all_to_all | solution.py:140
  51.0 17.4 %fusion.272 = bf16[1,64,32,256]{3,2,0,1:T(8,128)(2,1)} fusion(f32[1,64,32,256]{3,2,1,0:T(8,128)S(1)} %bitcast.277, f32[256]{0:T(256)S(1)} %bitcast.497, f32[256]{0:T(256)S(1)} %bitcast.499, f32[256]{0:T(256)S(1)} %bitcast.375, f32[256]{0:T(256)S(1)} %bitcast.377, f32[256]{0:T(256)S(1)} %bitcast.379, f32[256]{0:T(256)S(1)} %bitcast.381, ...), kind=kLoop, calls=%fused_computation.643 | loop fusion | flops 53477376 | bytes 3197952 | tf_op jit(solution)/shard_map/convert_element_type | solution.py:142
  68.4 4.4 %all-to-all-start.1 = ((bf16[1,64,32,256]{3,2,0,1:T(8,128)(2,1)}), bf16[1,64,32,256]{3,2,0,1:T(8,128)(2,1)}, u32[]{:S(2)}, u32[]{:S(2)}) async-start(bf16[1,64,32,256]{3,2,0,1:T(8,128)(2,1)} %fusion.272), calls=%async_computation.1 | async-start | bytes 2097152 | tf_op jit(solution)/shard_map/all_to_all | solution.py:143
  74.3 12.8 %all-to-all-done.1 = bf16[1,64,32,256]{3,2,0,1:T(8,128)(2,1)} async-done(((bf16[1,64,32,256]{3,2,0,1:T(8,128)(2,1)}), bf16[1,64,32,256]{3,2,0,1:T(8,128)(2,1)}, u32[]{:S(2)}, u32[]{:S(2)}) %all-to-all-start.1) | async-done | bytes 1048608 | tf_op jit(solution)/shard_map/all_to_all | solution.py:143
  90.3 3.7 %multiply_convert_fusion = (bf16[2048,1024]{1,0:T(8,128)(2,1)S(1)}, f32[2048,1024]{1,0:T(8,128)S(1)}) fusion(f32[1024]{0:T(1024)S(1)} %copy-done.15, bf16[2048,256]{1,0:T(8,128)(2,1)S(1)} %add_convert_fusion, bf16[256,1024]{1,0:T(8,128)(2,1)S(1)} %copy-done), kind=kOutput, calls=%fused_computation.209 | convolution fusion | flops 1094713344 | bytes 14159872 | tf_op jit(solution)/shard_map/dot_general | solution.py:78
  94.1 2.6 %fusion.262 = (f32[256]{0:T(256)S(1)}, bf16[2048,256]{1,0:T(8,128)(2,1)}, bf16[2048,256]{1,0:T(8,128)(2,1)S(1)}) fusion(bf16[1,16,128,256]{3,2,1,0:T(8,128)(2,1)S(1)} %copy-done.6, f32[256]{0:T(256)S(1)} %copy-done.13, bf16[1,16,128,256]{3,2,1,0:T(8,128)(2,1)S(1)} %copy-done.2, f32[256]{0:T(256)S(1)} %copy-done.16, ...), kind=kOutput, calls=%fused_computation.571 | convolution fusion | flops 1078984448 | bytes 8915968 | tf_op jit(solution)/shard_map/dot_general | solution.py:80
  96.7 2.3 convolution_multiply_fusion
  99.0 6.4 %fusion.283 = (f32[1024]{0:T(1024)S(1)}, bf16[2048,1024]{1,0:T(8,128)(2,1)S(1)}) fusion(f32[2048,1024]{1,0:T(8,128)S(1)} %get-tuple-element.244, f32[1024]{0:T(1024)S(1)} %copy-done.15, bf16[2048,256]{1,0:T(8,128)(2,1)S(1)} %get-tuple-element.132, bf16[1024,256]{1,0:T(8,128)(2,1)S(1)} %copy-done.14), kind=kOutput, calls=%fused_computation.665 | convolution fusion | flops 1117780992 | bytes 14163968 | tf_op jit(solution)/shard_map/dot_general | solution.py:85
  105.4 1.9 multiply_reduce_fusion
  108.6 1.6 copy.31
  110.2 4.3 %all-to-all-start.2 = ((bf16[1,16,128,256]{3,1,0,2:T(8,128)(2,1)}), bf16[1,16,128,256]{3,1,0,2:T(8,128)(2,1)}, u32[]{:S(2)}, u32[]{:S(2)}) async-start(bf16[1,16,128,256]{3,1,0,2:T(8,128)(2,1)} %copy.31), calls=%async_computation.2 | async-start | bytes 2097152 | tf_op jit(solution)/shard_map/all_to_all | solution.py:161
  114.7 4.8 %fusion.269 = f32[256,1024]{1,0:T(8,128)} fusion(bf16[2048,256]{1,0:T(8,128)(2,1)} %copy-done.8, bf16[2048,1024]{1,0:T(8,128)(2,1)} %copy-done.17), kind=kOutput, calls=%fused_computation.638 | convolution fusion | flops 1074003968 | bytes 6291456 | tf_op jit(solution)/shard_map/dot_general | solution.py:109
  119.6 9.3 %all-to-all-done.2 = bf16[1,16,128,256]{3,1,0,2:T(8,128)(2,1)} async-done(((bf16[1,16,128,256]{3,1,0,2:T(8,128)(2,1)}), bf16[1,16,128,256]{3,1,0,2:T(8,128)(2,1)}, u32[]{:S(2)}, u32[]{:S(2)}) %all-to-all-start.2) | async-done | bytes 1048608 | tf_op jit(solution)/shard_map/all_to_all | solution.py:161
  128.9 1.6 copy_convert_fusion
  130.7 17.4 %fusion.273 = bf16[1,64,32,256]{3,2,0,1:T(8,128)(2,1)} fusion(f32[1,64,32,256]{3,2,1,0:T(8,128)S(1)} %bitcast.281, f32[256]{0:T(256)S(1)} %bitcast.374, f32[256]{0:T(256)S(1)} %bitcast.412, f32[256]{0:T(256)S(1)} %bitcast.476, f32[256]{0:T(256)S(1)} %bitcast.496, f32[256]{0:T(256)S(1)} %bitcast.494, f32[256]{0:T(256)S(1)} %bitcast.492, ...), kind=kLoop, calls=%fused_computation.644 | loop fusion | flops 53477376 | bytes 3197952 | tf_op jit(solution)/shard_map/convert_element_type | solution.py:166
  148.0 4.1 %multiply_reduce_fusion.1 = (f32[256]{0:T(256)S(1)}, f32[256]{0:T(256)S(1)}, f32[256]{0:T(256)S(1)}, f32[256]{0:T(256)S(1)}, f32[256]{0:T(256)S(1)}, /*index=5*/...) fusion(f32[1,64,32,256]{3,2,1,0:T(8,128)S(1)} %bitcast.282, ...), kind=kLoop, calls=%fused_computation.577 | loop fusion | flops 18869760 | bytes 4212736 | tf_op jit(solution)/shard_map/reduce_sum | solution.py:49
  152.2 4.9 %multiply_reduce_fusion.19 = (f32[256]{0:T(256)S(1)}, f32[256]{0:T(256)S(1)}, f32[256]{0:T(256)S(1)}, f32[256]{0:T(256)S(1)}, f32[256]{0:T(256)S(1)}, /*index=5*...) fusion(f32[1,64,32,256]{3,2,1,0:T(8,128)S(1)} %bitcast.283, ...), kind=kLoop, calls=%fused_computation.595 | loop fusion | flops 18869760 | bytes 4212736 | tf_op jit(solution)/shard_map/reduce_sum | solution.py:49
  157.1 4.5 %all-to-all-start.3 = ((bf16[1,64,32,256]{3,2,0,1:T(8,128)(2,1)}), bf16[1,64,32,256]{3,2,0,1:T(8,128)(2,1)}, u32[]{:S(2)}, u32[]{:S(2)}) async-start(bf16[1,64,32,256]{3,2,0,1:T(8,128)(2,1)} %fusion.273), calls=%async_computation.3 | async-start | bytes 2097152 | tf_op jit(solution)/shard_map/all_to_all | solution.py:167
  161.6 9.8 %multiply_reduce_fusion.38 = (f32[256]{0:T(256)S(1)}, f32[256]{0:T(256)S(1)}, f32[256]{0:T(256)S(1)}, f32[256]{0:T(256)S(1)}, f32[256]{0:T(256)S(1)}, /*index=5*...) fusion(f32[1,64,32,256]{3,2,1,0:T(8,128)} %bitcast.284, ...), kind=kLoop, calls=%fused_computation.614 | loop fusion | flops 14676480 | bytes 4208640 | tf_op jit(solution)/shard_map/reduce_sum | solution.py:49
  171.5 2.1 multiply_reduce_fusion.26
  173.8 2.0 all-to-all-done.3
  177.2 4.8 %fusion.157 = (f32[256]{0:T(256)S(1)}, f32[256]{0:T(256)S(1)}, f32[256]{0:T(256)S(1)}, f32[256]{0:T(256)S(1)}, f32[256]{0:T(256)S(1)}, /*index=5*/f32[256]{0:T(2...) fusion(bf16[1,16,128,256]{3,2,1,0:T(8,128)(2,1)S(1)} %bitcast.2, ...), kind=kLoop, calls=%fused_computation.462 | loop fusion | flops 28831232 | bytes 2115584 | tf_op jit(solution)/shard_map/reduce_sum | solution.py:49
  182.0 5.1 %fusion.156 = (f32[256]{0:T(256)S(1)}, f32[256]{0:T(256)S(1)}, f32[256]{0:T(256)S(1)}, f32[256]{0:T(256)S(1)}, f32[256]{0:T(256)S(1)}, /*index=5*/f32[256]{0:T(2...) fusion(bf16[1,16,128,256]{3,2,1,0:T(8,128)(2,1)S(1)} %bitcast.2, ...), kind=kLoop, calls=%fused_computation.461 | loop fusion | flops 28831232 | bytes 2115584 | tf_op jit(solution)/shard_map/reduce_sum | solution.py:49
  187.1 4.2 %fusion.155 = (f32[256]{0:T(256)S(1)}, f32[256]{0:T(256)S(1)}, f32[256]{0:T(256)S(1)}, f32[256]{0:T(256)S(1)}, f32[256]{0:T(256)S(1)}, /*index=5*/f32[256]{0:T(2...) fusion(bf16[1,16,128,256]{3,2,1,0:T(8,128)(2,1)S(1)} %bitcast.2, ...), kind=kLoop, calls=%fused_computation.460 | loop fusion | flops 24113408 | bytes 2112512 | tf_op jit(solution)/shard_map/reduce_sum | solution.py:49
  192.4 6.7 %all-to-all-start.4 = ((f32[16,14,128]{2,1,0:T(8,128)}), f32[16,14,128]{2,1,0:T(8,128)S(1)}, u32[]{:S(2)}, u32[]{:S(2)}) async-start(f32[16,14,128]{2,1,0:T(8,128)} %reshape.796), calls=%async_computation.4 | async-start | bytes 262144 | tf_op jit(solution)/shard_map/all_to_all | solution.py:210
  199.0 16.5 %fusion.260 = bf16[1,16,128,256]{3,2,1,0:T(8,128)(2,1)} fusion(bf16[1,16,128,256]{3,2,1,0:T(8,128)(2,1)S(1)} %copy-done.7, bf16[1,16,128,256]{3,2,1,0:T(8,128)(2,1)S(1)} %bitcast.288, f32[256]{0:T(256)S(1)} %bitcast.472, f32[256]{0:T(256)S(1)} %bitcast.474, f32[256]{0:T(256)S(1)} %bitcast.338, f32[256]{0:T(256)S(1)} %bitcast.340, f32[256]{0:T(256)S(1)} %bitcast.342, ...), kind=kLoop, calls=%fused_computation.569 | loop fusion | flops 81264640 | bytes 3197952 | tf_op jit(solution)/shard_map/convert_element_type | solution.py:174
  216.3 6.0 %all-to-all-start.5 = ((f32[16,14,128]{2,1,0:T(8,128)}), f32[16,14,128]{2,1,0:T(8,128)S(1)}, u32[]{:S(2)}, u32[]{:S(2)}) async-start(f32[16,14,128]{2,1,0:T(8,128)} %broadcast_in_dim.8), calls=%async_computation.5 | async-start | bytes 262144 | tf_op jit(solution)/shard_map/all_to_all | solution.py:213
  222.3 7.3 %all-to-all-done.5 = f32[16,14,128]{2,1,0:T(8,128)S(1)} async-done(((f32[16,14,128]{2,1,0:T(8,128)}), f32[16,14,128]{2,1,0:T(8,128)S(1)}, u32[]{:S(2)}, u32[]{:S(2)}) %all-to-all-start.5) | async-done | bytes 114720 | tf_op jit(solution)/shard_map/all_to_all | solution.py:213
  231.5 2.3 copy.44
  (80 shorter events, 18.1 us)
Async XLA Ops:
  7.2 83.0 %copy-start = (bf16[256,1024]{1,0:T(8,128)(2,1)S(1)}, bf16[256,1024]{1,0:T(8,128)(2,1)}, u32[]{:S(2)}) copy-start(bf16[256,1024]{1,0:T(8,128)(2,1)} %param.17) | copy-start | bytes 1572868
  28.4 7.0 %copy-start.10 = (f32[51,256]{1,0:T(8,128)S(1)}, f32[51,256]{1,0:T(8,128)}, u32[]{:S(2)}) copy-start(f32[51,256]{1,0:T(8,128)} %param.14) | copy-start | bytes 156676
  31.2 18.7 %all-to-all-start = ((bf16[1,16,128,256]{3,1,0,2:T(8,128)(2,1)}), bf16[1,16,128,256]{3,1,0,2:T(8,128)(2,1)S(1)}, u32[]{:S(2)}, u32[]{:S(2)}) async-start(bf16[1,16,128,256]{3,1,0,2:T(8,128)(2,1)} %copy.26), calls=%async_computation | async-start | bytes 2097152 | tf_op jit(solution)/shard_map/all_to_all | solution.py:140
  49.9 1.0 copy-start.4
  51.0 21.8 %copy-start.13 = (f32[256]{0:T(256)S(1)}, f32[256]{0:T(256)}, u32[]{:S(2)}) copy-start(f32[256]{0:T(256)} %param.21) | copy-start | bytes 3076
  68.4 18.7 %all-to-all-start.1 = ((bf16[1,64,32,256]{3,2,0,1:T(8,128)(2,1)}), bf16[1,64,32,256]{3,2,0,1:T(8,128)(2,1)}, u32[]{:S(2)}, u32[]{:S(2)}) async-start(bf16[1,64,32,256]{3,2,0,1:T(8,128)(2,1)} %fusion.272), calls=%async_computation.1 | async-start | bytes 2097152 | tf_op jit(solution)/shard_map/all_to_all | solution.py:143
  87.1 2.4 copy-start.11
  87.1 2.4 copy-start.12
  88.4 1.8 copy-start.15
  90.2 3.8 %copy-start.8 = (bf16[2048,256]{1,0:T(8,128)(2,1)}, bf16[2048,256]{1,0:T(8,128)(2,1)S(1)}, u32[]{:S(2)}) copy-start(bf16[2048,256]{1,0:T(8,128)(2,1)S(1)} %add_convert_fusion) | copy-start | bytes 3145732
  90.3 3.8 %copy-start.2 = (bf16[1,16,128,256]{3,2,1,0:T(8,128)(2,1)S(1)}, bf16[1,16,128,256]{3,2,1,0:T(8,128)(2,1)}, u32[]{:S(2)}) copy-start(bf16[1,16,128,256]{3,2,1,0:T(8,128)(2,1)} %param.11) | copy-start | bytes 3145732
  90.3 3.8 %copy-start.6 = (bf16[1,16,128,256]{3,2,1,0:T(8,128)(2,1)S(1)}, bf16[1,16,128,256]{3,2,1,0:T(8,128)(2,1)}, u32[]{:S(2)}) copy-start(bf16[1,16,128,256]{3,2,1,0:T(8,128)(2,1)} %param.12) | copy-start | bytes 3145732
  90.3 3.8 %copy-start.14 = (bf16[1024,256]{1,0:T(8,128)(2,1)S(1)}, bf16[1024,256]{1,0:T(8,128)(2,1)}, u32[]{:S(2)}) copy-start(bf16[1024,256]{1,0:T(8,128)(2,1)} %param.19) | copy-start | bytes 1572868
  90.3 3.8 %copy-start.16 = (f32[256]{0:T(256)S(1)}, f32[256]{0:T(256)}, u32[]{:S(2)}) copy-start(f32[256]{0:T(256)} %param.20) | copy-start | bytes 3076
  105.4 2.0 copy-start.17
  110.2 18.8 %all-to-all-start.2 = ((bf16[1,16,128,256]{3,1,0,2:T(8,128)(2,1)}), bf16[1,16,128,256]{3,1,0,2:T(8,128)(2,1)}, u32[]{:S(2)}, u32[]{:S(2)}) async-start(bf16[1,16,128,256]{3,1,0,2:T(8,128)(2,1)} %copy.31), calls=%async_computation.2 | async-start | bytes 2097152 | tf_op jit(solution)/shard_map/all_to_all | solution.py:161
  114.4 107.9 %all-reduce.9.cloned.1.call-start = ((), (), s32[]{:S(2)}) async-start(), calls=%async_computation.6 | async-start | bytes 4194304 | tf_op jit(solution)/shard_map/psum | solution.py:176
  130.6 21.5 %copy-start.1 = (f32[1,4,16,32,256]{4,3,2,1,0:T(8,128)}, f32[1,4,16,32,256]{4,3,2,1,0:T(8,128)S(1)}, u32[]{:S(2)}) copy-start(f32[1,4,16,32,256]{4,3,2,1,0:T(8,128)S(1)} %copy.33) | copy-start | bytes 6291460
  157.1 18.8 %all-to-all-start.3 = ((bf16[1,64,32,256]{3,2,0,1:T(8,128)(2,1)}), bf16[1,64,32,256]{3,2,0,1:T(8,128)(2,1)}, u32[]{:S(2)}, u32[]{:S(2)}) async-start(bf16[1,64,32,256]{3,2,0,1:T(8,128)(2,1)} %fusion.273), calls=%async_computation.3 | async-start | bytes 2097152 | tf_op jit(solution)/shard_map/all_to_all | solution.py:167
  161.6 9.9 %copy-start.5 = (bf16[1,16,128,256]{3,1,0,2:T(8,128)(2,1)S(1)}, bf16[1,16,128,256]{3,1,0,2:T(8,128)(2,1)}, u32[]{:S(2)}) copy-start(bf16[1,16,128,256]{3,1,0,2:T(8,128)(2,1)} %copy-done.4) | copy-start | bytes 3145732
  171.5 5.7 %copy-start.3 = (bf16[1,16,128,256]{3,2,1,0:T(8,128)(2,1)S(1)}, bf16[1,16,128,256]{3,2,1,0:T(8,128)(2,1)}, u32[]{:S(2)}) copy-start(bf16[1,16,128,256]{3,2,1,0:T(8,128)(2,1)} %param.11) | copy-start | bytes 3145732
  191.3 7.8 %copy-start.7 = (bf16[1,16,128,256]{3,2,1,0:T(8,128)(2,1)S(1)}, bf16[1,16,128,256]{3,2,1,0:T(8,128)(2,1)}, u32[]{:S(2)}) copy-start(bf16[1,16,128,256]{3,2,1,0:T(8,128)(2,1)} %param.12) | copy-start | bytes 3145732
  192.4 23.2 %all-to-all-start.4 = ((f32[16,14,128]{2,1,0:T(8,128)}), f32[16,14,128]{2,1,0:T(8,128)S(1)}, u32[]{:S(2)}, u32[]{:S(2)}) async-start(f32[16,14,128]{2,1,0:T(8,128)} %reshape.796), calls=%async_computation.4 | async-start | bytes 262144 | tf_op jit(solution)/shard_map/all_to_all | solution.py:210
  216.3 13.4 %all-to-all-start.5 = ((f32[16,14,128]{2,1,0:T(8,128)}), f32[16,14,128]{2,1,0:T(8,128)S(1)}, u32[]{:S(2)}, u32[]{:S(2)}) async-start(f32[16,14,128]{2,1,0:T(8,128)} %broadcast_in_dim.8), calls=%async_computation.5 | async-start | bytes 262144 | tf_op jit(solution)/shard_map/all_to_all | solution.py:213
  222.3 11.5 %copy-start.9 = (f32[256,1024]{1,0:T(8,128)S(1)}, f32[256,1024]{1,0:T(8,128)}, u32[]{:S(2)}) copy-start(f32[256,1024]{1,0:T(8,128)} %get-tuple-element.264) | copy-start | bytes 3145732
Sparse Core Ops, SparseCore 0:
  119.7 101.7 all-reduce.8

commit v8 on v7

--- a/solution.py
+++ b/solution.py
@@ -115,6 +115,14 @@
     return (block_rows, grad_rows, partials)
 
 
+def to_columns(band):
+    count = lax.axis_size("rows")
+    tiles, rows, width, chans = band.shape
+    split = band.reshape(tiles, rows, count, width // count, chans).transpose(2, 0, 1, 3, 4)
+    split = lax.all_to_all(split, "rows", 0, 0, tiled=True)
+    return split.transpose(1, 0, 2, 3, 4).reshape(tiles, count * rows, width // count, chans)
+
+
 def per_device(
     images,
     cotangent,
@@ -137,7 +145,7 @@
     image_padded = pad_along(images.astype(jnp.float32), 2, half_reach)
     row_mix = slide_padded(image_padded, row_taps, 2, columns).astype(jnp.bfloat16)
     row_mix = lax.optimization_barrier(row_mix)
-    mix_columns = lax.all_to_all(row_mix, "rows", split_axis=2, concat_axis=1, tiled=True)
+    mix_columns = to_columns(row_mix)
     mix_padded = pad_along(mix_columns.astype(jnp.float32), 1, half_reach)
     col_local = slide_padded(mix_padded, col_taps, 1, mix_columns.shape[1]).astype(jnp.bfloat16)
     col_mix = lax.all_to_all(col_local, "rows", split_axis=1, concat_axis=2, tiled=True)
@@ -158,7 +166,7 @@
     block_out = block_rows.reshape(images.shape)
     grad_rows = lax.optimization_barrier(grad_rows)
     col_grad = grad_rows.reshape(images.shape)
-    grad_columns = lax.all_to_all(col_grad, "rows", split_axis=2, concat_axis=1, tiled=True)
+    grad_columns = to_columns(col_grad)
     grad_float = grad_columns.astype(jnp.float32)
     col_part = tap_sums(grad_float, mix_padded, taps_count, 1)
     row_local = slide_padded(

time: 243 us -> 242 us (level)
    optimization_barrier x1 -> x0, local copies, waits for them, and re-layouts: 2.78 us -> none  [per_device(): row_mix = lax.optimization_barrier(row_mix)]
where the time goes in v8:
time: 242 us
  other arithmetic  111 us (46%)
  waiting for transfers between devices  47.6 us (20%)
  starting transfers between devices  30.4 us (13%)
  matrix products  21.7 us (9%)
  local copies, waits for them, and re-layouts  16.3 us (7%)
  between operations  14.6 us (6%)
    reduce_sum x7, other arithmetic, tap_sums(): jnp.sum(cot_field.astype(jnp.float32) * lax.slice_in_dim(padded, offset,...  34 us
    all_to_all x2, waiting for transfers between devices, to_columns(): split = lax.all_to_all(split, 'rows', 0, 0, tiled=True)  24.5 us
    convert_element_type x1, other arithmetic, per_device(): row_local = slide_padded(pad_along(grad_float, 1, half_reach), col_taps[:...  17.4 us
    convert_element_type x1, other arithmetic, per_device(): slide_padded(mix_padded, col_taps, 1, mix_columns.shape[1])  17.4 us
    convert_element_type x1, other arithmetic, per_device(): slide_padded(image_padded, row_taps, 2, columns).astype(jnp.bfloat16)  16.8 us
    convert_element_type x1, other arithmetic, per_device(): image_grad = (cotangent.astype(jnp.float32) + slide_padded(pad_along(row_...  16.5 us
    all_to_all x1, waiting for transfers between devices, per_device(): lax.all_to_all(col_local, 'rows', split_axis=1, concat_axis=2, tiled=True)  12.8 us
    all_to_all x2, starting transfers between devices, to_columns(): split = lax.all_to_all(split, 'rows', 0, 0, tiled=True)  8.49 us
  transfers between devices with their start and end apart: 7, of which 5 were waited for; matrix products, arithmetic and copies ran while one was open for 33% of the time, Pallas kernels for 0%

profile of v8, /device:TPU:0, one launch (start us, length us, event | category | flops | bytes accessed | tf_op | source)
XLA Modules:
  0.0 241.5 jit_solution(3152138587347678176)
XLA Ops:
  11.7 16.8 %fusion.101 = bf16[1,16,128,256]{3,2,1,0:T(8,128)(2,1)} fusion(f32[1,16,128,256]{3,2,1,0:T(8,128)S(1)} %convert_element_type.597, f32[256]{0:T(256)S(1)} %bitcast.479, f32[256]{0:T(256)S(1)} %bitcast.481, f32[256]{0:T(256)S(1)} %bitcast.345, f32[256]{0:T(256)S(1)} %bitcast.347, f32[256]{0:T(256)S(1)} %bitcast.349, f32[256]{0:T(256)S(1)} %bitcast.351, ...), kind=kLoop, calls=%fused_computation.406 | loop fusion | flops 53477376 | bytes 3197952 | tf_op jit(solution)/shard_map/convert_element_type | solution.py:146
  28.4 2.3 copy.27
  30.7 4.2 %all-to-all-start = ((bf16[4,1,16,32,256]{4,3,2,1,0:T(8,128)(2,1)}), bf16[4,1,16,32,256]{4,3,2,1,0:T(8,128)(2,1)}, u32[]{:S(2)}, u32[]{:S(2)}) async-start(bf16[4,1,16,32,256]{4,3,2,1,0:T(8,128)(2,1)} %copy.27), calls=%async_computation | async-start | bytes 2097152 | tf_op jit(solution)/shard_map/all_to_all | solution.py:122
  35.0 15.1 %all-to-all-done = bf16[4,1,16,32,256]{4,3,2,1,0:T(8,128)(2,1)} async-done(((bf16[4,1,16,32,256]{4,3,2,1,0:T(8,128)(2,1)}), bf16[4,1,16,32,256]{4,3,2,1,0:T(8,128)(2,1)}, u32[]{:S(2)}, u32[]{:S(2)}) %all-to-all-start) | async-done | bytes 1048608 | tf_op jit(solution)/shard_map/all_to_all | solution.py:122
  51.6 17.4 %fusion.272 = bf16[1,64,32,256]{3,2,0,1:T(8,128)(2,1)} fusion(f32[1,64,32,256]{3,2,1,0:T(8,128)S(1)} %bitcast.285, f32[256]{0:T(256)S(1)} %bitcast.505, f32[256]{0:T(256)S(1)} %bitcast.507, f32[256]{0:T(256)S(1)} %bitcast.383, f32[256]{0:T(256)S(1)} %bitcast.385, f32[256]{0:T(256)S(1)} %bitcast.387, f32[256]{0:T(256)S(1)} %bitcast.389, ...), kind=kLoop, calls=%fused_computation.644 | loop fusion | flops 53477376 | bytes 3197952 | tf_op jit(solution)/shard_map/convert_element_type | solution.py:150
  69.0 4.4 %all-to-all-start.1 = ((bf16[1,64,32,256]{3,2,0,1:T(8,128)(2,1)}), bf16[1,64,32,256]{3,2,0,1:T(8,128)(2,1)}, u32[]{:S(2)}, u32[]{:S(2)}) async-start(bf16[1,64,32,256]{3,2,0,1:T(8,128)(2,1)} %fusion.272), calls=%async_computation.1 | async-start | bytes 2097152 | tf_op jit(solution)/shard_map/all_to_all | solution.py:151
  73.4 1.5 fusion.259
  75.0 12.8 %all-to-all-done.1 = bf16[1,64,32,256]{3,2,0,1:T(8,128)(2,1)} async-done(((bf16[1,64,32,256]{3,2,0,1:T(8,128)(2,1)}), bf16[1,64,32,256]{3,2,0,1:T(8,128)(2,1)}, u32[]{:S(2)}, u32[]{:S(2)}) %all-to-all-start.1) | async-done | bytes 1048608 | tf_op jit(solution)/shard_map/all_to_all | solution.py:151
  91.0 3.7 %multiply_convert_fusion = (bf16[2048,1024]{1,0:T(8,128)(2,1)S(1)}, f32[2048,1024]{1,0:T(8,128)S(1)}) fusion(f32[1024]{0:T(1024)S(1)} %copy-done.14, bf16[2048,256]{1,0:T(8,128)(2,1)S(1)} %add_convert_fusion, bf16[256,1024]{1,0:T(8,128)(2,1)S(1)} %copy-done), kind=kOutput, calls=%fused_computation.209 | convolution fusion | flops 1094713344 | bytes 14159872 | tf_op jit(solution)/shard_map/dot_general | solution.py:78
  94.7 2.6 %fusion.262 = (f32[256]{0:T(256)S(1)}, bf16[2048,256]{1,0:T(8,128)(2,1)}, bf16[2048,256]{1,0:T(8,128)(2,1)S(1)}) fusion(bf16[1,16,128,256]{3,2,1,0:T(8,128)(2,1)S(1)} %copy-done.5, f32[256]{0:T(256)S(1)} %copy-done.12, bf16[1,16,128,256]{3,2,1,0:T(8,128)(2,1)S(1)} %copy-done.3, f32[256]{0:T(256)S(1)} %copy-done.15, ...), kind=kOutput, calls=%fused_computation.571 | convolution fusion | flops 1078984448 | bytes 8915968 | tf_op jit(solution)/shard_map/dot_general | solution.py:80
  97.4 2.3 convolution_multiply_fusion
  99.6 6.4 %fusion.283 = (f32[1024]{0:T(1024)S(1)}, bf16[2048,1024]{1,0:T(8,128)(2,1)S(1)}) fusion(f32[2048,1024]{1,0:T(8,128)S(1)} %get-tuple-element.244, f32[1024]{0:T(1024)S(1)} %copy-done.14, bf16[2048,256]{1,0:T(8,128)(2,1)S(1)} %get-tuple-element.132, bf16[1024,256]{1,0:T(8,128)(2,1)S(1)} %copy-done.13), kind=kOutput, calls=%fused_computation.666 | convolution fusion | flops 1117780992 | bytes 14163968 | tf_op jit(solution)/shard_map/dot_general | solution.py:85
  106.0 1.9 multiply_reduce_fusion
  110.3 4.3 %all-to-all-start.2 = ((bf16[4,1,16,32,256]{4,3,2,1,0:T(8,128)(2,1)}), bf16[4,1,16,32,256]{4,3,2,1,0:T(8,128)(2,1)}, u32[]{:S(2)}, u32[]{:S(2)}) async-start(bf16[4,1,16,32,256]{4,3,2,1,0:T(8,128)(2,1)} %bitcast.304), calls=%async_computation.2 | async-start | bytes 2097152 | tf_op jit(solution)/shard_map/all_to_all | solution.py:122
  114.8 4.8 %fusion.269 = f32[256,1024]{1,0:T(8,128)} fusion(bf16[2048,256]{1,0:T(8,128)(2,1)} %copy-done.7, bf16[2048,1024]{1,0:T(8,128)(2,1)} %copy-done.16), kind=kOutput, calls=%fused_computation.638 | convolution fusion | flops 1074003968 | bytes 6291456 | tf_op jit(solution)/shard_map/dot_general | solution.py:109
  119.7 9.4 %all-to-all-done.2 = bf16[4,1,16,32,256]{4,3,2,1,0:T(8,128)(2,1)} async-done(((bf16[4,1,16,32,256]{4,3,2,1,0:T(8,128)(2,1)}), bf16[4,1,16,32,256]{4,3,2,1,0:T(8,128)(2,1)}, u32[]{:S(2)}, u32[]{:S(2)}) %all-to-all-start.2) | async-done | bytes 1048608 | tf_op jit(solution)/shard_map/all_to_all | solution.py:122
  129.1 1.5 bitcast_convert_fusion
  130.6 17.4 %fusion.273 = bf16[1,64,32,256]{3,2,0,1:T(8,128)(2,1)} fusion(f32[1,64,32,256]{3,2,1,0:T(8,128)S(1)} %bitcast.289, f32[256]{0:T(256)S(1)} %bitcast.382, f32[256]{0:T(256)S(1)} %bitcast.420, f32[256]{0:T(256)S(1)} %bitcast.484, f32[256]{0:T(256)S(1)} %bitcast.504, f32[256]{0:T(256)S(1)} %bitcast.502, f32[256]{0:T(256)S(1)} %bitcast.500, ...), kind=kLoop, calls=%fused_computation.645 | loop fusion | flops 53477376 | bytes 3197952 | tf_op jit(solution)/shard_map/convert_element_type | solution.py:174
  147.9 4.1 %multiply_reduce_fusion.1 = (f32[256]{0:T(256)S(1)}, f32[256]{0:T(256)S(1)}, f32[256]{0:T(256)S(1)}, f32[256]{0:T(256)S(1)}, f32[256]{0:T(256)S(1)}, /*index=5*/...) fusion(f32[1,64,32,256]{3,2,1,0:T(8,128)S(1)} %bitcast.290, ...), kind=kLoop, calls=%fused_computation.577 | loop fusion | flops 18869760 | bytes 4212736 | tf_op jit(solution)/shard_map/reduce_sum | solution.py:49
  152.1 4.9 %multiply_reduce_fusion.19 = (f32[256]{0:T(256)S(1)}, f32[256]{0:T(256)S(1)}, f32[256]{0:T(256)S(1)}, f32[256]{0:T(256)S(1)}, f32[256]{0:T(256)S(1)}, /*index=5*...) fusion(f32[1,64,32,256]{3,2,1,0:T(8,128)S(1)} %bitcast.291, ...), kind=kLoop, calls=%fused_computation.595 | loop fusion | flops 18869760 | bytes 4212736 | tf_op jit(solution)/shard_map/reduce_sum | solution.py:49
  157.0 4.5 %all-to-all-start.3 = ((bf16[1,64,32,256]{3,2,0,1:T(8,128)(2,1)}), bf16[1,64,32,256]{3,2,0,1:T(8,128)(2,1)}, u32[]{:S(2)}, u32[]{:S(2)}) async-start(bf16[1,64,32,256]{3,2,0,1:T(8,128)(2,1)} %fusion.273), calls=%async_computation.3 | async-start | bytes 2097152 | tf_op jit(solution)/shard_map/all_to_all | solution.py:175
  161.5 2.1 multiply_reduce_fusion.26
  163.7 8.8 %multiply_reduce_fusion.38 = (f32[256]{0:T(256)S(1)}, f32[256]{0:T(256)S(1)}, f32[256]{0:T(256)S(1)}, f32[256]{0:T(256)S(1)}, f32[256]{0:T(256)S(1)}, /*index=5*...) fusion(f32[1,64,32,256]{3,2,1,0:T(8,128)S(1)} %bitcast.292, ...), kind=kLoop, calls=%fused_computation.614 | loop fusion | flops 14676480 | bytes 4208640 | tf_op jit(solution)/shard_map/reduce_sum | solution.py:49
  172.7 3.0 %all-to-all-done.3 = bf16[1,64,32,256]{3,2,0,1:T(8,128)(2,1)} async-done(((bf16[1,64,32,256]{3,2,0,1:T(8,128)(2,1)}), bf16[1,64,32,256]{3,2,0,1:T(8,128)(2,1)}, u32[]{:S(2)}, u32[]{:S(2)}) %all-to-all-start.3) | async-done | bytes 1048608 | tf_op jit(solution)/shard_map/all_to_all | solution.py:175
  177.1 4.8 %fusion.157 = (f32[256]{0:T(256)S(1)}, f32[256]{0:T(256)S(1)}, f32[256]{0:T(256)S(1)}, f32[256]{0:T(256)S(1)}, f32[256]{0:T(256)S(1)}, /*index=5*/f32[256]{0:T(2...) fusion(bf16[1,16,128,256]{3,2,1,0:T(8,128)(2,1)S(1)} %bitcast.2, ...), kind=kLoop, calls=%fused_computation.462 | loop fusion | flops 28831232 | bytes 2115584 | tf_op jit(solution)/shard_map/reduce_sum | solution.py:49
  181.9 5.1 %fusion.156 = (f32[256]{0:T(256)S(1)}, f32[256]{0:T(256)S(1)}, f32[256]{0:T(256)S(1)}, f32[256]{0:T(256)S(1)}, f32[256]{0:T(256)S(1)}, /*index=5*/f32[256]{0:T(2...) fusion(bf16[1,16,128,256]{3,2,1,0:T(8,128)(2,1)S(1)} %bitcast.2, ...), kind=kLoop, calls=%fused_computation.461 | loop fusion | flops 28831232 | bytes 2115584 | tf_op jit(solution)/shard_map/reduce_sum | solution.py:49
  187.0 4.2 %fusion.155 = (f32[256]{0:T(256)S(1)}, f32[256]{0:T(256)S(1)}, f32[256]{0:T(256)S(1)}, f32[256]{0:T(256)S(1)}, f32[256]{0:T(256)S(1)}, /*index=5*/f32[256]{0:T(2...) fusion(bf16[1,16,128,256]{3,2,1,0:T(8,128)(2,1)S(1)} %bitcast.2, ...), kind=kLoop, calls=%fused_computation.460 | loop fusion | flops 24113408 | bytes 2112512 | tf_op jit(solution)/shard_map/reduce_sum | solution.py:49
  192.3 6.7 %all-to-all-start.4 = ((f32[16,14,128]{2,1,0:T(8,128)}), f32[16,14,128]{2,1,0:T(8,128)S(1)}, u32[]{:S(2)}, u32[]{:S(2)}) async-start(f32[16,14,128]{2,1,0:T(8,128)} %reshape.789), calls=%async_computation.4 | async-start | bytes 262144 | tf_op jit(solution)/shard_map/all_to_all | solution.py:218
  199.0 16.5 %fusion.260 = bf16[1,16,128,256]{3,2,1,0:T(8,128)(2,1)} fusion(bf16[1,16,128,256]{3,2,1,0:T(8,128)(2,1)S(1)} %copy-done.6, bf16[1,16,128,256]{3,2,1,0:T(8,128)(2,1)S(1)} %bitcast.296, f32[256]{0:T(256)S(1)} %bitcast.480, f32[256]{0:T(256)S(1)} %bitcast.482, f32[256]{0:T(256)S(1)} %bitcast.346, f32[256]{0:T(256)S(1)} %bitcast.348, f32[256]{0:T(256)S(1)} %bitcast.350, ...), kind=kLoop, calls=%fused_computation.569 | loop fusion | flops 81264640 | bytes 3197952 | tf_op jit(solution)/shard_map/convert_element_type | solution.py:182
  216.2 6.0 %all-to-all-start.5 = ((f32[16,14,128]{2,1,0:T(8,128)}), f32[16,14,128]{2,1,0:T(8,128)S(1)}, u32[]{:S(2)}, u32[]{:S(2)}) async-start(f32[16,14,128]{2,1,0:T(8,128)} %broadcast_in_dim.8), calls=%async_computation.5 | async-start | bytes 262144 | tf_op jit(solution)/shard_map/all_to_all | solution.py:221
  222.2 7.3 %all-to-all-done.5 = f32[16,14,128]{2,1,0:T(8,128)S(1)} async-done(((f32[16,14,128]{2,1,0:T(8,128)}), f32[16,14,128]{2,1,0:T(8,128)S(1)}, u32[]{:S(2)}, u32[]{:S(2)}) %all-to-all-start.5) | async-done | bytes 114720 | tf_op jit(solution)/shard_map/all_to_all | solution.py:221
  231.4 2.3 copy.39
  (76 shorter events, 18.0 us)
Async XLA Ops:
  7.2 83.7 %copy-start = (bf16[256,1024]{1,0:T(8,128)(2,1)S(1)}, bf16[256,1024]{1,0:T(8,128)(2,1)}, u32[]{:S(2)}) copy-start(bf16[256,1024]{1,0:T(8,128)(2,1)} %param.17) | copy-start | bytes 1572868
  28.4 6.5 %copy-start.9 = (f32[51,256]{1,0:T(8,128)S(1)}, f32[51,256]{1,0:T(8,128)}, u32[]{:S(2)}) copy-start(f32[51,256]{1,0:T(8,128)} %param.14) | copy-start | bytes 156676
  30.7 19.4 %all-to-all-start = ((bf16[4,1,16,32,256]{4,3,2,1,0:T(8,128)(2,1)}), bf16[4,1,16,32,256]{4,3,2,1,0:T(8,128)(2,1)}, u32[]{:S(2)}, u32[]{:S(2)}) async-start(bf16[4,1,16,32,256]{4,3,2,1,0:T(8,128)(2,1)} %copy.27), calls=%async_computation | async-start | bytes 2097152 | tf_op jit(solution)/shard_map/all_to_all | solution.py:122
  51.6 21.8 %copy-start.12 = (f32[256]{0:T(256)S(1)}, f32[256]{0:T(256)}, u32[]{:S(2)}) copy-start(f32[256]{0:T(256)} %param.21) | copy-start | bytes 3076
  69.0 18.7 %all-to-all-start.1 = ((bf16[1,64,32,256]{3,2,0,1:T(8,128)(2,1)}), bf16[1,64,32,256]{3,2,0,1:T(8,128)(2,1)}, u32[]{:S(2)}, u32[]{:S(2)}) async-start(bf16[1,64,32,256]{3,2,0,1:T(8,128)(2,1)} %fusion.272), calls=%async_computation.1 | async-start | bytes 2097152 | tf_op jit(solution)/shard_map/all_to_all | solution.py:151
  87.7 2.4 copy-start.10
  87.7 2.4 copy-start.11
  89.1 1.8 copy-start.14
  90.9 3.8 %copy-start.7 = (bf16[2048,256]{1,0:T(8,128)(2,1)}, bf16[2048,256]{1,0:T(8,128)(2,1)S(1)}, u32[]{:S(2)}) copy-start(bf16[2048,256]{1,0:T(8,128)(2,1)S(1)} %add_convert_fusion) | copy-start | bytes 3145732
  90.9 3.8 %copy-start.3 = (bf16[1,16,128,256]{3,2,1,0:T(8,128)(2,1)S(1)}, bf16[1,16,128,256]{3,2,1,0:T(8,128)(2,1)}, u32[]{:S(2)}) copy-start(bf16[1,16,128,256]{3,2,1,0:T(8,128)(2,1)} %param.11) | copy-start | bytes 3145732
  90.9 3.8 %copy-start.5 = (bf16[1,16,128,256]{3,2,1,0:T(8,128)(2,1)S(1)}, bf16[1,16,128,256]{3,2,1,0:T(8,128)(2,1)}, u32[]{:S(2)}) copy-start(bf16[1,16,128,256]{3,2,1,0:T(8,128)(2,1)} %param.12) | copy-start | bytes 3145732
  90.9 3.8 %copy-start.13 = (bf16[1024,256]{1,0:T(8,128)(2,1)S(1)}, bf16[1024,256]{1,0:T(8,128)(2,1)}, u32[]{:S(2)}) copy-start(bf16[1024,256]{1,0:T(8,128)(2,1)} %param.19) | copy-start | bytes 1572868
  90.9 3.8 %copy-start.15 = (f32[256]{0:T(256)S(1)}, f32[256]{0:T(256)}, u32[]{:S(2)}) copy-start(f32[256]{0:T(256)} %param.20) | copy-start | bytes 3076
  106.0 1.9 copy-start.16
  110.3 18.8 %all-to-all-start.2 = ((bf16[4,1,16,32,256]{4,3,2,1,0:T(8,128)(2,1)}), bf16[4,1,16,32,256]{4,3,2,1,0:T(8,128)(2,1)}, u32[]{:S(2)}, u32[]{:S(2)}) async-start(bf16[4,1,16,32,256]{4,3,2,1,0:T(8,128)(2,1)} %bitcast.304), calls=%async_computation.2 | async-start | bytes 2097152 | tf_op jit(solution)/shard_map/all_to_all | solution.py:122
  114.6 107.6 %all-reduce.9.cloned.1.call-start = ((), (), s32[]{:S(2)}) async-start(), calls=%async_computation.6 | async-start | bytes 4194304 | tf_op jit(solution)/shard_map/psum | solution.py:184
  130.5 21.5 %copy-start.1 = (f32[4,1,16,32,256]{4,3,2,0,1:T(8,128)}, f32[4,1,16,32,256]{4,3,2,0,1:T(8,128)S(1)}, u32[]{:S(2)}) copy-start(f32[4,1,16,32,256]{4,3,2,0,1:T(8,128)S(1)} %bitcast_convert_fusion) | copy-start | bytes 6291460
  157.0 18.8 %all-to-all-start.3 = ((bf16[1,64,32,256]{3,2,0,1:T(8,128)(2,1)}), bf16[1,64,32,256]{3,2,0,1:T(8,128)(2,1)}, u32[]{:S(2)}, u32[]{:S(2)}) async-start(bf16[1,64,32,256]{3,2,0,1:T(8,128)(2,1)} %fusion.273), calls=%async_computation.3 | async-start | bytes 2097152 | tf_op jit(solution)/shard_map/all_to_all | solution.py:175
  161.5 2.2 copy-start.2
  172.5 4.5 %copy-start.4 = (bf16[1,16,128,256]{3,2,1,0:T(8,128)(2,1)S(1)}, bf16[1,16,128,256]{3,2,1,0:T(8,128)(2,1)}, u32[]{:S(2)}) copy-start(bf16[1,16,128,256]{3,2,1,0:T(8,128)(2,1)} %param.11) | copy-start | bytes 3145732
  191.2 7.8 %copy-start.6 = (bf16[1,16,128,256]{3,2,1,0:T(8,128)(2,1)S(1)}, bf16[1,16,128,256]{3,2,1,0:T(8,128)(2,1)}, u32[]{:S(2)}) copy-start(bf16[1,16,128,256]{3,2,1,0:T(8,128)(2,1)} %param.12) | copy-start | bytes 3145732
  192.3 23.2 %all-to-all-start.4 = ((f32[16,14,128]{2,1,0:T(8,128)}), f32[16,14,128]{2,1,0:T(8,128)S(1)}, u32[]{:S(2)}, u32[]{:S(2)}) async-start(f32[16,14,128]{2,1,0:T(8,128)} %reshape.789), calls=%async_computation.4 | async-start | bytes 262144 | tf_op jit(solution)/shard_map/all_to_all | solution.py:218
  216.2 13.4 %all-to-all-start.5 = ((f32[16,14,128]{2,1,0:T(8,128)}), f32[16,14,128]{2,1,0:T(8,128)S(1)}, u32[]{:S(2)}, u32[]{:S(2)}) async-start(f32[16,14,128]{2,1,0:T(8,128)} %broadcast_in_dim.8), calls=%async_computation.5 | async-start | bytes 262144 | tf_op jit(solution)/shard_map/all_to_all | solution.py:221
  222.2 11.5 %copy-start.8 = (f32[256,1024]{1,0:T(8,128)S(1)}, f32[256,1024]{1,0:T(8,128)}, u32[]{:S(2)}) copy-start(f32[256,1024]{1,0:T(8,128)} %get-tuple-element.264) | copy-start | bytes 3145732
Sparse Core Ops, SparseCore 0:
  119.8 102.1 all-reduce.8

commit v9 on v8

--- a/solution.py
+++ b/solution.py
@@ -147,8 +147,19 @@
     row_mix = lax.optimization_barrier(row_mix)
     mix_columns = to_columns(row_mix)
     mix_padded = pad_along(mix_columns.astype(jnp.float32), 1, half_reach)
-    col_local = slide_padded(mix_padded, col_taps, 1, mix_columns.shape[1]).astype(jnp.bfloat16)
-    col_mix = lax.all_to_all(col_local, "rows", split_axis=1, concat_axis=2, tiled=True)
+    strip = mix_columns.shape[2]
+    parts = 2 if strip % 16 == 0 else 1
+    step = strip // parts
+    pieces = []
+    for part in range(parts):
+        local = slide_padded(
+            mix_padded[:, :, part * step : (part + 1) * step], col_taps, 1, mix_columns.shape[1]
+        ).astype(jnp.bfloat16)
+        pieces.append(lax.all_to_all(local, "rows", split_axis=1, concat_axis=2, tiled=True))
+    count = lax.axis_size("rows")
+    col_mix = jnp.stack(
+        [piece.reshape(tiles_here, band_rows, count, step, channels) for piece in pieces], axis=3
+    ).reshape(images.shape)
     col_mix = lax.optimization_barrier(col_mix)
     block_rows, grad_rows, partials = pointwise(
         col_mix.reshape(-1, channels),

time: 242 us -> 241 us (level)
  waiting for transfers between devices: 47.6 us -> 40.8 us
  starting transfers between devices: 30.4 us -> 33.7 us
    all_to_all x1 -> x2, waiting for transfers between devices: 12.8 us -> 6.62 us  [per_device(): lax.all_to_all(local, 'rows', split_axis=1, concat_axis=2, tiled=True)]
    all_to_all x1 -> x2, starting transfers between devices: 4.42 us -> 7.78 us  [per_device(): lax.all_to_all(local, 'rows', split_axis=1, concat_axis=2, tiled=True)]
    convert_element_type x1 -> x2, other arithmetic: 17.4 us -> 18.1 us  [per_device(): local = slide_padded(mix_padded[:, :, part * step:(part + 1) * step], col...]
  transfers between devices with their start and end apart: 7 -> 8, of which waited for: 5 -> 5; matrix products, arithmetic and copies ran while one was open for 33% -> 37% of each run, Pallas kernels for 0% -> 0%
where the time goes in v9:
time: 241 us; the launch traced here: 240 us
  other arithmetic  113 us (47%)
  waiting for transfers between devices  40.8 us (17%)
  starting transfers between devices  33.7 us (14%)
  matrix products  21.7 us (9%)
  local copies, waits for them, and re-layouts  15.8 us (7%)
  between operations  14.6 us (6%)
    reduce_sum x7, other arithmetic, tap_sums(): jnp.sum(cot_field.astype(jnp.float32) * lax.slice_in_dim(padded, offset,...  34 us
    all_to_all x2, waiting for transfers between devices, to_columns(): split = lax.all_to_all(split, 'rows', 0, 0, tiled=True)  23.8 us
    convert_element_type x2, other arithmetic, per_device(): local = slide_padded(mix_padded[:, :, part * step:(part + 1) * step], col...  18.1 us
    convert_element_type x1, other arithmetic, per_device(): row_local = slide_padded(pad_along(grad_float, 1, half_reach), col_taps[:...  17.4 us
    convert_element_type x1, other arithmetic, per_device(): slide_padded(image_padded, row_taps, 2, columns).astype(jnp.bfloat16)  16.8 us
    convert_element_type x1, other arithmetic, per_device(): image_grad = (cotangent.astype(jnp.float32) + slide_padded(pad_along(row_...  16.5 us
    all_to_all x2, starting transfers between devices, to_columns(): split = lax.all_to_all(split, 'rows', 0, 0, tiled=True)  8.49 us
    all_to_all x2, starting transfers between devices, per_device(): lax.all_to_all(local, 'rows', split_axis=1, concat_axis=2, tiled=True)  7.78 us
  transfers between devices with their start and end apart: 8, of which 5 were waited for; matrix products, arithmetic and copies ran while one was open for 37% of the time, Pallas kernels for 0%

profile of v9, /device:TPU:0, one launch (start us, length us, event | category | flops | bytes accessed | tf_op | source)
XLA Modules:
  0.0 240.1 jit_solution(12502348580914584605)
XLA Ops:
  11.7 16.8 %fusion.101 = bf16[1,16,128,256]{3,2,1,0:T(8,128)(2,1)} fusion(f32[1,16,128,256]{3,2,1,0:T(8,128)S(1)} %convert_element_type.597, f32[256]{0:T(256)S(1)} %bitcast.567, f32[256]{0:T(256)S(1)} %bitcast.569, f32[256]{0:T(256)S(1)} %bitcast.509, f32[256]{0:T(256)S(1)} %bitcast.511, f32[256]{0:T(256)S(1)} %bitcast.513, f32[256]{0:T(256)S(1)} %bitcast.515, ...), kind=kLoop, calls=%fused_computation.506 | loop fusion | flops 53477376 | bytes 3197952 | tf_op jit(solution)/shard_map/convert_element_type | solution.py:146
  28.5 2.3 copy.27
  30.8 4.2 %all-to-all-start = ((bf16[4,1,16,32,256]{4,3,2,1,0:T(8,128)(2,1)}), bf16[4,1,16,32,256]{4,3,2,1,0:T(8,128)(2,1)}, u32[]{:S(2)}, u32[]{:S(2)}) async-start(bf16[4,1,16,32,256]{4,3,2,1,0:T(8,128)(2,1)} %copy.27), calls=%async_computation | async-start | bytes 2097152 | tf_op jit(solution)/shard_map/all_to_all | solution.py:122
  35.1 15.1 %all-to-all-done = bf16[4,1,16,32,256]{4,3,2,1,0:T(8,128)(2,1)} async-done(((bf16[4,1,16,32,256]{4,3,2,1,0:T(8,128)(2,1)}), bf16[4,1,16,32,256]{4,3,2,1,0:T(8,128)(2,1)}, u32[]{:S(2)}, u32[]{:S(2)}) %all-to-all-start) | async-done | bytes 1048608 | tf_op jit(solution)/shard_map/all_to_all | solution.py:122
  51.7 9.0 %fusion.575 = bf16[1,64,16,256]{3,2,0,1:T(8,128)(2,1)} fusion(f32[1,64,32,256]{3,2,1,0:T(8,128)S(1)} %bitcast.294, f32[256]{0:T(256)S(1)} %bitcast.463, f32[256]{0:T(256)S(1)} %bitcast.466, f32[256]{0:T(256)S(1)} %bitcast.319, f32[256]{0:T(256)S(1)} %bitcast.322, f32[256]{0:T(256)S(1)} %bitcast.325, f32[256]{0:T(256)S(1)} %bitcast.328, ...), kind=kLoop, calls=%fused_computation.999 | loop fusion | flops 26738688 | bytes 3722240 | tf_op jit(solution)/shard_map/convert_element_type | solution.py:157
  60.7 3.5 %all-to-all-start.1 = ((bf16[1,64,16,256]{3,2,0,1:T(8,128)(2,1)}), bf16[1,64,16,256]{3,2,0,1:T(8,128)(2,1)S(1)}, u32[]{:S(2)}, u32[]{:S(2)}) async-start(bf16[1,64,16,256]{3,2,0,1:T(8,128)(2,1)} %fusion.575), calls=%async_computation.1 | async-start | bytes 1048576 | tf_op jit(solution)/shard_map/all_to_all | solution.py:158
  64.2 9.0 %fusion.576 = bf16[1,64,16,256]{3,2,0,1:T(8,128)(2,1)} fusion(f32[1,64,32,256]{3,2,1,0:T(8,128)S(1)} %bitcast.295, f32[256]{0:T(256)S(1)} %bitcast.464, f32[256]{0:T(256)S(1)} %bitcast.467, f32[256]{0:T(256)S(1)} %bitcast.320, f32[256]{0:T(256)S(1)} %bitcast.323, f32[256]{0:T(256)S(1)} %bitcast.326, f32[256]{0:T(256)S(1)} %bitcast.329, ...), kind=kLoop, calls=%fused_computation.1000 | loop fusion | flops 26738688 | bytes 3722240 | tf_op jit(solution)/shard_map/convert_element_type | solution.py:157
  73.2 4.3 %all-to-all-start.2 = ((bf16[1,64,16,256]{3,2,0,1:T(8,128)(2,1)}), bf16[1,64,16,256]{3,2,0,1:T(8,128)(2,1)}, u32[]{:S(2)}, u32[]{:S(2)}) async-start(bf16[1,64,16,256]{3,2,0,1:T(8,128)(2,1)} %fusion.576), calls=%async_computation.2 | async-start | bytes 1048576 | tf_op jit(solution)/shard_map/all_to_all | solution.py:158
  77.6 2.1 fusion.359
  79.7 6.6 %all-to-all-done.2 = bf16[1,64,16,256]{3,2,0,1:T(8,128)(2,1)} async-done(((bf16[1,64,16,256]{3,2,0,1:T(8,128)(2,1)}), bf16[1,64,16,256]{3,2,0,1:T(8,128)(2,1)}, u32[]{:S(2)}, u32[]{:S(2)}) %all-to-all-start.2) | async-done | bytes 524320 | tf_op jit(solution)/shard_map/all_to_all | solution.py:158
  89.4 3.7 %multiply_convert_fusion = (bf16[2048,1024]{1,0:T(8,128)(2,1)S(1)}, f32[2048,1024]{1,0:T(8,128)S(1)}) fusion(f32[1024]{0:T(1024)S(1)} %copy-done.19, bf16[2048,256]{1,0:T(8,128)(2,1)S(1)} %add_convert_fusion, bf16[256,1024]{1,0:T(8,128)(2,1)S(1)} %copy-done), kind=kOutput, calls=%fused_computation.309 | convolution fusion | flops 1094713344 | bytes 14159872 | tf_op jit(solution)/shard_map/dot_general | solution.py:78
  93.2 2.6 %fusion.362 = (f32[256]{0:T(256)S(1)}, bf16[2048,256]{1,0:T(8,128)(2,1)}, bf16[2048,256]{1,0:T(8,128)(2,1)S(1)}) fusion(bf16[1,16,128,256]{3,2,1,0:T(8,128)(2,1)S(1)} %copy-done.5, f32[256]{0:T(256)S(1)} %copy-done.17, bf16[1,16,128,256]{3,2,1,0:T(8,128)(2,1)S(1)} %copy-done.3, f32[256]{0:T(256)S(1)} %copy-done.20, ...), kind=kOutput, calls=%fused_computation.771 | convolution fusion | flops 1078984448 | bytes 8915968 | tf_op jit(solution)/shard_map/dot_general | solution.py:80
  95.9 2.3 convolution_multiply_fusion
  98.1 6.4 %fusion.586 = (f32[1024]{0:T(1024)S(1)}, bf16[2048,1024]{1,0:T(8,128)(2,1)S(1)}) fusion(f32[2048,1024]{1,0:T(8,128)S(1)} %get-tuple-element.244, f32[1024]{0:T(1024)S(1)} %copy-done.19, bf16[2048,256]{1,0:T(8,128)(2,1)S(1)} %get-tuple-element.132, bf16[1024,256]{1,0:T(8,128)(2,1)S(1)} %copy-done.18), kind=kOutput, calls=%fused_computation.1021 | convolution fusion | flops 1117780992 | bytes 14163968 | tf_op jit(solution)/shard_map/dot_general | solution.py:85
  108.8 4.3 %all-to-all-start.3 = ((bf16[4,1,16,32,256]{4,3,2,1,0:T(8,128)(2,1)}), bf16[4,1,16,32,256]{4,3,2,1,0:T(8,128)(2,1)}, u32[]{:S(2)}, u32[]{:S(2)}) async-start(bf16[4,1,16,32,256]{4,3,2,1,0:T(8,128)(2,1)} %bitcast.314), calls=%async_computation.3 | async-start | bytes 2097152 | tf_op jit(solution)/shard_map/all_to_all | solution.py:122
  113.3 4.8 %fusion.369 = f32[256,1024]{1,0:T(8,128)} fusion(bf16[2048,256]{1,0:T(8,128)(2,1)} %copy-done.7, bf16[2048,1024]{1,0:T(8,128)(2,1)} %copy-done.21), kind=kOutput, calls=%fused_computation.787 | convolution fusion | flops 1074003968 | bytes 6291456 | tf_op jit(solution)/shard_map/dot_general | solution.py:109
  118.8 8.7 %all-to-all-done.3 = bf16[4,1,16,32,256]{4,3,2,1,0:T(8,128)(2,1)} async-done(((bf16[4,1,16,32,256]{4,3,2,1,0:T(8,128)(2,1)}), bf16[4,1,16,32,256]{4,3,2,1,0:T(8,128)(2,1)}, u32[]{:S(2)}, u32[]{:S(2)}) %all-to-all-start.3) | async-done | bytes 1048608 | tf_op jit(solution)/shard_map/all_to_all | solution.py:122
  129.1 17.4 %fusion.574 = bf16[1,64,32,256]{3,2,0,1:T(8,128)(2,1)} fusion(f32[1,64,32,256]{3,2,1,0:T(8,128)S(1)} %bitcast.299, f32[256]{0:T(256)S(1)} %bitcast.318, f32[256]{0:T(256)S(1)} %bitcast.375, f32[256]{0:T(256)S(1)} %bitcast.432, f32[256]{0:T(256)S(1)} %bitcast.462, f32[256]{0:T(256)S(1)} %bitcast.459, f32[256]{0:T(256)S(1)} %bitcast.456, ...), kind=kLoop, calls=%fused_computation.998 | loop fusion | flops 53477376 | bytes 3197952 | tf_op jit(solution)/shard_map/convert_element_type | solution.py:185
  146.4 4.1 %fusion.358 = (f32[256]{0:T(256)S(1)}, f32[256]{0:T(256)S(1)}, f32[256]{0:T(256)S(1)}, f32[256]{0:T(256)S(1)}, f32[256]{0:T(256)S(1)}, /*index=5*/f32[256]{0:T(2...) fusion(f32[1,64,32,256]{3,2,1,0:T(8,128)S(1)} %bitcast.300, ...), kind=kLoop, calls=%fused_computation.763 | loop fusion | flops 18869760 | bytes 4212736 | tf_op jit(solution)/shard_map/reduce_sum | solution.py:49
  150.6 4.9 %fusion.322 = (f32[256]{0:T(256)S(1)}, f32[256]{0:T(256)S(1)}, f32[256]{0:T(256)S(1)}, f32[256]{0:T(256)S(1)}, f32[256]{0:T(256)S(1)}, /*index=5*/f32[256]{0:T(2...) fusion(f32[1,64,32,256]{3,2,1,0:T(8,128)S(1)} %bitcast.301, ...), kind=kLoop, calls=%fused_computation.727 | loop fusion | flops 18869760 | bytes 4212736 | tf_op jit(solution)/shard_map/reduce_sum | solution.py:49
  155.5 4.5 %all-to-all-start.4 = ((bf16[1,64,32,256]{3,2,0,1:T(8,128)(2,1)}), bf16[1,64,32,256]{3,2,0,1:T(8,128)(2,1)}, u32[]{:S(2)}, u32[]{:S(2)}) async-start(bf16[1,64,32,256]{3,2,0,1:T(8,128)(2,1)} %fusion.574), calls=%async_computation.4 | async-start | bytes 2097152 | tf_op jit(solution)/shard_map/all_to_all | solution.py:186
  160.0 2.1 multiply_reduce_fusion.1
  162.2 8.8 %fusion.286 = (f32[256]{0:T(256)S(1)}, f32[256]{0:T(256)S(1)}, f32[256]{0:T(256)S(1)}, f32[256]{0:T(256)S(1)}, f32[256]{0:T(256)S(1)}, /*index=5*/f32[256]{0:T(2...) fusion(f32[1,64,32,256]{3,2,1,0:T(8,128)S(1)} %bitcast.302, ...), kind=kLoop, calls=%fused_computation.691 | loop fusion | flops 14676480 | bytes 4208640 | tf_op jit(solution)/shard_map/reduce_sum | solution.py:49
  171.2 3.0 %all-to-all-done.4 = bf16[1,64,32,256]{3,2,0,1:T(8,128)(2,1)} async-done(((bf16[1,64,32,256]{3,2,0,1:T(8,128)(2,1)}), bf16[1,64,32,256]{3,2,0,1:T(8,128)(2,1)}, u32[]{:S(2)}, u32[]{:S(2)}) %all-to-all-start.4) | async-done | bytes 1048608 | tf_op jit(solution)/shard_map/all_to_all | solution.py:186
  175.6 4.8 %fusion.157 = (f32[256]{0:T(256)S(1)}, f32[256]{0:T(256)S(1)}, f32[256]{0:T(256)S(1)}, f32[256]{0:T(256)S(1)}, f32[256]{0:T(256)S(1)}, /*index=5*/f32[256]{0:T(2...) fusion(bf16[1,16,128,256]{3,2,1,0:T(8,128)(2,1)S(1)} %bitcast.3, ...), kind=kLoop, calls=%fused_computation.562 | loop fusion | flops 28831232 | bytes 2115584 | tf_op jit(solution)/shard_map/reduce_sum | solution.py:49
  180.4 5.1 %fusion.156 = (f32[256]{0:T(256)S(1)}, f32[256]{0:T(256)S(1)}, f32[256]{0:T(256)S(1)}, f32[256]{0:T(256)S(1)}, f32[256]{0:T(256)S(1)}, /*index=5*/f32[256]{0:T(2...) fusion(bf16[1,16,128,256]{3,2,1,0:T(8,128)(2,1)S(1)} %bitcast.3, ...), kind=kLoop, calls=%fused_computation.561 | loop fusion | flops 28831232 | bytes 2115584 | tf_op jit(solution)/shard_map/reduce_sum | solution.py:49
  185.5 4.2 %fusion.155 = (f32[256]{0:T(256)S(1)}, f32[256]{0:T(256)S(1)}, f32[256]{0:T(256)S(1)}, f32[256]{0:T(256)S(1)}, f32[256]{0:T(256)S(1)}, /*index=5*/f32[256]{0:T(2...) fusion(bf16[1,16,128,256]{3,2,1,0:T(8,128)(2,1)S(1)} %bitcast.3, ...), kind=kLoop, calls=%fused_computation.560 | loop fusion | flops 24113408 | bytes 2112512 | tf_op jit(solution)/shard_map/reduce_sum | solution.py:49
  190.8 6.6 %all-to-all-start.5 = ((f32[16,14,128]{2,1,0:T(8,128)}), f32[16,14,128]{2,1,0:T(8,128)S(1)}, u32[]{:S(2)}, u32[]{:S(2)}) async-start(f32[16,14,128]{2,1,0:T(8,128)} %reshape.787), calls=%async_computation.5 | async-start | bytes 262144 | tf_op jit(solution)/shard_map/all_to_all | solution.py:229
  197.5 16.5 %fusion.360 = bf16[1,16,128,256]{3,2,1,0:T(8,128)(2,1)} fusion(bf16[1,16,128,256]{3,2,1,0:T(8,128)(2,1)S(1)} %copy-done.6, bf16[1,16,128,256]{3,2,1,0:T(8,128)(2,1)S(1)} %bitcast.306, f32[256]{0:T(256)S(1)} %bitcast.568, f32[256]{0:T(256)S(1)} %bitcast.570, f32[256]{0:T(256)S(1)} %bitcast.510, f32[256]{0:T(256)S(1)} %bitcast.512, f32[256]{0:T(256)S(1)} %bitcast.514, ...), kind=kLoop, calls=%fused_computation.769 | loop fusion | flops 81264640 | bytes 3197952 | tf_op jit(solution)/shard_map/convert_element_type | solution.py:193
  214.7 6.0 %all-to-all-start.6 = ((f32[16,14,128]{2,1,0:T(8,128)}), f32[16,14,128]{2,1,0:T(8,128)S(1)}, u32[]{:S(2)}, u32[]{:S(2)}) async-start(f32[16,14,128]{2,1,0:T(8,128)} %broadcast_in_dim.8), calls=%async_computation.6 | async-start | bytes 262144 | tf_op jit(solution)/shard_map/all_to_all | solution.py:232
  220.8 7.3 %all-to-all-done.6 = f32[16,14,128]{2,1,0:T(8,128)S(1)} async-done(((f32[16,14,128]{2,1,0:T(8,128)}), f32[16,14,128]{2,1,0:T(8,128)S(1)}, u32[]{:S(2)}, u32[]{:S(2)}) %all-to-all-start.6) | async-done | bytes 114720 | tf_op jit(solution)/shard_map/all_to_all | solution.py:232
  230.0 2.3 copy.40
  (90 shorter events, 22.0 us)
Async XLA Ops:
  7.2 82.2 %copy-start = (bf16[256,1024]{1,0:T(8,128)(2,1)S(1)}, bf16[256,1024]{1,0:T(8,128)(2,1)}, u32[]{:S(2)}) copy-start(bf16[256,1024]{1,0:T(8,128)(2,1)} %param.17) | copy-start | bytes 1572868
  10.2 18.3 %copy-start.10 = (f32[1,256]{1,0:T(1,128)}, f32[1,256]{1,0:T(1,128)S(1)}, u32[]{:S(2)}) copy-start(f32[1,256]{1,0:T(1,128)S(1)} %get-tuple-element.239) | copy-start | bytes 3076
  10.2 18.3 %copy-start.12 = (f32[1,256]{1,0:T(1,128)}, f32[1,256]{1,0:T(1,128)S(1)}, u32[]{:S(2)}) copy-start(f32[1,256]{1,0:T(1,128)S(1)} %get-tuple-element.240) | copy-start | bytes 3076
  28.5 6.5 %copy-start.9 = (f32[51,256]{1,0:T(8,128)S(1)}, f32[51,256]{1,0:T(8,128)}, u32[]{:S(2)}) copy-start(f32[51,256]{1,0:T(8,128)} %param.14) | copy-start | bytes 156676
  30.8 19.4 %all-to-all-start = ((bf16[4,1,16,32,256]{4,3,2,1,0:T(8,128)(2,1)}), bf16[4,1,16,32,256]{4,3,2,1,0:T(8,128)(2,1)}, u32[]{:S(2)}, u32[]{:S(2)}) async-start(bf16[4,1,16,32,256]{4,3,2,1,0:T(8,128)(2,1)} %copy.27), calls=%async_computation | async-start | bytes 2097152 | tf_op jit(solution)/shard_map/all_to_all | solution.py:122
  60.7 12.5 %all-to-all-start.1 = ((bf16[1,64,16,256]{3,2,0,1:T(8,128)(2,1)}), bf16[1,64,16,256]{3,2,0,1:T(8,128)(2,1)S(1)}, u32[]{:S(2)}, u32[]{:S(2)}) async-start(bf16[1,64,16,256]{3,2,0,1:T(8,128)(2,1)} %fusion.575), calls=%async_computation.1 | async-start | bytes 1048576 | tf_op jit(solution)/shard_map/all_to_all | solution.py:158
  73.2 13.0 %all-to-all-start.2 = ((bf16[1,64,16,256]{3,2,0,1:T(8,128)(2,1)}), bf16[1,64,16,256]{3,2,0,1:T(8,128)(2,1)}, u32[]{:S(2)}, u32[]{:S(2)}) async-start(bf16[1,64,16,256]{3,2,0,1:T(8,128)(2,1)} %fusion.576), calls=%async_computation.2 | async-start | bytes 1048576 | tf_op jit(solution)/shard_map/all_to_all | solution.py:158
  87.4 1.2 copy-start.14
  87.4 1.2 copy-start.16
  87.6 1.8 copy-start.19
  89.4 3.8 %copy-start.7 = (bf16[2048,256]{1,0:T(8,128)(2,1)}, bf16[2048,256]{1,0:T(8,128)(2,1)S(1)}, u32[]{:S(2)}) copy-start(bf16[2048,256]{1,0:T(8,128)(2,1)S(1)} %add_convert_fusion) | copy-start | bytes 3145732
  89.4 3.8 %copy-start.3 = (bf16[1,16,128,256]{3,2,1,0:T(8,128)(2,1)S(1)}, bf16[1,16,128,256]{3,2,1,0:T(8,128)(2,1)}, u32[]{:S(2)}) copy-start(bf16[1,16,128,256]{3,2,1,0:T(8,128)(2,1)} %param.11) | copy-start | bytes 3145732
  89.4 3.8 %copy-start.5 = (bf16[1,16,128,256]{3,2,1,0:T(8,128)(2,1)S(1)}, bf16[1,16,128,256]{3,2,1,0:T(8,128)(2,1)}, u32[]{:S(2)}) copy-start(bf16[1,16,128,256]{3,2,1,0:T(8,128)(2,1)} %param.12) | copy-start | bytes 3145732
  89.4 3.8 %copy-start.17 = (f32[256]{0:T(256)S(1)}, f32[256]{0:T(256)}, u32[]{:S(2)}) copy-start(f32[256]{0:T(256)} %param.21) | copy-start | bytes 3076
  89.4 3.8 %copy-start.18 = (bf16[1024,256]{1,0:T(8,128)(2,1)S(1)}, bf16[1024,256]{1,0:T(8,128)(2,1)}, u32[]{:S(2)}) copy-start(bf16[1024,256]{1,0:T(8,128)(2,1)} %param.19) | copy-start | bytes 1572868
  89.4 3.8 %copy-start.20 = (f32[256]{0:T(256)S(1)}, f32[256]{0:T(256)}, u32[]{:S(2)}) copy-start(f32[256]{0:T(256)} %param.20) | copy-start | bytes 3076
  104.5 1.9 copy-start.21
  108.8 18.8 %all-to-all-start.3 = ((bf16[4,1,16,32,256]{4,3,2,1,0:T(8,128)(2,1)}), bf16[4,1,16,32,256]{4,3,2,1,0:T(8,128)(2,1)}, u32[]{:S(2)}, u32[]{:S(2)}) async-start(bf16[4,1,16,32,256]{4,3,2,1,0:T(8,128)(2,1)} %bitcast.314), calls=%async_computation.3 | async-start | bytes 2097152 | tf_op jit(solution)/shard_map/all_to_all | solution.py:122
  113.1 107.7 %all-reduce.9.cloned.1.call-start = ((), (), s32[]{:S(2)}) async-start(), calls=%async_computation.7 | async-start | bytes 4194304 | tf_op jit(solution)/shard_map/psum | solution.py:195
  118.2 0.7 copy-start.15
  129.0 21.5 %copy-start.1 = (f32[4,1,16,32,256]{4,3,2,0,1:T(8,128)}, f32[4,1,16,32,256]{4,3,2,0,1:T(8,128)S(1)}, u32[]{:S(2)}) copy-start(f32[4,1,16,32,256]{4,3,2,0,1:T(8,128)S(1)} %bitcast_convert_fusion) | copy-start | bytes 6291460
  155.5 18.8 %all-to-all-start.4 = ((bf16[1,64,32,256]{3,2,0,1:T(8,128)(2,1)}), bf16[1,64,32,256]{3,2,0,1:T(8,128)(2,1)}, u32[]{:S(2)}, u32[]{:S(2)}) async-start(bf16[1,64,32,256]{3,2,0,1:T(8,128)(2,1)} %fusion.574), calls=%async_computation.4 | async-start | bytes 2097152 | tf_op jit(solution)/shard_map/all_to_all | solution.py:186
  160.0 2.2 copy-start.2
  171.0 4.5 %copy-start.4 = (bf16[1,16,128,256]{3,2,1,0:T(8,128)(2,1)S(1)}, bf16[1,16,128,256]{3,2,1,0:T(8,128)(2,1)}, u32[]{:S(2)}) copy-start(bf16[1,16,128,256]{3,2,1,0:T(8,128)(2,1)} %param.11) | copy-start | bytes 3145732
  185.5 11.9 %copy-start.11 = (f32[1,256]{1,0:T(1,128)S(1)}, f32[1,256]{1,0:T(1,128)}, u32[]{:S(2)}) copy-start(f32[1,256]{1,0:T(1,128)} %copy-done.10) | copy-start | bytes 3076
  185.5 11.9 %copy-start.13 = (f32[1,256]{1,0:T(1,128)S(1)}, f32[1,256]{1,0:T(1,128)}, u32[]{:S(2)}) copy-start(f32[1,256]{1,0:T(1,128)} %copy-done.12) | copy-start | bytes 3076
  189.7 7.8 %copy-start.6 = (bf16[1,16,128,256]{3,2,1,0:T(8,128)(2,1)S(1)}, bf16[1,16,128,256]{3,2,1,0:T(8,128)(2,1)}, u32[]{:S(2)}) copy-start(bf16[1,16,128,256]{3,2,1,0:T(8,128)(2,1)} %param.12) | copy-start | bytes 3145732
  190.8 23.2 %all-to-all-start.5 = ((f32[16,14,128]{2,1,0:T(8,128)}), f32[16,14,128]{2,1,0:T(8,128)S(1)}, u32[]{:S(2)}, u32[]{:S(2)}) async-start(f32[16,14,128]{2,1,0:T(8,128)} %reshape.787), calls=%async_computation.5 | async-start | bytes 262144 | tf_op jit(solution)/shard_map/all_to_all | solution.py:229
  214.7 13.4 %all-to-all-start.6 = ((f32[16,14,128]{2,1,0:T(8,128)}), f32[16,14,128]{2,1,0:T(8,128)S(1)}, u32[]{:S(2)}, u32[]{:S(2)}) async-start(f32[16,14,128]{2,1,0:T(8,128)} %broadcast_in_dim.8), calls=%async_computation.6 | async-start | bytes 262144 | tf_op jit(solution)/shard_map/all_to_all | solution.py:232
  220.8 11.5 %copy-start.8 = (f32[256,1024]{1,0:T(8,128)S(1)}, f32[256,1024]{1,0:T(8,128)}, u32[]{:S(2)}) copy-start(f32[256,1024]{1,0:T(8,128)} %get-tuple-element.264) | copy-start | bytes 3145732
Sparse Core Ops, SparseCore 0:
  118.3 102.1 all-reduce.8

commit v10 on v9

--- a/solution.py
+++ b/solution.py
@@ -142,10 +142,23 @@
     pixel_scale = 1.0 / math.sqrt(
         tiles_here * lax.axis_size("rep") * band_rows * lax.axis_size("rows") * columns
     )
-    image_padded = pad_along(images.astype(jnp.float32), 2, half_reach)
-    row_mix = slide_padded(image_padded, row_taps, 2, columns).astype(jnp.bfloat16)
-    row_mix = lax.optimization_barrier(row_mix)
-    mix_columns = to_columns(row_mix)
+    bands = 2 if band_rows % 2 == 0 else 1
+    band_step = band_rows // bands
+    band_pieces = []
+    for band in range(bands):
+        image_padded = pad_along(
+            images[:, band * band_step : (band + 1) * band_step].astype(jnp.float32), 2, half_reach
+        )
+        row_mix = slide_padded(image_padded, row_taps, 2, columns).astype(jnp.bfloat16)
+        row_mix = lax.optimization_barrier(row_mix)
+        band_pieces.append(to_columns(row_mix))
+    mix_columns = jnp.stack(
+        [
+            piece.reshape(tiles_here, lax.axis_size("rows"), band_step, piece.shape[2], channels)
+            for piece in band_pieces
+        ],
+        axis=2,
+    ).reshape(tiles_here, band_rows * lax.axis_size("rows"), columns // lax.axis_size("rows"), channels)
     mix_padded = pad_along(mix_columns.astype(jnp.float32), 1, half_reach)
     strip = mix_columns.shape[2]
     parts = 2 if strip % 16 == 0 else 1

time: 241 us -> 238 us (0.988)
  waiting for transfers between devices: 40.8 us -> 33.7 us
  starting transfers between devices: 33.7 us -> 37.3 us
    all_to_all x2 -> x3, waiting for transfers between devices: 23.8 us -> 17 us  [to_columns(): split = lax.all_to_all(split, 'rows', 0, 0, tiled=True)]
    all_to_all x2 -> x3, starting transfers between devices: 8.49 us -> 12.2 us  [to_columns(): split = lax.all_to_all(split, 'rows', 0, 0, tiled=True)]
    convert_element_type x1 -> x2, other arithmetic: 16.8 us -> 16 us  [per_device(): slide_padded(image_padded, row_taps, 2, columns).astype(jnp.bfloat16)]
  transfers between devices with their start and end apart: 8 -> 9, of which waited for: 5 -> 5; matrix products, arithmetic and copies ran while one was open for 37% -> 42% of each run, Pallas kernels for 0% -> 0%
where the time goes in v10:
time: 238 us; the launch traced here: 237 us
  other arithmetic  113 us (47%)
  starting transfers between devices  37.3 us (16%)
  waiting for transfers between devices  33.7 us (14%)
  matrix products  21.7 us (9%)
  local copies, waits for them, and re-layouts  16.3 us (7%)
  between operations  14.6 us (6%)
    reduce_sum x7, other arithmetic, tap_sums(): jnp.sum(cot_field.astype(jnp.float32) * lax.slice_in_dim(padded, offset,...  34.4 us
    convert_element_type x2, other arithmetic, per_device(): local = slide_padded(mix_padded[:, :, part * step:(part + 1) * step], col...  18.8 us
    convert_element_type x1, other arithmetic, per_device(): row_local = slide_padded(pad_along(grad_float, 1, half_reach), col_taps[:...  17.4 us
    all_to_all x3, waiting for transfers between devices, to_columns(): split = lax.all_to_all(split, 'rows', 0, 0, tiled=True)  17 us
    convert_element_type x1, other arithmetic, per_device(): image_grad = (cotangent.astype(jnp.float32) + slide_padded(pad_along(row_...  16.5 us
    convert_element_type x2, other arithmetic, per_device(): slide_padded(image_padded, row_taps, 2, columns).astype(jnp.bfloat16)  16 us
    all_to_all x3, starting transfers between devices, to_columns(): split = lax.all_to_all(split, 'rows', 0, 0, tiled=True)  12.2 us
    all_to_all x2, starting transfers between devices, per_device(): lax.all_to_all(local, 'rows', split_axis=1, concat_axis=2, tiled=True)  7.78 us
  transfers between devices with their start and end apart: 9, of which 5 were waited for; matrix products, arithmetic and copies ran while one was open for 42% of the time, Pallas kernels for 0%

profile of v10, /device:TPU:0, one launch (start us, length us, event | category | flops | bytes accessed | tf_op | source)
XLA Modules:
  0.0 237.0 jit_solution(5064997916751183123)
XLA Ops:
  11.6 8.1 %fusion.366 = bf16[1,8,128,256]{3,2,1,0:T(8,128)(2,1)S(1)} fusion(f32[1,8,128,256]{3,2,1,0:T(8,128)S(1)} %get-tuple-element.133, f32[256]{0:T(256)S(1)} %bitcast.469, f32[256]{0:T(256)S(1)} %bitcast.472, f32[256]{0:T(256)S(1)} %bitcast.382, f32[256]{0:T(256)S(1)} %bitcast.385, f32[256]{0:T(256)S(1)} %bitcast.388, f32[256]{0:T(256)S(1)} %bitcast.391, ...), kind=kLoop, calls=%fused_computation.834 | loop fusion | flops 26738688 | bytes 1625088 | tf_op jit(solution)/shard_map/convert_element_type | solution.py:152
  20.5 4.4 %all-to-all-start = ((bf16[4,1,8,32,256]{4,3,2,1,0:T(8,128)(2,1)}), bf16[4,1,8,32,256]{4,3,2,1,0:T(8,128)(2,1)S(1)}, u32[]{:S(2)}, u32[]{:S(2)}) async-start(bf16[4,1,8,32,256]{4,3,2,1,0:T(8,128)(2,1)} %copy.28), calls=%async_computation | async-start | bytes 1048576 | tf_op jit(solution)/shard_map/all_to_all | solution.py:122
  24.9 7.9 %fusion.467 = bf16[1,8,128,256]{3,2,1,0:T(8,128)(2,1)S(1)} fusion(f32[1,8,128,256]{3,2,1,0:T(8,128)S(1)} %get-tuple-element.134, f32[256]{0:T(256)S(1)} %bitcast.470, f32[256]{0:T(256)S(1)} %bitcast.473, f32[256]{0:T(256)S(1)} %bitcast.383, f32[256]{0:T(256)S(1)} %bitcast.386, f32[256]{0:T(256)S(1)} %bitcast.389, f32[256]{0:T(256)S(1)} %bitcast.392, ...), kind=kLoop, calls=%fused_computation.935 | loop fusion | flops 26738688 | bytes 1625088 | tf_op jit(solution)/shard_map/convert_element_type | solution.py:152
  33.7 3.6 %all-to-all-start.1 = ((bf16[4,1,8,32,256]{4,3,2,1,0:T(8,128)(2,1)}), bf16[4,1,8,32,256]{4,3,2,1,0:T(8,128)(2,1)S(1)}, u32[]{:S(2)}, u32[]{:S(2)}) async-start(bf16[4,1,8,32,256]{4,3,2,1,0:T(8,128)(2,1)} %copy.29), calls=%async_computation.1 | async-start | bytes 1048576 | tf_op jit(solution)/shard_map/all_to_all | solution.py:122
  37.9 8.2 %all-to-all-done.1 = bf16[4,1,8,32,256]{4,3,2,1,0:T(8,128)(2,1)S(1)} async-done(((bf16[4,1,8,32,256]{4,3,2,1,0:T(8,128)(2,1)}), bf16[4,1,8,32,256]{4,3,2,1,0:T(8,128)(2,1)S(1)}, u32[]{:S(2)}, u32[]{:S(2)}) %all-to-all-start.1) | async-done | bytes 524320 | tf_op jit(solution)/shard_map/all_to_all | solution.py:122
  48.1 9.0 %fusion.676 = bf16[1,64,16,256]{3,2,0,1:T(8,128)(2,1)} fusion(f32[1,64,32,256]{3,2,1,0:T(8,128)S(1)} %bitcast.296, f32[256]{0:T(256)S(1)} %bitcast.623, f32[256]{0:T(256)S(1)} %bitcast.626, f32[256]{0:T(256)S(1)} %bitcast.478, f32[256]{0:T(256)S(1)} %bitcast.481, f32[256]{0:T(256)S(1)} %bitcast.484, f32[256]{0:T(256)S(1)} %bitcast.487, ...), kind=kLoop, calls=%fused_computation.1152 | loop fusion | flops 26738688 | bytes 3722240 | tf_op jit(solution)/shard_map/convert_element_type | solution.py:170
  57.2 3.5 %all-to-all-start.2 = ((bf16[1,64,16,256]{3,2,0,1:T(8,128)(2,1)}), bf16[1,64,16,256]{3,2,0,1:T(8,128)(2,1)S(1)}, u32[]{:S(2)}, u32[]{:S(2)}) async-start(bf16[1,64,16,256]{3,2,0,1:T(8,128)(2,1)} %fusion.676), calls=%async_computation.2 | async-start | bytes 1048576 | tf_op jit(solution)/shard_map/all_to_all | solution.py:171
  60.7 9.7 %fusion.677 = bf16[1,64,16,256]{3,2,0,1:T(8,128)(2,1)} fusion(f32[1,64,32,256]{3,2,1,0:T(8,128)S(1)} %bitcast.297, f32[256]{0:T(256)} %bitcast.622, f32[256]{0:T(256)} %bitcast.625, f32[256]{0:T(256)S(1)} %bitcast.479, f32[256]{0:T(256)S(1)} %bitcast.482, f32[256]{0:T(256)S(1)} %bitcast.485, f32[256]{0:T(256)S(1)} %bitcast.488, f32[256]{0:T(256)S(1)} %bitcast.491, ...), kind=kLoop, calls=%fused_computation.1153 | loop fusion | flops 26738688 | bytes 3722240 | tf_op jit(solution)/shard_map/convert_element_type | solution.py:170
  70.4 4.3 %all-to-all-start.3 = ((bf16[1,64,16,256]{3,2,0,1:T(8,128)(2,1)}), bf16[1,64,16,256]{3,2,0,1:T(8,128)(2,1)}, u32[]{:S(2)}, u32[]{:S(2)}) async-start(bf16[1,64,16,256]{3,2,0,1:T(8,128)(2,1)} %fusion.677), calls=%async_computation.3 | async-start | bytes 1048576 | tf_op jit(solution)/shard_map/all_to_all | solution.py:171
  74.7 2.1 fusion.258
  76.8 6.7 %all-to-all-done.3 = bf16[1,64,16,256]{3,2,0,1:T(8,128)(2,1)} async-done(((bf16[1,64,16,256]{3,2,0,1:T(8,128)(2,1)}), bf16[1,64,16,256]{3,2,0,1:T(8,128)(2,1)}, u32[]{:S(2)}, u32[]{:S(2)}) %all-to-all-start.3) | async-done | bytes 524320 | tf_op jit(solution)/shard_map/all_to_all | solution.py:171
  86.6 3.7 %multiply_convert_fusion = (bf16[2048,1024]{1,0:T(8,128)(2,1)S(1)}, f32[2048,1024]{1,0:T(8,128)S(1)}) fusion(f32[1024]{0:T(1024)S(1)} %copy-done.19, bf16[2048,256]{1,0:T(8,128)(2,1)S(1)} %add_convert_fusion, bf16[256,1024]{1,0:T(8,128)(2,1)S(1)} %copy-done), kind=kOutput, calls=%fused_computation.259 | convolution fusion | flops 1094713344 | bytes 14159872 | tf_op jit(solution)/shard_map/dot_general | solution.py:78
  90.4 2.6 %fusion.261 = (f32[256]{0:T(256)S(1)}, bf16[2048,256]{1,0:T(8,128)(2,1)}, bf16[2048,256]{1,0:T(8,128)(2,1)S(1)}) fusion(bf16[1,16,128,256]{3,2,1,0:T(8,128)(2,1)S(1)} %copy-done.4, f32[256]{0:T(256)S(1)} %copy-done.17, bf16[1,16,128,256]{3,2,1,0:T(8,128)(2,1)S(1)} %copy-done.2, f32[256]{0:T(256)S(1)} %copy-done.20, ...), kind=kOutput, calls=%fused_computation.720 | convolution fusion | flops 1078984448 | bytes 8915968 | tf_op jit(solution)/shard_map/dot_general | solution.py:80
  93.0 2.3 convolution_multiply_fusion
  95.3 6.4 %fusion.687 = (f32[1024]{0:T(1024)S(1)}, bf16[2048,1024]{1,0:T(8,128)(2,1)S(1)}) fusion(f32[2048,1024]{1,0:T(8,128)S(1)} %get-tuple-element.246, f32[1024]{0:T(1024)S(1)} %copy-done.19, bf16[2048,256]{1,0:T(8,128)(2,1)S(1)} %get-tuple-element.132, bf16[1024,256]{1,0:T(8,128)(2,1)S(1)} %copy-done.18), kind=kOutput, calls=%fused_computation.1174 | convolution fusion | flops 1117780992 | bytes 14163968 | tf_op jit(solution)/shard_map/dot_general | solution.py:85
  106.0 4.3 %all-to-all-start.4 = ((bf16[4,1,16,32,256]{4,3,2,1,0:T(8,128)(2,1)}), bf16[4,1,16,32,256]{4,3,2,1,0:T(8,128)(2,1)}, u32[]{:S(2)}, u32[]{:S(2)}) async-start(bf16[4,1,16,32,256]{4,3,2,1,0:T(8,128)(2,1)} %bitcast.316), calls=%async_computation.4 | async-start | bytes 2097152 | tf_op jit(solution)/shard_map/all_to_all | solution.py:122
  110.5 4.8 %fusion.268 = f32[256,1024]{1,0:T(8,128)} fusion(bf16[2048,256]{1,0:T(8,128)(2,1)} %copy-done.7, bf16[2048,1024]{1,0:T(8,128)(2,1)} %copy-done.21), kind=kOutput, calls=%fused_computation.736 | convolution fusion | flops 1074003968 | bytes 6291456 | tf_op jit(solution)/shard_map/dot_general | solution.py:109
  116.0 8.8 %all-to-all-done.4 = bf16[4,1,16,32,256]{4,3,2,1,0:T(8,128)(2,1)} async-done(((bf16[4,1,16,32,256]{4,3,2,1,0:T(8,128)(2,1)}), bf16[4,1,16,32,256]{4,3,2,1,0:T(8,128)(2,1)}, u32[]{:S(2)}, u32[]{:S(2)}) %all-to-all-start.4) | async-done | bytes 1048608 | tf_op jit(solution)/shard_map/all_to_all | solution.py:122
  126.2 17.4 %fusion.675 = bf16[1,64,32,256]{3,2,0,1:T(8,128)(2,1)} fusion(f32[1,64,32,256]{3,2,1,0:T(8,128)S(1)} %bitcast.302, f32[256]{0:T(256)S(1)} %bitcast.477, f32[256]{0:T(256)S(1)} %bitcast.534, f32[256]{0:T(256)S(1)} %bitcast.591, f32[256]{0:T(256)S(1)} %bitcast.621, f32[256]{0:T(256)S(1)} %bitcast.618, f32[256]{0:T(256)S(1)} %bitcast.615, ...), kind=kLoop, calls=%fused_computation.1149 | loop fusion | flops 53477376 | bytes 3197952 | tf_op jit(solution)/shard_map/convert_element_type | solution.py:198
  143.6 4.1 %fusion.257 = (f32[256]{0:T(256)S(1)}, f32[256]{0:T(256)S(1)}, f32[256]{0:T(256)S(1)}, f32[256]{0:T(256)S(1)}, f32[256]{0:T(256)S(1)}, /*index=5*/f32[256]{0:T(2...) fusion(f32[1,64,32,256]{3,2,1,0:T(8,128)S(1)} %bitcast.303, ...), kind=kLoop, calls=%fused_computation.712 | loop fusion | flops 18869760 | bytes 4212736 | tf_op jit(solution)/shard_map/reduce_sum | solution.py:49
  147.8 4.9 %fusion.221 = (f32[256]{0:T(256)S(1)}, f32[256]{0:T(256)S(1)}, f32[256]{0:T(256)S(1)}, f32[256]{0:T(256)S(1)}, f32[256]{0:T(256)S(1)}, /*index=5*/f32[256]{0:T(2...) fusion(f32[1,64,32,256]{3,2,1,0:T(8,128)S(1)} %bitcast.304, ...), kind=kLoop, calls=%fused_computation.676 | loop fusion | flops 18869760 | bytes 4212736 | tf_op jit(solution)/shard_map/reduce_sum | solution.py:49
  152.6 4.5 %all-to-all-start.5 = ((bf16[1,64,32,256]{3,2,0,1:T(8,128)(2,1)}), bf16[1,64,32,256]{3,2,0,1:T(8,128)(2,1)}, u32[]{:S(2)}, u32[]{:S(2)}) async-start(bf16[1,64,32,256]{3,2,0,1:T(8,128)(2,1)} %fusion.675), calls=%async_computation.5 | async-start | bytes 2097152 | tf_op jit(solution)/shard_map/all_to_all | solution.py:199
  157.2 9.8 %fusion.185 = (f32[256]{0:T(256)S(1)}, f32[256]{0:T(256)S(1)}, f32[256]{0:T(256)S(1)}, f32[256]{0:T(256)S(1)}, f32[256]{0:T(256)S(1)}, /*index=5*/f32[256]{0:T(2...) fusion(f32[1,64,32,256]{3,2,1,0:T(8,128)} %bitcast.305, ...), kind=kLoop, calls=%fused_computation.640 | loop fusion | flops 14676480 | bytes 4208640 | tf_op jit(solution)/shard_map/reduce_sum | solution.py:49
  168.7 2.7 %all-to-all-done.5 = bf16[1,64,32,256]{3,2,0,1:T(8,128)(2,1)} async-done(((bf16[1,64,32,256]{3,2,0,1:T(8,128)(2,1)}), bf16[1,64,32,256]{3,2,0,1:T(8,128)(2,1)}, u32[]{:S(2)}, u32[]{:S(2)}) %all-to-all-start.5) | async-done | bytes 1048608 | tf_op jit(solution)/shard_map/all_to_all | solution.py:199
  172.8 4.8 %fusion.56 = (f32[256]{0:T(256)S(1)}, f32[256]{0:T(256)S(1)}, f32[256]{0:T(256)S(1)}, f32[256]{0:T(256)S(1)}, f32[256]{0:T(256)S(1)}, /*index=5*/f32[256]{0:T(25...) fusion(bf16[1,16,128,256]{3,2,1,0:T(8,128)(2,1)S(1)} %bitcast.3, ...), kind=kLoop, calls=%fused_computation.511 | loop fusion | flops 28831232 | bytes 2115584 | tf_op jit(solution)/shard_map/reduce_sum | solution.py:49
  177.6 5.1 %fusion.55 = (f32[256]{0:T(256)S(1)}, f32[256]{0:T(256)S(1)}, f32[256]{0:T(256)S(1)}, f32[256]{0:T(256)S(1)}, f32[256]{0:T(256)S(1)}, /*index=5*/f32[256]{0:T(25...) fusion(bf16[1,16,128,256]{3,2,1,0:T(8,128)(2,1)S(1)} %bitcast.3, ...), kind=kLoop, calls=%fused_computation.510 | loop fusion | flops 28831232 | bytes 2115584 | tf_op jit(solution)/shard_map/reduce_sum | solution.py:49
  182.7 4.2 %fusion.54 = (f32[256]{0:T(256)S(1)}, f32[256]{0:T(256)S(1)}, f32[256]{0:T(256)S(1)}, f32[256]{0:T(256)S(1)}, f32[256]{0:T(256)S(1)}, /*index=5*/f32[256]{0:T(25...) fusion(bf16[1,16,128,256]{3,2,1,0:T(8,128)(2,1)S(1)} %bitcast.3, ...), kind=kLoop, calls=%fused_computation.509 | loop fusion | flops 24113408 | bytes 2112512 | tf_op jit(solution)/shard_map/reduce_sum | solution.py:49
  188.0 6.5 %all-to-all-start.6 = ((f32[16,14,128]{2,1,0:T(8,128)}), f32[16,14,128]{2,1,0:T(8,128)S(1)}, u32[]{:S(2)}, u32[]{:S(2)}) async-start(f32[16,14,128]{2,1,0:T(8,128)} %reshape.804), calls=%async_computation.6 | async-start | bytes 262144 | tf_op jit(solution)/shard_map/all_to_all | solution.py:242
  194.5 16.5 %fusion.259 = bf16[1,16,128,256]{3,2,1,0:T(8,128)(2,1)} fusion(bf16[1,16,128,256]{3,2,1,0:T(8,128)(2,1)S(1)} %copy-done.5, bf16[1,16,128,256]{3,2,1,0:T(8,128)(2,1)S(1)} %bitcast.309, f32[256]{0:T(256)S(1)} %bitcast.381, f32[256]{0:T(256)S(1)} %bitcast.324, f32[256]{0:T(256)S(1)} %bitcast.438, f32[256]{0:T(256)S(1)} %bitcast.468, f32[256]{0:T(256)S(1)} %bitcast.465, ...), kind=kLoop, calls=%fused_computation.718 | loop fusion | flops 81264640 | bytes 3197952 | tf_op jit(solution)/shard_map/convert_element_type | solution.py:206
  211.7 6.0 %all-to-all-start.7 = ((f32[16,14,128]{2,1,0:T(8,128)}), f32[16,14,128]{2,1,0:T(8,128)S(1)}, u32[]{:S(2)}, u32[]{:S(2)}) async-start(f32[16,14,128]{2,1,0:T(8,128)} %broadcast_in_dim.8), calls=%async_computation.7 | async-start | bytes 262144 | tf_op jit(solution)/shard_map/all_to_all | solution.py:245
  217.7 7.3 %all-to-all-done.7 = f32[16,14,128]{2,1,0:T(8,128)S(1)} async-done(((f32[16,14,128]{2,1,0:T(8,128)}), f32[16,14,128]{2,1,0:T(8,128)S(1)}, u32[]{:S(2)}, u32[]{:S(2)}) %all-to-all-start.7) | async-done | bytes 114720 | tf_op jit(solution)/shard_map/all_to_all | solution.py:245
  226.9 2.3 copy.41
  (94 shorter events, 26.1 us)
Async XLA Ops:
  7.2 79.3 %copy-start = (bf16[256,1024]{1,0:T(8,128)(2,1)S(1)}, bf16[256,1024]{1,0:T(8,128)(2,1)}, u32[]{:S(2)}) copy-start(bf16[256,1024]{1,0:T(8,128)(2,1)} %param.17) | copy-start | bytes 1572868
  20.5 13.2 %copy-start.9 = (f32[51,256]{1,0:T(8,128)S(1)}, f32[51,256]{1,0:T(8,128)}, u32[]{:S(2)}) copy-start(f32[51,256]{1,0:T(8,128)} %param.14) | copy-start | bytes 156676
  20.5 13.2 %all-to-all-start = ((bf16[4,1,8,32,256]{4,3,2,1,0:T(8,128)(2,1)}), bf16[4,1,8,32,256]{4,3,2,1,0:T(8,128)(2,1)S(1)}, u32[]{:S(2)}, u32[]{:S(2)}) async-start(bf16[4,1,8,32,256]{4,3,2,1,0:T(8,128)(2,1)} %copy.28), calls=%async_computation | async-start | bytes 1048576 | tf_op jit(solution)/shard_map/all_to_all | solution.py:122
  33.7 12.4 %all-to-all-start.1 = ((bf16[4,1,8,32,256]{4,3,2,1,0:T(8,128)(2,1)}), bf16[4,1,8,32,256]{4,3,2,1,0:T(8,128)(2,1)S(1)}, u32[]{:S(2)}, u32[]{:S(2)}) async-start(bf16[4,1,8,32,256]{4,3,2,1,0:T(8,128)(2,1)} %copy.29), calls=%async_computation.1 | async-start | bytes 1048576 | tf_op jit(solution)/shard_map/all_to_all | solution.py:122
  46.1 0.8 copy-start.6
  46.1 2.0 copy-start.10
  46.1 2.0 copy-start.12
  57.2 13.2 %all-to-all-start.2 = ((bf16[1,64,16,256]{3,2,0,1:T(8,128)(2,1)}), bf16[1,64,16,256]{3,2,0,1:T(8,128)(2,1)S(1)}, u32[]{:S(2)}, u32[]{:S(2)}) async-start(bf16[1,64,16,256]{3,2,0,1:T(8,128)(2,1)} %fusion.676), calls=%async_computation.2 | async-start | bytes 1048576 | tf_op jit(solution)/shard_map/all_to_all | solution.py:171
  70.4 13.1 %all-to-all-start.3 = ((bf16[1,64,16,256]{3,2,0,1:T(8,128)(2,1)}), bf16[1,64,16,256]{3,2,0,1:T(8,128)(2,1)}, u32[]{:S(2)}, u32[]{:S(2)}) async-start(bf16[1,64,16,256]{3,2,0,1:T(8,128)(2,1)} %fusion.677), calls=%async_computation.3 | async-start | bytes 1048576 | tf_op jit(solution)/shard_map/all_to_all | solution.py:171
  84.6 1.2 copy-start.14
  84.6 1.2 copy-start.16
  84.7 1.8 copy-start.19
  86.5 3.8 %copy-start.7 = (bf16[2048,256]{1,0:T(8,128)(2,1)}, bf16[2048,256]{1,0:T(8,128)(2,1)S(1)}, u32[]{:S(2)}) copy-start(bf16[2048,256]{1,0:T(8,128)(2,1)S(1)} %add_convert_fusion) | copy-start | bytes 3145732
  86.5 3.8 %copy-start.2 = (bf16[1,16,128,256]{3,2,1,0:T(8,128)(2,1)S(1)}, bf16[1,16,128,256]{3,2,1,0:T(8,128)(2,1)}, u32[]{:S(2)}) copy-start(bf16[1,16,128,256]{3,2,1,0:T(8,128)(2,1)} %param.11) | copy-start | bytes 3145732
  86.6 3.8 %copy-start.4 = (bf16[1,16,128,256]{3,2,1,0:T(8,128)(2,1)S(1)}, bf16[1,16,128,256]{3,2,1,0:T(8,128)(2,1)}, u32[]{:S(2)}) copy-start(bf16[1,16,128,256]{3,2,1,0:T(8,128)(2,1)} %param.12) | copy-start | bytes 3145732
  86.6 3.8 %copy-start.17 = (f32[256]{0:T(256)S(1)}, f32[256]{0:T(256)}, u32[]{:S(2)}) copy-start(f32[256]{0:T(256)} %param.21) | copy-start | bytes 3076
  86.6 3.8 %copy-start.18 = (bf16[1024,256]{1,0:T(8,128)(2,1)S(1)}, bf16[1024,256]{1,0:T(8,128)(2,1)}, u32[]{:S(2)}) copy-start(bf16[1024,256]{1,0:T(8,128)(2,1)} %param.19) | copy-start | bytes 1572868
  86.6 3.8 %copy-start.20 = (f32[256]{0:T(256)S(1)}, f32[256]{0:T(256)}, u32[]{:S(2)}) copy-start(f32[256]{0:T(256)} %param.20) | copy-start | bytes 3076
  101.7 1.9 copy-start.21
  106.0 18.8 %all-to-all-start.4 = ((bf16[4,1,16,32,256]{4,3,2,1,0:T(8,128)(2,1)}), bf16[4,1,16,32,256]{4,3,2,1,0:T(8,128)(2,1)}, u32[]{:S(2)}, u32[]{:S(2)}) async-start(bf16[4,1,16,32,256]{4,3,2,1,0:T(8,128)(2,1)} %bitcast.316), calls=%async_computation.4 | async-start | bytes 2097152 | tf_op jit(solution)/shard_map/all_to_all | solution.py:122
  110.2 107.5 %all-reduce.10.cloned.1.call-start = ((), (), s32[]{:S(2)}) async-start(), calls=%async_computation.8 | async-start | bytes 4194304 | tf_op jit(solution)/shard_map/psum | solution.py:208
  115.3 0.7 copy-start.15
  115.3 10.9 %copy-start.11 = (f32[1,256]{1,0:T(1,128)S(1)}, f32[1,256]{1,0:T(1,128)}, u32[]{:S(2)}) copy-start(f32[1,256]{1,0:T(1,128)} %get-tuple-element.190) | copy-start | bytes 3076
  115.3 10.9 %copy-start.13 = (f32[1,256]{1,0:T(1,128)S(1)}, f32[1,256]{1,0:T(1,128)}, u32[]{:S(2)}) copy-start(f32[1,256]{1,0:T(1,128)} %get-tuple-element.191) | copy-start | bytes 3076
  126.2 21.6 %copy-start.1 = (f32[4,1,16,32,256]{4,3,2,0,1:T(8,128)}, f32[4,1,16,32,256]{4,3,2,0,1:T(8,128)S(1)}, u32[]{:S(2)}) copy-start(f32[4,1,16,32,256]{4,3,2,0,1:T(8,128)S(1)} %bitcast_convert_fusion) | copy-start | bytes 6291460
  152.6 18.8 %all-to-all-start.5 = ((bf16[1,64,32,256]{3,2,0,1:T(8,128)(2,1)}), bf16[1,64,32,256]{3,2,0,1:T(8,128)(2,1)}, u32[]{:S(2)}, u32[]{:S(2)}) async-start(bf16[1,64,32,256]{3,2,0,1:T(8,128)(2,1)} %fusion.675), calls=%async_computation.5 | async-start | bytes 2097152 | tf_op jit(solution)/shard_map/all_to_all | solution.py:199
  168.5 4.3 %copy-start.3 = (bf16[1,16,128,256]{3,2,1,0:T(8,128)(2,1)S(1)}, bf16[1,16,128,256]{3,2,1,0:T(8,128)(2,1)}, u32[]{:S(2)}) copy-start(bf16[1,16,128,256]{3,2,1,0:T(8,128)(2,1)} %param.11) | copy-start | bytes 3145732
  186.9 7.7 %copy-start.5 = (bf16[1,16,128,256]{3,2,1,0:T(8,128)(2,1)S(1)}, bf16[1,16,128,256]{3,2,1,0:T(8,128)(2,1)}, u32[]{:S(2)}) copy-start(bf16[1,16,128,256]{3,2,1,0:T(8,128)(2,1)} %param.12) | copy-start | bytes 3145732
  188.0 23.0 %all-to-all-start.6 = ((f32[16,14,128]{2,1,0:T(8,128)}), f32[16,14,128]{2,1,0:T(8,128)S(1)}, u32[]{:S(2)}, u32[]{:S(2)}) async-start(f32[16,14,128]{2,1,0:T(8,128)} %reshape.804), calls=%async_computation.6 | async-start | bytes 262144 | tf_op jit(solution)/shard_map/all_to_all | solution.py:242
  211.7 13.4 %all-to-all-start.7 = ((f32[16,14,128]{2,1,0:T(8,128)}), f32[16,14,128]{2,1,0:T(8,128)S(1)}, u32[]{:S(2)}, u32[]{:S(2)}) async-start(f32[16,14,128]{2,1,0:T(8,128)} %broadcast_in_dim.8), calls=%async_computation.7 | async-start | bytes 262144 | tf_op jit(solution)/shard_map/all_to_all | solution.py:245
  217.7 11.5 %copy-start.8 = (f32[256,1024]{1,0:T(8,128)S(1)}, f32[256,1024]{1,0:T(8,128)}, u32[]{:S(2)}) copy-start(f32[256,1024]{1,0:T(8,128)} %get-tuple-element.266) | copy-start | bytes 3145732
Sparse Core Ops, SparseCore 0:
  115.4 102.0 all-reduce.9
